TPU v7x, 256 devices: a whole 4x4x8 slice. The times are simulated.
256 devices in a mesh: dp: 4 (over z_lo, core), cp: 16 (over y, z_hi), tp: 4 (over x).
Axes of the slice: x: 4, y: 4, z: 8 (z_hi: 4, z_lo: 2; z = z_hi * 2 + z_lo), core: 2. Of those that a mesh axis runs over, the one named last changes fastest.
Arguments:
- hidden: bfloat16 [4, 2048, 8192], P('dp', 'cp'), may hold values from -6 to 6
- query: bfloat16 [4, 2048, 8192], P('dp', 'cp', 'tp'), may hold values from -360 to 360
- grad_out: bfloat16 [4, 2048, 8192], P('dp', 'cp', 'tp'), may hold values from -6 to 6
- k_weight: bfloat16 [8192, 1024], P('dp', 'tp'), may hold values from -0.0625 to 0.0625
- v_weight: bfloat16 [8192, 1024], P('dp', 'tp'), may hold values from -0.0625 to 0.0625
- doc_starts: int32 [4, 4], P('dp'), may hold values from 0 to 2047, as said below
Outputs:
- attn_out: bfloat16 [4, 2048, 8192], P('dp', 'cp', 'tp')
- query_grad: bfloat16 [4, 2048, 8192], P('dp', 'cp', 'tp')
- k_weight_grad: float32 [8192, 1024], P(('dp', 'cp'), 'tp')
- v_weight_grad: float32 [8192, 1024], P(('dp', 'cp'), 'tp')
Inputs may be any that keep to these rules, and one draw needn't show every extreme that they name: `doc_starts`: in each sequence the starts strictly increase and the first is 0.
All inputs are finite; a program needn't handle non-finite values.
Results may differ from a plain program's by a relative error of at most 0.04.
The roundings to bfloat16 on the way count: a program that leaves them out, or rounds other values in their place, can miss the bound.
Values may be sent and summed in bfloat16 or wider, within the bound.
No kernel may reach another device: no remote copies, remote signals or barrier semaphores. Data moves between devices by JAX's collectives and lax.ppermute only.
A program may use at most 128 MiB of HBM per device.

v0:
```python
import math

import jax
import jax.numpy as jnp
from jax import lax
from jax.sharding import PartitionSpec as P

DH = 128


NEG_BIG = -1e30


def place(rows, tok_rows, seq_rows):
    stretch = rows // tok_rows
    within = rows % tok_rows
    half_rows = tok_rows // 2
    return jnp.where(
        within < half_rows,
        stretch * half_rows + within,
        seq_rows - (stretch + 1) * half_rows + within - half_rows,
    )


def doc_index(positions, starts):
    return jnp.sum((starts[None, :] <= positions[:, None]).astype(jnp.int32), axis=1) - 1


def sweep(update, initial, all_keys, all_vals, span):

    def step_fn(block_index, running):
        first_row = block_index * span
        pieces = (
            lax.dynamic_slice_in_dim(all_keys, first_row, span, 0),
            lax.dynamic_slice_in_dim(all_vals, first_row, span, 0),
        )
        return update(running, pieces, first_row)

    return lax.fori_loop(0, all_keys.shape[0] // span, step_fn, initial)


def on_device(hidden, query, grad_out, k_weight, v_weight, doc_starts):
    inputs = hidden[0]
    tok_rows = inputs.shape[0]
    cp_count = lax.axis_size("cp")
    seq_rows = tok_rows * cp_count
    score_scale = DH ** (-0.5)
    kv_width = k_weight.shape[1]
    kv_heads = kv_width // DH
    per_group = query.shape[2] // DH // kv_heads
    starts = doc_starts[0]
    own_rows = lax.axis_index("cp") * tok_rows + jnp.arange(tok_rows, dtype=jnp.int32)
    own_place = place(own_rows, tok_rows, seq_rows)
    own_doc = doc_index(own_place, starts)

    def allowed_pairs(first_row, piece_rows):
        key_place = place(first_row + jnp.arange(piece_rows, dtype=jnp.int32), tok_rows, seq_rows)
        key_doc = doc_index(key_place, starts)
        return (key_place[None, :] <= own_place[:, None]) & (key_doc[None, :] == own_doc[:, None])

    pieces = (
        lax.all_gather(k_weight, "dp", axis=0, tiled=True),
        lax.all_gather(v_weight, "dp", axis=0, tiled=True),
    )
    columns = inputs
    key_sums = jnp.dot(columns, pieces[0], preferred_element_type=jnp.float32)
    value_sums = jnp.dot(columns, pieces[1], preferred_element_type=jnp.float32)
    keys = key_sums.astype(jnp.bfloat16)
    values = value_sums.astype(jnp.bfloat16)
    queries = query[0].reshape(tok_rows, kv_heads, per_group, DH)
    upstream = grad_out[0].reshape(tok_rows, kv_heads, per_group, DH)

    def totals_step(running, pieces, first_row):
        key_piece = pieces[0]
        piece_rows = key_piece.shape[0]
        allowed = allowed_pairs(first_row, piece_rows)
        top_score, denom = running
        key_heads = key_piece.reshape(piece_rows, kv_heads, DH)
        scores = (
            jnp.einsum("qgid,kgd->giqk", queries, key_heads, preferred_element_type=jnp.float32)
            * score_scale
        )
        scores = jnp.where(allowed, scores, NEG_BIG)
        fresh_top = jnp.maximum(top_score, jnp.max(scores, axis=-1))
        expos = jnp.where(allowed, jnp.exp(scores - fresh_top[..., None]), 0.0)
        denom = denom * jnp.exp(top_score - fresh_top) + jnp.sum(expos, axis=-1)
        return (fresh_top, denom)

    start_totals = (
        jnp.full((kv_heads, per_group, tok_rows), NEG_BIG, jnp.float32),
        jnp.zeros((kv_heads, per_group, tok_rows), jnp.float32),
    )
    span = tok_rows * math.gcd(cp_count, max(1, 512 // tok_rows))
    all_keys, all_vals = (
        lax.all_gather(keys, "cp", axis=0, tiled=True),
        lax.all_gather(values, "cp", axis=0, tiled=True),
    )
    top_score, denom = sweep(totals_step, start_totals, all_keys, all_vals, span)
    log_total = top_score + jnp.log(denom)

    def output_step(running, pieces, first_row):
        key_piece, value_piece = pieces
        piece_rows = key_piece.shape[0]
        allowed = allowed_pairs(first_row, piece_rows)
        key_heads = key_piece.reshape(piece_rows, kv_heads, DH)
        value_heads = value_piece.reshape(piece_rows, kv_heads, DH)
        scores = (
            jnp.einsum("qgid,kgd->giqk", queries, key_heads, preferred_element_type=jnp.float32)
            * score_scale
        )
        weights_bf = jnp.where(allowed, jnp.exp(scores - log_total[..., None]), 0.0).astype(
            jnp.bfloat16
        )
        return running + jnp.einsum(
            "giqk,kgd->qgid", weights_bf, value_heads, preferred_element_type=jnp.float32
        )

    start_output = jnp.zeros((tok_rows, kv_heads, per_group, DH), jnp.float32)
    accum = sweep(output_step, start_output, all_keys, all_vals, span)
    out_rows = accum.astype(jnp.bfloat16)
    delta = jnp.transpose(
        jnp.sum(upstream.astype(jnp.float32) * out_rows.astype(jnp.float32), axis=-1), (1, 2, 0)
    )

    def backward(running, pieces, first_row):
        key_piece, value_piece = pieces
        piece_rows = key_piece.shape[0]
        allowed = allowed_pairs(first_row, piece_rows)
        query_acc, key_term, value_term = running
        key_heads = key_piece.reshape(piece_rows, kv_heads, DH)
        value_heads = value_piece.reshape(piece_rows, kv_heads, DH)
        scores = (
            jnp.einsum("qgid,kgd->giqk", queries, key_heads, preferred_element_type=jnp.float32)
            * score_scale
        )
        weights = jnp.where(allowed, jnp.exp(scores - log_total[..., None]), 0.0)
        weights_bf = weights.astype(jnp.bfloat16)
        prob_grads = jnp.einsum(
            "qgid,kgd->giqk", upstream, value_heads, preferred_element_type=jnp.float32
        )
        score_grads = (weights * (prob_grads - delta[..., None])).astype(jnp.bfloat16)
        query_acc = (
            query_acc
            + jnp.einsum(
                "giqk,kgd->qgid", score_grads, key_heads, preferred_element_type=jnp.float32
            )
            * score_scale
        )
        key_piece_grad = (
            jnp.einsum("giqk,qgid->kgd", score_grads, queries, preferred_element_type=jnp.float32)
            * score_scale
        )
        value_piece_grad = jnp.einsum(
            "giqk,qgid->kgd", weights_bf, upstream, preferred_element_type=jnp.float32
        )
        key_term = lax.dynamic_update_slice_in_dim(
            key_term, key_piece_grad.reshape(piece_rows, kv_width), first_row, 0
        )
        value_term = lax.dynamic_update_slice_in_dim(
            value_term, value_piece_grad.reshape(piece_rows, kv_width), first_row, 0
        )
        return (query_acc, key_term, value_term)

    start_backward = (
        jnp.zeros((tok_rows, kv_heads, per_group, DH), jnp.float32),
        jnp.zeros((seq_rows, kv_width), jnp.float32),
        jnp.zeros((seq_rows, kv_width), jnp.float32),
    )
    query_acc, key_term, value_term = sweep(backward, start_backward, all_keys, all_vals, span)
    key_sum, value_sum = (
        lax.psum_scatter(
            key_term.astype(jnp.bfloat16), "cp", scatter_dimension=0, tiled=True
        ).astype(jnp.float32),
        lax.psum_scatter(
            value_term.astype(jnp.bfloat16), "cp", scatter_dimension=0, tiled=True
        ).astype(jnp.float32),
    )
    both_grads = jnp.concatenate(
        [key_sum.astype(jnp.bfloat16), value_sum.astype(jnp.bfloat16)], axis=1
    )
    columns = inputs
    result = lax.psum_scatter(
        jnp.dot(columns.T, both_grads, preferred_element_type=jnp.float32),
        ("dp", "cp"),
        scatter_dimension=0,
        tiled=True,
    )
    attn_rows = out_rows.reshape(1, tok_rows, kv_heads * per_group * DH)
    query_rows = query_acc.astype(jnp.bfloat16).reshape(1, tok_rows, kv_heads * per_group * DH)
    return (attn_rows, query_rows, result[:, :kv_width], result[:, kv_width:])


def solution(mesh):
    placed = (
        P("dp", "cp", None),
        P("dp", "cp", "tp"),
        P("dp", "cp", "tp"),
        P("dp", "tp"),
        P("dp", "tp"),
        P("dp", None),
    )
    return jax.shard_map(
        on_device,
        mesh=mesh,
        in_specs=placed,
        out_specs=(
            P("dp", "cp", "tp"),
            P("dp", "cp", "tp"),
            P(("dp", "cp"), "tp"),
            P(("dp", "cp"), "tp"),
        ),
        check_vma=False,
    )
```

profile of v0, /device:TPU:36, one launch (start us, length us, event | category | flops | bytes accessed | tf_op | source)
XLA Modules:
  0.0 896.1 jit_solution(16444612808211321503)
XLA Ops:
  8.7 51.0 %all-gather.9.cloned.1.call-done = bf16[8192,256]{1,0:T(8,128)(2,1)} async-done(((bf16[2048,256]{1,0:T(8,128)(2,1)}), bf16[8192,256]{1,0:T(8,128)(2,1)}) %all-gather.9.cloned.1.call-update) | async-done | bytes 4194320 | tf_op jit(solution)/shard_map/all_gather | solution.py:62
  59.8 3.5 fusion.43
  64.0 2.0 copy.106
  66.2 44.9 %all-gather.5.cloned.1.call-done = bf16[8192,256]{1,0:T(8,128)(2,1)} async-done(((bf16[2048,256]{1,0:T(8,128)(2,1)}), bf16[8192,256]{1,0:T(8,128)(2,1)}) %all-gather.5.cloned.1.call-update) | async-done | bytes 4194320 | tf_op jit(solution)/shard_map/all_gather | solution.py:63
  111.0 3.5 fusion.40
  114.6 53.1 %all-gather.11.cloned.1.call-done = bf16[2048,256]{1,0:T(8,128)(2,1)} async-done(((bf16[128,256]{1,0:T(8,128)(2,1)}), bf16[2048,256]{1,0:T(8,128)(2,1)}) %all-gather.11.cloned.1.call-update) | async-done | bytes 1048592 | tf_op jit(solution)/shard_map/all_gather | solution.py:95
  167.7 2.3 copy.103
  170.0 12.9 %while.57 = (s32[]{:T(128)}, f32[2,8,128]{2,1,0:T(8,128)S(1)}, f32[2,8,128]{2,1,0:T(8,128)S(1)}, s32[1,4]{1,0:T(1,128)S(1)}, s32[128]{0:T(128)S(1)}, /*index=5*/...) while((s32[]{:T(128)}, f32[2,8,128]{2,1,0:T(8,128)S(1)}, ...), condition=%wide.region_5.6_spmd.clone, body=%wide.region_1.5_spmd.clone.sunk | while | flops 277055616 | bytes 10018514 | solution.py:39
  182.9 38.2 %all-gather.7.cloned.1.call-done = bf16[2048,256]{1,0:T(8,128)(2,1)} async-done(((bf16[128,256]{1,0:T(8,128)(2,1)}), bf16[2048,256]{1,0:T(8,128)(2,1)}) %all-gather.7.cloned.1.call-update) | async-done | bytes 1048592 | tf_op jit(solution)/shard_map/all_gather | solution.py:96
  221.2 2.3 copy.102
  223.5 22.7 %while.58 = (s32[]{:T(128)}, f32[128,2,8,128]{0,3,2,1:T(8,128)}, bf16[2048,256]{0,1:T(8,128)(2,1)}, s32[1,4]{1,0:T(1,128)S(1)}, s32[128]{0:T(128)S(1)}, /*index=...) while((s32[]{:T(128)}, f32[128,2,8,128]{0,3,2,1:T(8,128)}, ...), condition=%wide.region_8.9_spmd.clone, body=%wide.region_6.8_spmd.clone.sunk | while | flops 541810816 | bytes 4349657 | solution.py:39
  225.6 3.3 fusion.98
  229.2 1.8 constant_dynamic-slice_fusion.10
  231.0 3.6 fusion.98
  236.7 3.6 fusion.98
  242.5 3.6 fusion.98
  246.1 2.4 multiply_reduce_fusion
  250.8 32.6 %while.59 = (s32[]{:T(128)}, f32[128,2,8,128]{0,3,2,1:T(8,128)}, bf16[2048,256]{0,1:T(8,128)(2,1)}, bf16[2048,256]{0,1:T(8,128)(2,1)}, bf16[2048,256]{0,1:T(8,12...) while((s32[]{:T(128)}, f32[128,2,8,128]{0,3,2,1:T(8,128)}, ...), condition=%wide.region_12.13_spmd.clone, body=%wide.region_10.12_spmd.clone.sunk | while | flops 1353932928 | bytes 35102520 | solution.py:39
  283.4 2.3 copy.138
  285.7 2.3 copy.136
  288.3 83.3 %reduce-scatter.12.cloned.1.call-done = bf16[128,256]{1,0:T(8,128)(2,1)} async-done(((bf16[2048,256]{1,0:T(8,128)(2,1)}), bf16[128,256]{1,0:T(8,128)(2,1)}) %reduce-scatter.12.cloned.1.call-update) | async-done | bytes 65552
  372.5 87.5 %reduce-scatter.10.cloned.1.call-done = bf16[128,256]{1,0:T(8,128)(2,1)} async-done(((bf16[2048,256]{1,0:T(8,128)(2,1)}), bf16[128,256]{1,0:T(8,128)(2,1)}) %reduce-scatter.10.cloned.1.call-update) | async-done | bytes 65552
  461.0 8.1 convolution_bitcast_fusion.1
  473.4 413.3 %reduce-scatter.8.cloned.1.call-done = f32[128,512]{0,1:T(8,128)} async-done(((f32[8192,512]{0,1:T(8,128)}), f32[128,512]{0,1:T(8,128)}) %reduce-scatter.8.cloned.1.call-update) | async-done | bytes 262160 | tf_op jit(solution)/shard_map/reduce_scatter | solution.py:182
  (179 shorter events, 65.2 us)
Async XLA Ops:
  7.2 52.6 %copy-start = (bf16[1,128,8192]{2,1,0:T(8,128)(2,1)S(1)}, bf16[1,128,8192]{2,1,0:T(8,128)(2,1)}, u32[]{:S(2)}) copy-start(bf16[1,128,8192]{2,1,0:T(8,128)(2,1)} %param.12) | copy-start | bytes 6291460
  7.2 56.2 %copy-start.5 = (bf16[1,128,2048]{2,1,0:T(8,128)(2,1)S(1)}, bf16[1,128,2048]{2,1,0:T(8,128)(2,1)}, u32[]{:S(2)}) copy-start(bf16[1,128,2048]{2,1,0:T(8,128)(2,1)} %param.13) | copy-start | bytes 1572868
  7.2 52.6 %all-gather.9.cloned.1.call-start = ((), (), s32[]{:S(2)}) async-start(), calls=%async_computation.5 | async-start | bytes 5242880 | tf_op jit(solution)/shard_map/all_gather | solution.py:62
  7.9 103.1 %all-gather.5.cloned.1.call-start = ((), (), s32[]{:S(2)}) async-start(), calls=%async_computation.3 | async-start | bytes 5242880 | tf_op jit(solution)/shard_map/all_gather | solution.py:63
  8.7 57.4 %copy-start.6 = (s32[1,4]{1,0:T(1,128)S(1)}, s32[1,4]{1,0:T(1,128)}, u32[]{:S(2)}) copy-start(s32[1,4]{1,0:T(1,128)} %param.17) | copy-start | bytes 52
  8.7 159.0 %all-gather.11.cloned.1.call-start = ((), (), s32[]{:S(2)}) async-start(), calls=%async_computation.6 | async-start | bytes 1114112 | tf_op jit(solution)/shard_map/all_gather | solution.py:95
  63.3 157.9 %all-gather.7.cloned.1.call-start = ((), (), s32[]{:S(2)}) async-start(), calls=%async_computation.4 | async-start | bytes 1114112 | tf_op jit(solution)/shard_map/all_gather | solution.py:96
  114.6 257.0 %reduce-scatter.12.cloned.1.call-start = ((), (), s32[]{:S(2)}) async-start(), calls=%async_computation.9 | async-start | bytes 1114112
  246.1 4.6 copy-start.3
  254.8 2.3 copy-start.1
  257.7 1.2 copy-start.2
  262.9 2.3 copy-start.1
  265.9 1.2 copy-start.2
  271.1 2.3 copy-start.1
  274.1 1.2 copy-start.2
  279.3 2.3 copy-start.1
  282.2 1.2 copy-start.2
  285.7 174.3 %reduce-scatter.10.cloned.1.call-start = ((), (), s32[]{:S(2)}) async-start(), calls=%async_computation.8 | async-start | bytes 1114112
  288.1 598.7 %reduce-scatter.8.cloned.1.call-start = ((), (), s32[]{:S(2)}) async-start(), calls=%async_computation.7 | async-start | bytes 17039360 | tf_op jit(solution)/shard_map/reduce_scatter | solution.py:182
  469.1 1.0 copy-start.4
Sparse Core Ops, SparseCore 0:
  9.8 49.9 all-gather.8
  61.6 49.4 all-gather.4
  114.0 53.6 all-gather.10
  170.6 50.5 all-gather.6
  285.8 85.6 reduce-scatter.11
  374.9 85.0 reduce-scatter.9
  469.2 417.5 reduce-scatter.7
where the time goes:
time: 897 us; the launch traced here: 896 us
  waiting for transfers between devices  773 us (86%)
  matrix products  51.1 us (6%)
  local copies, waits for them, and re-layouts  45 us (5%)
  between operations  14.3 us (2%)
  other arithmetic  11.9 us (1%)
    reduce_scatter x1, waiting for transfers between devices, on_device(): lax.psum_scatter(jnp.dot(columns.T, both_grads, preferred_element_type=jn...  413 us
    unnamed x9, waiting for transfers between devices  172 us
    all_gather x1, waiting for transfers between devices, on_device(): lax.all_gather(keys, 'cp', axis=0, tiled=True)  53.1 us
    all_gather x1, waiting for transfers between devices, on_device(): lax.all_gather(k_weight, 'dp', axis=0, tiled=True)  51 us
    all_gather x1, waiting for transfers between devices, on_device(): lax.all_gather(v_weight, 'dp', axis=0, tiled=True)  44.9 us
    all_gather x1, waiting for transfers between devices, on_device(): lax.all_gather(values, 'cp', axis=0, tiled=True)  38.2 us
  transfers between devices with their start and end apart: 7, of which 7 were waited for; matrix products, arithmetic and copies ran while one was open for 3% of the time, Pallas kernels for 0%

commit v1 on v0

v1 whole, which is shorter than its diff:
```python
import jax
import jax.numpy as jnp
from jax import lax
from jax.sharding import PartitionSpec as P

DH = 128


NEG_BIG = -1e30


def place(rows, tok_rows, seq_rows):
    stretch = rows // tok_rows
    within = rows % tok_rows
    half_rows = tok_rows // 2
    return jnp.where(
        within < half_rows,
        stretch * half_rows + within,
        seq_rows - (stretch + 1) * half_rows + within - half_rows,
    )


def doc_index(positions, starts):
    return jnp.sum((starts[None, :] <= positions[:, None]).astype(jnp.int32), axis=1) - 1


def on_device(hidden, query, grad_out, k_weight, v_weight, doc_starts):
    inputs = hidden[0]
    tok_rows, width = inputs.shape
    cp_count = lax.axis_size("cp")
    dp_count = lax.axis_size("dp")
    seq_rows = tok_rows * cp_count
    score_scale = DH ** (-0.5)
    kv_width = k_weight.shape[1]
    kv_heads = kv_width // DH
    per_group = query.shape[2] // DH // kv_heads
    starts = doc_starts[0]

    blk = width // (dp_count * cp_count)
    cols = inputs.reshape(tok_rows, dp_count, cp_count, blk).transpose(2, 0, 1, 3)
    cols = lax.all_to_all(cols, "cp", 0, 0, tiled=True)

    both_w = jnp.concatenate([k_weight, v_weight], axis=1)
    both_w = lax.all_gather(both_w, "dp", axis=0, tiled=True)
    kv = jnp.dot(inputs, both_w, preferred_element_type=jnp.float32).astype(jnp.bfloat16)
    kv_all = lax.all_gather(kv, "cp", axis=0, tiled=True)
    key_heads = kv_all[:, :kv_width].reshape(seq_rows, kv_heads, DH)
    value_heads = kv_all[:, kv_width:].reshape(seq_rows, kv_heads, DH)

    own_rows = lax.axis_index("cp") * tok_rows + jnp.arange(tok_rows, dtype=jnp.int32)
    own_place = place(own_rows, tok_rows, seq_rows)
    own_doc = doc_index(own_place, starts)
    key_place = place(jnp.arange(seq_rows, dtype=jnp.int32), tok_rows, seq_rows)
    key_doc = doc_index(key_place, starts)
    allowed = (key_place[None, :] <= own_place[:, None]) & (key_doc[None, :] == own_doc[:, None])

    queries = query[0].reshape(tok_rows, kv_heads, per_group, DH)
    upstream = grad_out[0].reshape(tok_rows, kv_heads, per_group, DH)

    scores = (
        jnp.einsum("qgid,kgd->giqk", queries, key_heads, preferred_element_type=jnp.float32)
        * score_scale
    )
    scores = jnp.where(allowed, scores, NEG_BIG)
    top_score = jnp.max(scores, axis=-1)
    expos = jnp.where(allowed, jnp.exp(scores - top_score[..., None]), 0.0)
    log_total = top_score + jnp.log(jnp.sum(expos, axis=-1))
    weights = jnp.where(allowed, jnp.exp(scores - log_total[..., None]), 0.0)
    weights_bf = weights.astype(jnp.bfloat16)
    out_rows = jnp.einsum(
        "giqk,kgd->qgid", weights_bf, value_heads, preferred_element_type=jnp.float32
    ).astype(jnp.bfloat16)
    delta = jnp.transpose(
        jnp.sum(upstream.astype(jnp.float32) * out_rows.astype(jnp.float32), axis=-1), (1, 2, 0)
    )
    prob_grads = jnp.einsum(
        "qgid,kgd->giqk", upstream, value_heads, preferred_element_type=jnp.float32
    )
    score_grads = (weights * (prob_grads - delta[..., None])).astype(jnp.bfloat16)
    query_acc = (
        jnp.einsum("giqk,kgd->qgid", score_grads, key_heads, preferred_element_type=jnp.float32)
        * score_scale
    )
    key_term = (
        jnp.einsum("giqk,qgid->kgd", score_grads, queries, preferred_element_type=jnp.float32)
        * score_scale
    )
    value_term = jnp.einsum(
        "giqk,qgid->kgd", weights_bf, upstream, preferred_element_type=jnp.float32
    )
    both_terms = jnp.concatenate(
        [key_term.reshape(seq_rows, kv_width), value_term.reshape(seq_rows, kv_width)], axis=1
    ).astype(jnp.bfloat16)
    both_grads = lax.psum(both_terms, "cp")

    grads = both_grads.reshape(cp_count, tok_rows, 2 * kv_width)
    partial = jnp.einsum("ctjb,ctn->jbn", cols, grads, preferred_element_type=jnp.float32)
    result = lax.psum_scatter(partial, "dp", scatter_dimension=0, tiled=True)[0]

    attn_rows = out_rows.reshape(1, tok_rows, kv_heads * per_group * DH)
    query_rows = query_acc.astype(jnp.bfloat16).reshape(1, tok_rows, kv_heads * per_group * DH)
    return (attn_rows, query_rows, result[:, :kv_width], result[:, kv_width:])


def solution(mesh):
    placed = (
        P("dp", "cp", None),
        P("dp", "cp", "tp"),
        P("dp", "cp", "tp"),
        P("dp", "tp"),
        P("dp", "tp"),
        P("dp", None),
    )
    return jax.shard_map(
        on_device,
        mesh=mesh,
        in_specs=placed,
        out_specs=(
            P("dp", "cp", "tp"),
            P("dp", "cp", "tp"),
            P(("dp", "cp"), "tp"),
            P(("dp", "cp"), "tp"),
        ),
        check_vma=False,
    )
```

time: 897 us -> 460 us (0.51)
  waiting for transfers between devices: 773 us -> 349 us
  local copies, waits for them, and re-layouts: 45 us -> 24.5 us
    reduce_scatter x1, waiting for transfers between devices: 413 us -> 14 us  [on_device(): result = lax.psum_scatter(partial, 'dp', scatter_dimension=0, tiled=True)[0]]
    psum x0 -> x1, waiting for transfers between devices: none -> 179 us  [on_device(): both_grads = lax.psum(both_terms, 'cp')]
    unnamed x9 -> x4, waiting for transfers between devices: 172 us -> 0.07 us
    all_gather x4 -> x2, waiting for transfers between devices: 187 us -> 156 us  [the longest x1 84.9 us: on_device(): both_w = lax.all_gather(both_w, 'dp', axis=0, tiled=True)]
    dynamic_slice x16 -> x0, local copies, waits for them, and re-layouts: 18.8 us -> none  [the longest x12 14.9 us: step_fn(): lax.dynamic_slice_in_dim(all_keys, first_row, span, 0)]
    dot_general x31 -> x8, matrix products: 51.1 us -> 50.2 us  [the longest x1 11.1 us: on_device(): jnp.einsum('giqk,kgd->qgid', weights_bf, value_heads, preferred_element_t...]
  transfers between devices with their start and end apart: 7 -> 5, of which waited for: 7 -> 4; matrix products, arithmetic and copies ran while one was open for 3% -> 14% of each run, Pallas kernels for 0% -> 0%
where the time goes in v1:
time: 460 us; the launch traced here: 457 us
  waiting for transfers between devices  349 us (76%)
  matrix products  50.2 us (11%)
  local copies, waits for them, and re-layouts  24.5 us (5%)
  between operations  14 us (3%)
  other arithmetic  10.3 us (2%)
  starting transfers between devices  9.27 us (2%)
    psum x1, waiting for transfers between devices, on_device(): both_grads = lax.psum(both_terms, 'cp')  179 us
    all_gather x1, waiting for transfers between devices, on_device(): both_w = lax.all_gather(both_w, 'dp', axis=0, tiled=True)  84.9 us
    all_gather x1, waiting for transfers between devices, on_device(): kv_all = lax.all_gather(kv, 'cp', axis=0, tiled=True)  71.6 us
    reduce_scatter x1, waiting for transfers between devices, on_device(): result = lax.psum_scatter(partial, 'dp', scatter_dimension=0, tiled=True)[0]  14 us
    unnamed x22, local copies, waits for them, and re-layouts  12.8 us
    dot_general x1, matrix products, on_device(): jnp.einsum('giqk,kgd->qgid', weights_bf, value_heads, preferred_element_t...  11.1 us
    dot_general x1, matrix products, on_device(): jnp.einsum('qgid,kgd->giqk', upstream, value_heads, preferred_element_typ...  9.25 us
  transfers between devices with their start and end apart: 5, of which 4 were waited for; matrix products, arithmetic and copies ran while one was open for 14% of the time, Pallas kernels for 0%

profile of v1, /device:TPU:36, one launch (start us, length us, event | category | flops | bytes accessed | tf_op | source)
XLA Modules:
  0.0 457.4 jit_solution(11077758612200397458)
XLA Ops:
  7.2 3.1 pad_maximum_fusion
  10.3 84.9 %all-gather.3.cloned.1.call-done = bf16[8192,512]{1,0:T(8,128)(2,1)} async-done(((bf16[2048,512]{1,0:T(8,128)(2,1)}), bf16[8192,512]{1,0:T(8,128)(2,1)}) %all-gather.3.cloned.1.call-update) | async-done | bytes 8388624 | tf_op jit(solution)/shard_map/all_gather | solution.py:44
  95.2 7.0 %fusion.18 = bf16[128,512]{0,1:T(8,128)(2,1)} fusion(bf16[8192,512]{1,0:T(8,128)(2,1)} %all-gather.3.cloned.1.call-done, bf16[1,128,8192]{2,1,0:T(8,128)(2,1)} %param.6), kind=kOutput, calls=%fused_computation.24 | convolution fusion | flops 1073807360 | bytes 10616832 | tf_op jit(solution)/shard_map/dot_general | solution.py:45
  102.3 3.3 copy.76
  105.6 2.6 copy.77
  108.2 8.9 %all-to-all-start = ((bf16[16,128,4,128]{3,1,2,0:T(8,128)(2,1)}), bf16[16,128,4,128]{3,1,2,0:T(8,128)(2,1)}, u32[]{:S(2)}, u32[]{:S(2)}) async-start(bf16[16,128,4,128]{3,1,2,0:T(8,128)(2,1)} %copy.77), calls=%async_computation | async-start | bytes 4194304 | tf_op jit(solution)/shard_map/all_to_all | solution.py:41
  118.9 1.3 compare_and_fusion
  120.3 71.6 %all-gather.5.cloned.1.call-done = bf16[2048,512]{0,1:T(8,128)(2,1)} async-done(((bf16[128,512]{0,1:T(8,128)(2,1)}), bf16[2048,512]{0,1:T(8,128)(2,1)}) %all-gather.5.cloned.1.call-update) | async-done | bytes 2097168 | tf_op jit(solution)/shard_map/all_gather | solution.py:46
  191.8 2.7 fusion.39
  194.6 2.6 fusion.3
  197.2 4.0 select_reduce_fusion
  201.2 1.7 copy-done
  202.9 8.2 %fusion.6 = bf16[2,2048,128]{1,2,0:T(8,128)(2,1)S(1)} fusion(bf16[128,2,8,128]{0,3,2,1:T(8,128)(2,1)S(1)} %bitcast.117, f32[2,2048,128,8]{2,1,3,0:T(8,128)} %copy-done, f32[2,8,128]{2,1,0:T(8,128)S(1)} %log_add_fusion, pred[128,2048]{0,1:T(8,128)(4,1)S(1)} %compare_and_fusion), kind=kOutput, calls=%fused_computation.12 | convolution fusion | flops 1095237632 | bytes 18620416 | tf_op jit(solution)/shard_map/giqk,qgid->kgd/dot_general | solution.py:88
  212.5 11.1 %multiply_reduce_fusion = (f32[128,2,8]{0,2,1:T(8,128)S(1)}, bf16[2,128,8,128]{3,1,2,0:T(8,128)(2,1)}) fusion(bf16[128,2,8,128]{0,3,2,1:T(8,128)(2,1)S(1)} %bitcast.118, bf16[2048,2,128,1]{0,2,3,1:T(8,128)(2,1)} %bitcast.114, f32[2,2048,128,8]{2,1,3,0:T(8,128)} %copy-done, f32[2,8,128]{2,1,0:T(8,128)S(1)} %log_add_fusion, ...), kind=kOutput, calls=%fused_computation.25 | convolution fusion | flops 1096022016 | bytes 19152896 | tf_op jit(solution)/shard_map/giqk,kgd->qgid/dot_general | solution.py:70
  223.6 9.3 %fusion.1 = bf16[2,8,128,2048]{2,3,1,0:T(8,128)(2,1)S(1)} fusion(f32[2,2048,128,8]{2,1,3,0:T(8,128)} %copy-done, f32[2,8,128]{2,1,0:T(8,128)S(1)} %bitcast.123, f32[2,8,128]{2,1,0:T(8,128)S(1)} %log_add_fusion, pred[128,2048]{0,1:T(8,128)(4,1)S(1)} %compare_and_fusion, bf16[2048,2,128,1]{0,2,3,1:T(8,128)(2,1)S(1)} %bitcast.115, ...), kind=kOutput, calls=%fused_computation.2 | convolution fusion | flops 1103101952 | bytes 27017216 | tf_op jit(solution)/shard_map/qgid,kgd->giqk/dot_general | solution.py:76
  232.9 3.2 copy-done.1
  236.1 2.8 fusion.5
  239.0 1.3 copy.73
  240.3 1.7 pad_maximum_fusion.1
  242.0 2.4 copy.75
  244.5 178.7 %all-reduce.2.cloned.1.call-done = bf16[16,128,512]{1,2,0:T(8,128)(2,1)} async-done(((bf16[16,128,512]{1,2,0:T(8,128)(2,1)}), bf16[16,128,512]{1,2,0:T(8,128)(2,1)}) %all-reduce.2.cloned.1.call-update) | async-done | bytes 2097168 | tf_op jit(solution)/shard_map/psum | solution.py:94
  423.1 4.4 fusion.11
  427.6 4.7 %fusion.14 = bf16[2,128,8,128]{3,1,2,0:T(8,128)(2,1)S(1)} fusion(bf16[2048,2,128,1]{0,2,3,1:T(8,128)(2,1)S(1)} %bitcast.106, bf16[2,8,128,2048]{2,3,1,0:T(8,128)(2,1)} %copy-done.1), kind=kOutput, calls=%fused_computation.21 | convolution fusion | flops 1074266112 | bytes 9961472 | tf_op jit(solution)/shard_map/giqk,kgd->qgid/dot_general | solution.py:81
  434.3 14.0 %reduce-scatter.2.cloned.1.call-done = f32[1,128,512]{1,2,0:T(8,128)} async-done(((f32[4,128,512]{1,2,0:T(8,128)}), f32[1,128,512]{1,2,0:T(8,128)}) %reduce-scatter.2.cloned.1.call-update) | async-done | bytes 262160 | tf_op jit(solution)/shard_map/reduce_scatter | solution.py:98
  (38 shorter events, 7.8 us)
Async XLA Ops:
  7.2 88.1 %all-gather.3.cloned.1.call-start = ((), (), s32[]{:S(2)}) async-start(), calls=%async_computation.2 | async-start | bytes 10485760 | tf_op jit(solution)/shard_map/all_gather | solution.py:44
  10.3 181.6 %all-gather.5.cloned.1.call-start = ((), (), s32[]{:S(2)}) async-start(), calls=%async_computation.3 | async-start | bytes 2228224 | tf_op jit(solution)/shard_map/all_gather | solution.py:46
  102.2 15.1 %copy-start.3 = (bf16[1,128,2048]{2,1,0:T(8,128)(2,1)S(1)}, bf16[1,128,2048]{2,1,0:T(8,128)(2,1)}, u32[]{:S(2)}) copy-start(bf16[1,128,2048]{2,1,0:T(8,128)(2,1)} %param.7) | copy-start | bytes 1572868
  102.2 15.4 %copy-start.4 = (bf16[1,128,2048]{2,1,0:T(8,128)(2,1)S(1)}, bf16[1,128,2048]{2,1,0:T(8,128)(2,1)}, u32[]{:S(2)}) copy-start(bf16[1,128,2048]{2,1,0:T(8,128)(2,1)} %param.8) | copy-start | bytes 1572868
  102.2 16.5 %copy-start.7 = (s32[1,4]{1,0:T(1,128)S(1)}, s32[1,4]{1,0:T(1,128)}, u32[]{:S(2)}) copy-start(s32[1,4]{1,0:T(1,128)} %param.11) | copy-start | bytes 52
  108.2 136.2 %all-to-all-start = ((bf16[16,128,4,128]{3,1,2,0:T(8,128)(2,1)}), bf16[16,128,4,128]{3,1,2,0:T(8,128)(2,1)}, u32[]{:S(2)}, u32[]{:S(2)}) async-start(bf16[16,128,4,128]{3,1,2,0:T(8,128)(2,1)} %copy.77), calls=%async_computation | async-start | bytes 4194304 | tf_op jit(solution)/shard_map/all_to_all | solution.py:41
  117.1 306.0 %all-reduce.2.cloned.1.call-start = ((), (), s32[]{:S(2)}) async-start(), calls=%async_computation.4 | async-start | bytes 4194304 | tf_op jit(solution)/shard_map/psum | solution.py:94
  197.2 5.7 %copy-start = (f32[2,2048,128,8]{2,1,3,0:T(8,128)}, f32[2,2048,128,8]{2,1,3,0:T(8,128)S(1)}, u32[]{:S(2)}) copy-start(f32[2,2048,128,8]{2,1,3,0:T(8,128)S(1)} %get-tuple-element.25) | copy-start | bytes 50331652
  197.2 5.7 %copy-start.6 = (bf16[1,128,2048]{1,2,0:T(8,128)(2,1)S(1)}, bf16[1,128,2048]{1,2,0:T(8,128)(2,1)}, u32[]{:S(2)}) copy-start(bf16[1,128,2048]{1,2,0:T(8,128)(2,1)} %copy.66) | copy-start | bytes 1572868
  212.5 11.1 %copy-start.2 = (bf16[2048,256]{0,1:T(8,128)(2,1)S(1)}, bf16[2048,256]{0,1:T(8,128)(2,1)}, u32[]{:S(2)}) copy-start(bf16[2048,256]{0,1:T(8,128)(2,1)} %get-tuple-element.21) | copy-start | bytes 3145732
  232.9 3.2 copy-start.1
  244.4 203.9 %reduce-scatter.2.cloned.1.call-start = ((), (), s32[]{:S(2)}) async-start(), calls=%async_computation.5 | async-start | bytes 1310720 | tf_op jit(solution)/shard_map/reduce_scatter | solution.py:98
  427.6 5.7 %copy-start.5 = (bf16[2,128,8,128]{3,1,2,0:T(8,128)(2,1)S(1)}, bf16[2,128,8,128]{3,1,2,0:T(8,128)(2,1)}, u32[]{:S(2)}) copy-start(bf16[2,128,8,128]{3,1,2,0:T(8,128)(2,1)} %get-tuple-element.27) | copy-start | bytes 1572868
Sparse Core Ops, SparseCore 0:
  10.4 84.7 all-gather.2
  102.4 89.4 all-gather.4
  244.5 178.5 all-reduce.1
  427.7 20.5 reduce-scatter.1

commit v2 on v1

--- a/solution.py
+++ b/solution.py
@@ -24,6 +24,16 @@
     return jnp.sum((starts[None, :] <= positions[:, None]).astype(jnp.int32), axis=1) - 1
 
 
+def gather_over(piece, axis, count):
+    spread = jnp.broadcast_to(piece[None], (count,) + piece.shape)
+    return lax.all_to_all(spread, axis, 0, 0, tiled=True)
+
+
+def reduce_over(blocks, axis):
+    received = lax.all_to_all(blocks, axis, 0, 0, tiled=True)
+    return jnp.sum(received.astype(jnp.float32), axis=0)
+
+
 def on_device(hidden, query, grad_out, k_weight, v_weight, doc_starts):
     inputs = hidden[0]
     tok_rows, width = inputs.shape
@@ -41,9 +51,12 @@
     cols = lax.all_to_all(cols, "cp", 0, 0, tiled=True)
 
     both_w = jnp.concatenate([k_weight, v_weight], axis=1)
-    both_w = lax.all_gather(both_w, "dp", axis=0, tiled=True)
-    kv = jnp.dot(inputs, both_w, preferred_element_type=jnp.float32).astype(jnp.bfloat16)
-    kv_all = lax.all_gather(kv, "cp", axis=0, tiled=True)
+    w_rows = both_w.shape[0]
+    by_dp = inputs.reshape(tok_rows, dp_count, w_rows).transpose(1, 0, 2)
+    by_dp = lax.all_to_all(by_dp, "dp", 0, 0, tiled=True)
+    kv_part = jnp.einsum("str,rn->stn", by_dp, both_w, preferred_element_type=jnp.float32)
+    kv = reduce_over(kv_part, "dp").astype(jnp.bfloat16)
+    kv_all = gather_over(kv, "cp", cp_count).reshape(seq_rows, 2 * kv_width)
     key_heads = kv_all[:, :kv_width].reshape(seq_rows, kv_heads, DH)
     value_heads = kv_all[:, kv_width:].reshape(seq_rows, kv_heads, DH)
 
@@ -91,11 +104,11 @@
     both_terms = jnp.concatenate(
         [key_term.reshape(seq_rows, kv_width), value_term.reshape(seq_rows, kv_width)], axis=1
     ).astype(jnp.bfloat16)
-    both_grads = lax.psum(both_terms, "cp")
+    own_grads = reduce_over(both_terms.reshape(cp_count, tok_rows, 2 * kv_width), "cp")
+    grads = gather_over(own_grads.astype(jnp.bfloat16), "cp", cp_count)
 
-    grads = both_grads.reshape(cp_count, tok_rows, 2 * kv_width)
     partial = jnp.einsum("ctjb,ctn->jbn", cols, grads, preferred_element_type=jnp.float32)
-    result = lax.psum_scatter(partial, "dp", scatter_dimension=0, tiled=True)[0]
+    result = reduce_over(partial, "dp")
 
     attn_rows = out_rows.reshape(1, tok_rows, kv_heads * per_group * DH)
     query_rows = query_acc.astype(jnp.bfloat16).reshape(1, tok_rows, kv_heads * per_group * DH)

time: 460 us -> 394 us (0.86)
  waiting for transfers between devices: 349 us -> 148 us
  starting transfers between devices: 9.27 us -> 78.7 us
  blocking collectives: 0 us -> 65.8 us
  between operations: 14 us -> 0.87 us
  local copies, waits for them, and re-layouts: 24.5 us -> 36.1 us
    psum x1 -> x0, waiting for transfers between devices: 179 us -> none  [on_device(): both_grads = lax.psum(both_terms, 'cp')]
    all_gather x2 -> x0, waiting for transfers between devices: 156 us -> none  [the longest x1 84.9 us: on_device(): both_w = lax.all_gather(both_w, 'dp', axis=0, tiled=True)]
    all_to_all x0 -> x4, waiting for transfers between devices: none -> 109 us  [the longest x2 46 us: reduce_over(): received = lax.all_to_all(blocks, axis, 0, 0, tiled=True)]
    all_to_all x0 -> x4, starting transfers between devices: none -> 72.5 us  [the longest x2 56.8 us: reduce_over(): received = lax.all_to_all(blocks, axis, 0, 0, tiled=True)]
    all_to_all x0 -> x2, blocking collectives: none -> 65.8 us  [the longest x1 48.3 us: gather_over(): return lax.all_to_all(spread, axis, 0, 0, tiled=True)]
    all_to_all x1, waiting for transfers between devices: 0.01 us -> 38.9 us  [on_device(): cols = lax.all_to_all(cols, 'cp', 0, 0, tiled=True)]
    reduce_scatter x1 -> x0, waiting for transfers between devices: 14 us -> none  [on_device(): result = lax.psum_scatter(partial, 'dp', scatter_dimension=0, tiled=True)[0]]
    unnamed x22 -> x29, local copies, waits for them, and re-layouts: 12.8 us -> 19.2 us
  transfers between devices with their start and end apart: 5 -> 5, of which waited for: 4 -> 5; matrix products, arithmetic and copies ran while one was open for 14% -> 5% of each run, Pallas kernels for 0% -> 0%
where the time goes in v2:
time: 394 us; the launch traced here: 391 us
  waiting for transfers between devices  148 us (38%)
  starting transfers between devices  78.7 us (20%)
  blocking collectives  65.8 us (17%)
  matrix products  51.2 us (13%)
  local copies, waits for them, and re-layouts  36.1 us (9%)
  other arithmetic  10.4 us (3%)
    all_to_all x2, starting transfers between devices, reduce_over(): received = lax.all_to_all(blocks, axis, 0, 0, tiled=True)  56.8 us
    all_to_all x1, blocking collectives, gather_over(): return lax.all_to_all(spread, axis, 0, 0, tiled=True)  48.3 us
    all_to_all x2, waiting for transfers between devices, reduce_over(): received = lax.all_to_all(blocks, axis, 0, 0, tiled=True)  46 us
    all_to_all x1, waiting for transfers between devices, gather_over(): return lax.all_to_all(spread, axis, 0, 0, tiled=True)  43.7 us
    all_to_all x1, waiting for transfers between devices, on_device(): cols = lax.all_to_all(cols, 'cp', 0, 0, tiled=True)  38.9 us
    all_to_all x1, waiting for transfers between devices, on_device(): by_dp = lax.all_to_all(by_dp, 'dp', 0, 0, tiled=True)  19.6 us
    unnamed x29, local copies, waits for them, and re-layouts  19.2 us
    all_to_all x1, blocking collectives, reduce_over(): received = lax.all_to_all(blocks, axis, 0, 0, tiled=True)  17.6 us
  transfers between devices with their start and end apart: 5, of which 5 were waited for; matrix products, arithmetic and copies ran while one was open for 5% of the time, Pallas kernels for 0%

profile of v2, /device:TPU:36, one launch (start us, length us, event | category | flops | bytes accessed | tf_op | source)
XLA Modules:
  0.0 391.3 jit_solution(4551743920197237833)
XLA Ops:
  0.6 3.2 copy.68
  3.9 2.7 copy.69
  6.6 4.5 %all-to-all-start = ((bf16[4,128,2048]{2,1,0:T(8,128)(2,1)}), bf16[4,128,2048]{2,1,0:T(8,128)(2,1)}, u32[]{:S(2)}, u32[]{:S(2)}) async-start(bf16[4,128,2048]{2,1,0:T(8,128)(2,1)} %bitcast.125), calls=%async_computation | async-start | bytes 4194304 | tf_op jit(solution)/shard_map/all_to_all | solution.py:56
  15.6 19.6 %all-to-all-done = bf16[4,128,2048]{2,1,0:T(8,128)(2,1)} async-done(((bf16[4,128,2048]{2,1,0:T(8,128)(2,1)}), bf16[4,128,2048]{2,1,0:T(8,128)(2,1)}, u32[]{:S(2)}, u32[]{:S(2)}) %all-to-all-start) | async-done | bytes 2097184 | tf_op jit(solution)/shard_map/all_to_all | solution.py:56
  35.2 3.5 fusion.14
  38.7 17.6 %all_to_all.35 = f32[4,128,512]{1,2,0:T(8,128)} all-to-all(f32[4,128,512]{1,2,0:T(8,128)S(1)} %fusion.14), channel_id=1, replica_groups=mesh['dp'=4,'cp'=16,'tp'=4] {'dp'}, dimensions={0} | all-to-all | bytes 2097152 | tf_op jit(solution)/shard_map/all_to_all | solution.py:33
  59.3 11.2 %all-to-all-start.2 = ((bf16[16,128,512]{1,2,0:T(8,128)(2,1)}), bf16[16,128,512]{1,2,0:T(8,128)(2,1)}, u32[]{:S(2)}, u32[]{:S(2)}) async-start(bf16[16,128,512]{1,2,0:T(8,128)(2,1)} %broadcast_in_dim.18), calls=%async_computation.2 | async-start | bytes 4194304 | tf_op jit(solution)/shard_map/all_to_all | solution.py:29
  74.5 43.7 %all-to-all-done.2 = bf16[16,128,512]{1,2,0:T(8,128)(2,1)} async-done(((bf16[16,128,512]{1,2,0:T(8,128)(2,1)}), bf16[16,128,512]{1,2,0:T(8,128)(2,1)}, u32[]{:S(2)}, u32[]{:S(2)}) %all-to-all-start.2) | async-done | bytes 2097184 | tf_op jit(solution)/shard_map/all_to_all | solution.py:29
  121.3 2.7 fusion.3
  124.1 4.2 %select_reduce_fusion = f32[2,8,128]{2,1,0:T(8,128)S(1)} fusion(f32[2,2048,128,8]{2,1,3,0:T(8,128)S(1)} %get-tuple-element.25, f32[2,8,128]{2,1,0:T(8,128)S(1)} %get-tuple-element.24, pred[128,2048]{0,1:T(8,128)(4,1)S(1)} %compare_and_fusion), kind=kLoop, calls=%fused_computation.5 | loop fusion | flops 20969472 | bytes 17055744 | tf_op jit(solution)/shard_map/reduce_sum | solution.py:80
  129.8 10.6 %fusion.7 = bf16[2048,2,128]{2,0,1:T(8,128)(2,1)} fusion(bf16[128,2,8,128]{0,3,2,1:T(8,128)(2,1)S(1)} %bitcast.139, f32[2,2048,128,8]{2,1,3,0:T(8,128)} %copy-done, f32[2,8,128]{2,1,0:T(8,128)S(1)} %log_add_fusion, pred[128,2048]{0,1:T(8,128)(4,1)S(1)} %compare_and_fusion), kind=kOutput, calls=%fused_computation.13 | convolution fusion | flops 1095237632 | bytes 18620416 | tf_op jit(solution)/shard_map/giqk,qgid->kgd/dot_general | solution.py:101
  140.4 11.2 %multiply_reduce_fusion = (f32[128,2,8]{0,2,1:T(8,128)S(1)}, bf16[2,128,8,128]{3,1,2,0:T(8,128)(2,1)}) fusion(bf16[128,2,8,128]{0,3,2,1:T(8,128)(2,1)} %bitcast.137, bf16[2048,2,128,1]{0,2,3,1:T(8,128)(2,1)} %bitcast.133, f32[2,2048,128,8]{2,1,3,0:T(8,128)} %copy-done, f32[2,8,128]{2,1,0:T(8,128)S(1)} %log_add_fusion, pred[128,2048]{0,1:T(8,128)(4,1)S(1)} %compare_and_fusion), kind=kOutput, calls=%fused_computation.28 | convolution fusion | flops 1096022016 | bytes 19152896 | tf_op jit(solution)/shard_map/giqk,kgd->qgid/dot_general | solution.py:83
  151.7 9.2 %fusion.1 = bf16[2,8,128,2048]{2,3,1,0:T(8,128)(2,1)} fusion(f32[2,2048,128,8]{2,1,3,0:T(8,128)S(1)} %copy-done.1, f32[2,8,128]{2,1,0:T(8,128)S(1)} %bitcast.142, f32[2,8,128]{2,1,0:T(8,128)S(1)} %log_add_fusion, pred[128,2048]{0,1:T(8,128)(4,1)S(1)} %compare_and_fusion, bf16[2048,2,128,1]{0,2,3,1:T(8,128)(2,1)} %bitcast.134, ...), kind=kOutput, calls=%fused_computation.2 | convolution fusion | flops 1103101952 | bytes 27017216 | tf_op jit(solution)/shard_map/qgid,kgd->giqk/dot_general | solution.py:89
  160.9 6.8 %fusion.8 = bf16[2048,2,128]{2,0,1:T(8,128)(2,1)} fusion(bf16[2,8,128,2048]{2,3,1,0:T(8,128)(2,1)} %fusion.1, bf16[128,2,8,128]{3,2,1,0:T(8,128)(2,1)} %bitcast.132), kind=kOutput, calls=%fused_computation.14 | convolution fusion | flops 1074790400 | bytes 9961472 | tf_op jit(solution)/shard_map/giqk,qgid->kgd/dot_general | solution.py:98
  170.0 2.5 copy.107
  179.6 7.7 %all-to-all-start.3 = ((bf16[16,128,512]{1,2,0:T(8,128)(2,1)}), bf16[16,128,512]{1,2,0:T(8,128)(2,1)}, u32[]{:S(2)}, u32[]{:S(2)}) async-start(bf16[16,128,512]{1,2,0:T(8,128)(2,1)} %copy.82), calls=%async_computation.3 | async-start | bytes 4194304 | tf_op jit(solution)/shard_map/all_to_all | solution.py:33
  187.3 2.6 copy.84
  189.9 40.0 %all-to-all-done.3 = bf16[16,128,512]{1,2,0:T(8,128)(2,1)} async-done(((bf16[16,128,512]{1,2,0:T(8,128)(2,1)}), bf16[16,128,512]{1,2,0:T(8,128)(2,1)}, u32[]{:S(2)}, u32[]{:S(2)}) %all-to-all-start.3) | async-done | bytes 2097184 | tf_op jit(solution)/shard_map/all_to_all | solution.py:33
  229.9 6.1 %all-to-all-start.5 = ((bf16[16,128,4,128]{3,1,2,0:T(8,128)(2,1)}), bf16[16,128,4,128]{3,1,2,0:T(8,128)(2,1)S(1)}, u32[]{:S(2)}, u32[]{:S(2)}) async-start(bf16[16,128,4,128]{3,1,2,0:T(8,128)(2,1)} %copy.84), calls=%async_computation.5 | async-start | bytes 4194304 | tf_op jit(solution)/shard_map/all_to_all | solution.py:51
  237.9 38.9 %all-to-all-done.5 = bf16[16,128,4,128]{3,1,2,0:T(8,128)(2,1)S(1)} async-done(((bf16[16,128,4,128]{3,1,2,0:T(8,128)(2,1)}), bf16[16,128,4,128]{3,1,2,0:T(8,128)(2,1)S(1)}, u32[]{:S(2)}, u32[]{:S(2)}) %all-to-all-start.5) | async-done | bytes 2097184 | tf_op jit(solution)/shard_map/all_to_all | solution.py:51
  277.3 48.3 %all_to_all.36 = bf16[16,128,512]{1,2,0:T(8,128)(2,1)S(1)} all-to-all(bf16[16,128,512]{1,2,0:T(8,128)(2,1)S(1)} %broadcast_in_dim.39), channel_id=1, replica_groups=mesh['dp'=4,'cp'=16,'tp'=4] {'cp'}, dimensions={0} | all-to-all | bytes 4194304 | tf_op jit(solution)/shard_map/all_to_all | solution.py:29
  327.8 49.1 %all-to-all-start.6 = ((f32[4,128,512]{1,2,0:T(8,128)}), f32[4,128,512]{1,2,0:T(8,128)S(1)}, u32[]{:S(2)}, u32[]{:S(2)}) async-start(f32[4,128,512]{1,2,0:T(8,128)} %fusion.15), calls=%async_computation.6 | async-start | bytes 2097152 | tf_op jit(solution)/shard_map/all_to_all | solution.py:33
  376.9 4.7 %fusion.18 = bf16[2,128,8,128]{3,1,2,0:T(8,128)(2,1)S(1)} fusion(bf16[2048,2,128,1]{0,2,3,1:T(8,128)(2,1)S(1)} %bitcast.124, bf16[2,8,128,2048]{2,3,1,0:T(8,128)(2,1)} %fusion.1), kind=kOutput, calls=%fused_computation.26 | convolution fusion | flops 1074266112 | bytes 9961472 | tf_op jit(solution)/shard_map/giqk,kgd->qgid/dot_general | solution.py:94
  383.6 6.1 %all-to-all-done.6 = f32[4,128,512]{1,2,0:T(8,128)S(1)} async-done(((f32[4,128,512]{1,2,0:T(8,128)}), f32[4,128,512]{1,2,0:T(8,128)S(1)}, u32[]{:S(2)}, u32[]{:S(2)}) %all-to-all-start.6) | async-done | bytes 1048608 | tf_op jit(solution)/shard_map/all_to_all | solution.py:33
  (48 shorter events, 33.6 us)
Async XLA Ops:
  6.6 28.6 %all-to-all-start = ((bf16[4,128,2048]{2,1,0:T(8,128)(2,1)}), bf16[4,128,2048]{2,1,0:T(8,128)(2,1)}, u32[]{:S(2)}, u32[]{:S(2)}) async-start(bf16[4,128,2048]{2,1,0:T(8,128)(2,1)} %bitcast.125), calls=%async_computation | async-start | bytes 4194304 | tf_op jit(solution)/shard_map/all_to_all | solution.py:56
  15.6 54.9 %copy-start.5 = (bf16[1,128,2048]{2,1,0:T(8,128)(2,1)S(1)}, bf16[1,128,2048]{2,1,0:T(8,128)(2,1)}, u32[]{:S(2)}) copy-start(bf16[1,128,2048]{2,1,0:T(8,128)(2,1)} %param.7) | copy-start | bytes 1572868
  38.7 34.2 %copy-start.8 = (s32[1,4]{1,0:T(1,128)S(1)}, s32[1,4]{1,0:T(1,128)}, u32[]{:S(2)}) copy-start(s32[1,4]{1,0:T(1,128)} %param.11) | copy-start | bytes 52
  59.3 59.0 %all-to-all-start.2 = ((bf16[16,128,512]{1,2,0:T(8,128)(2,1)}), bf16[16,128,512]{1,2,0:T(8,128)(2,1)}, u32[]{:S(2)}, u32[]{:S(2)}) async-start(bf16[16,128,512]{1,2,0:T(8,128)(2,1)} %broadcast_in_dim.18), calls=%async_computation.2 | async-start | bytes 4194304 | tf_op jit(solution)/shard_map/all_to_all | solution.py:29
  70.7 53.4 %copy-start.4 = (bf16[16,8,16,128]{3,2,1,0:T(8,128)(2,1)}, bf16[16,8,16,128]{3,2,1,0:T(8,128)(2,1)S(1)}, u32[]{:S(2)}) copy-start(bf16[16,8,16,128]{3,2,1,0:T(8,128)(2,1)S(1)} %copy.106) | copy-start | bytes 1572868
  121.3 2.8 copy-start.2
  124.1 5.7 %copy-start = (f32[2,2048,128,8]{2,1,3,0:T(8,128)}, f32[2,2048,128,8]{2,1,3,0:T(8,128)S(1)}, u32[]{:S(2)}) copy-start(f32[2,2048,128,8]{2,1,3,0:T(8,128)S(1)} %get-tuple-element.25) | copy-start | bytes 50331652
  124.1 5.7 %copy-start.7 = (bf16[1,128,2048]{1,2,0:T(8,128)(2,1)S(1)}, bf16[1,128,2048]{1,2,0:T(8,128)(2,1)}, u32[]{:S(2)}) copy-start(bf16[1,128,2048]{1,2,0:T(8,128)(2,1)} %copy.74) | copy-start | bytes 1572868
  140.4 11.3 %copy-start.1 = (f32[2,2048,128,8]{2,1,3,0:T(8,128)S(1)}, f32[2,2048,128,8]{2,1,3,0:T(8,128)}, u32[]{:S(2)}) copy-start(f32[2,2048,128,8]{2,1,3,0:T(8,128)} %copy-done) | copy-start | bytes 50331652
  179.6 50.3 %all-to-all-start.3 = ((bf16[16,128,512]{1,2,0:T(8,128)(2,1)}), bf16[16,128,512]{1,2,0:T(8,128)(2,1)}, u32[]{:S(2)}, u32[]{:S(2)}) async-start(bf16[16,128,512]{1,2,0:T(8,128)(2,1)} %copy.82), calls=%async_computation.3 | async-start | bytes 4194304 | tf_op jit(solution)/shard_map/all_to_all | solution.py:33
  229.9 47.0 %all-to-all-start.5 = ((bf16[16,128,4,128]{3,1,2,0:T(8,128)(2,1)}), bf16[16,128,4,128]{3,1,2,0:T(8,128)(2,1)S(1)}, u32[]{:S(2)}, u32[]{:S(2)}) async-start(bf16[16,128,4,128]{3,1,2,0:T(8,128)(2,1)} %copy.84), calls=%async_computation.5 | async-start | bytes 4194304 | tf_op jit(solution)/shard_map/all_to_all | solution.py:51
  325.5 51.4 %copy-start.3 = (bf16[2048,256]{0,1:T(8,128)(2,1)S(1)}, bf16[2048,256]{0,1:T(8,128)(2,1)}, u32[]{:S(2)}) copy-start(bf16[2048,256]{0,1:T(8,128)(2,1)} %copy-done.2) | copy-start | bytes 3145732
  327.8 61.9 %all-to-all-start.6 = ((f32[4,128,512]{1,2,0:T(8,128)}), f32[4,128,512]{1,2,0:T(8,128)S(1)}, u32[]{:S(2)}, u32[]{:S(2)}) async-start(f32[4,128,512]{1,2,0:T(8,128)} %fusion.15), calls=%async_computation.6 | async-start | bytes 2097152 | tf_op jit(solution)/shard_map/all_to_all | solution.py:33
  376.9 5.7 %copy-start.6 = (bf16[2,128,8,128]{3,1,2,0:T(8,128)(2,1)S(1)}, bf16[2,128,8,128]{3,1,2,0:T(8,128)(2,1)}, u32[]{:S(2)}) copy-start(bf16[2,128,8,128]{3,1,2,0:T(8,128)(2,1)} %get-tuple-element.27) | copy-start | bytes 1572868

commit v3 on v2

--- a/solution.py
+++ b/solution.py
@@ -101,14 +101,15 @@
     value_term = jnp.einsum(
         "giqk,qgid->kgd", weights_bf, upstream, preferred_element_type=jnp.float32
     )
-    both_terms = jnp.concatenate(
-        [key_term.reshape(seq_rows, kv_width), value_term.reshape(seq_rows, kv_width)], axis=1
-    ).astype(jnp.bfloat16)
-    own_grads = reduce_over(both_terms.reshape(cp_count, tok_rows, 2 * kv_width), "cp")
-    grads = gather_over(own_grads.astype(jnp.bfloat16), "cp", cp_count)
+    value_terms = value_term.reshape(cp_count, tok_rows, kv_width).astype(jnp.bfloat16)
+    cols, value_terms = lax.optimization_barrier((cols, value_terms))
+    value_grads = gather_over(reduce_over(value_terms, "cp").astype(jnp.bfloat16), "cp", cp_count)
+    key_terms = key_term.reshape(cp_count, tok_rows, kv_width).astype(jnp.bfloat16)
+    key_grads = gather_over(reduce_over(key_terms, "cp").astype(jnp.bfloat16), "cp", cp_count)
 
-    partial = jnp.einsum("ctjb,ctn->jbn", cols, grads, preferred_element_type=jnp.float32)
-    result = reduce_over(partial, "dp")
+    value_part = jnp.einsum("ctjb,ctn->jbn", cols, value_grads, preferred_element_type=jnp.float32)
+    key_part = jnp.einsum("ctjb,ctn->jbn", cols, key_grads, preferred_element_type=jnp.float32)
+    result = reduce_over(jnp.concatenate([key_part, value_part], axis=2), "dp")
 
     attn_rows = out_rows.reshape(1, tok_rows, kv_heads * per_group * DH)
     query_rows = query_acc.astype(jnp.bfloat16).reshape(1, tok_rows, kv_heads * per_group * DH)

time: 394 us -> 324 us (0.82)
  blocking collectives: 65.8 us -> 16.9 us
  waiting for transfers between devices: 148 us -> 131 us
  starting transfers between devices: 78.7 us -> 73 us
    all_to_all x1 -> x0, blocking collectives: 48.3 us -> none  [gather_over(): return lax.all_to_all(spread, axis, 0, 0, tiled=True)]
    all_to_all x1, waiting for transfers between devices: 38.9 us -> 5.45 us  [on_device(): cols = lax.all_to_all(cols, 'cp', 0, 0, tiled=True)]
    all_to_all x1 -> x3, waiting for transfers between devices: 43.7 us -> 76.7 us  [gather_over(): return lax.all_to_all(spread, axis, 0, 0, tiled=True)]
    all_to_all x2 -> x3, waiting for transfers between devices: 46 us -> 28.1 us  [reduce_over(): received = lax.all_to_all(blocks, axis, 0, 0, tiled=True)]
    all_to_all x2 -> x3, starting transfers between devices: 56.8 us -> 39.6 us  [reduce_over(): received = lax.all_to_all(blocks, axis, 0, 0, tiled=True)]
    all_to_all x1 -> x3, starting transfers between devices: 11.2 us -> 21.1 us  [gather_over(): return lax.all_to_all(spread, axis, 0, 0, tiled=True)]
    unnamed x29 -> x23, local copies, waits for them, and re-layouts: 19.2 us -> 22.1 us
  transfers between devices with their start and end apart: 5 -> 8, of which waited for: 5 -> 8; matrix products, arithmetic and copies ran while one was open for 5% -> 21% of each run, Pallas kernels for 0% -> 0%
where the time goes in v3:
time: 324 us; the launch traced here: 318 us
  waiting for transfers between devices  131 us (40%)
  starting transfers between devices  73 us (23%)
  matrix products  49.4 us (15%)
  local copies, waits for them, and re-layouts  39.1 us (12%)
  blocking collectives  16.9 us (5%)
  other arithmetic  8.17 us (3%)
    all_to_all x3, waiting for transfers between devices, gather_over(): return lax.all_to_all(spread, axis, 0, 0, tiled=True)  76.7 us
    all_to_all x3, starting transfers between devices, reduce_over(): received = lax.all_to_all(blocks, axis, 0, 0, tiled=True)  39.6 us
    all_to_all x3, waiting for transfers between devices, reduce_over(): received = lax.all_to_all(blocks, axis, 0, 0, tiled=True)  28.1 us
    unnamed x23, local copies, waits for them, and re-layouts  22.1 us
    all_to_all x3, starting transfers between devices, gather_over(): return lax.all_to_all(spread, axis, 0, 0, tiled=True)  21.1 us
    all_to_all x1, waiting for transfers between devices, on_device(): by_dp = lax.all_to_all(by_dp, 'dp', 0, 0, tiled=True)  20.4 us
    all_to_all x1, blocking collectives, reduce_over(): received = lax.all_to_all(blocks, axis, 0, 0, tiled=True)  16.9 us
    dot_general x1, matrix products, on_device(): jnp.einsum('giqk,kgd->qgid', weights_bf, value_heads, preferred_element_t...  11.2 us
  transfers between devices with their start and end apart: 8, of which 8 were waited for; matrix products, arithmetic and copies ran while one was open for 21% of the time, Pallas kernels for 0%

profile of v3, /device:TPU:36, one launch (start us, length us, event | category | flops | bytes accessed | tf_op | source)
XLA Modules:
  0.0 318.2 jit_solution(6802776018033048755)
XLA Ops:
  6.6 4.6 %all-to-all-start = ((bf16[4,128,2048]{2,1,0:T(8,128)(2,1)}), bf16[4,128,2048]{2,1,0:T(8,128)(2,1)}, u32[]{:S(2)}, u32[]{:S(2)}) async-start(bf16[4,128,2048]{2,1,0:T(8,128)(2,1)} %bitcast.126), calls=%async_computation | async-start | bytes 4194304 | tf_op jit(solution)/shard_map/all_to_all | solution.py:56
  15.0 20.4 %all-to-all-done = bf16[4,128,2048]{2,1,0:T(8,128)(2,1)} async-done(((bf16[4,128,2048]{2,1,0:T(8,128)(2,1)}), bf16[4,128,2048]{2,1,0:T(8,128)(2,1)}, u32[]{:S(2)}, u32[]{:S(2)}) %all-to-all-start) | async-done | bytes 2097184 | tf_op jit(solution)/shard_map/all_to_all | solution.py:56
  38.6 16.9 %all_to_all.45 = f32[4,128,512]{1,2,0:T(8,128)S(1)} all-to-all(f32[4,128,512]{1,2,0:T(8,128)S(1)} %fusion.12), channel_id=1, replica_groups=mesh['dp'=4,'cp'=16,'tp'=4] {'dp'}, dimensions={0} | all-to-all | bytes 2097152 | tf_op jit(solution)/shard_map/all_to_all | solution.py:33
  57.2 11.3 %all-to-all-start.2 = ((bf16[16,128,512]{1,2,0:T(8,128)(2,1)}), bf16[16,128,512]{1,2,0:T(8,128)(2,1)}, u32[]{:S(2)}, u32[]{:S(2)}) async-start(bf16[16,128,512]{1,2,0:T(8,128)(2,1)} %broadcast_in_dim.20), calls=%async_computation.2 | async-start | bytes 4194304 | tf_op jit(solution)/shard_map/all_to_all | solution.py:29
  74.2 42.1 %all-to-all-done.2 = bf16[16,128,512]{1,2,0:T(8,128)(2,1)} async-done(((bf16[16,128,512]{1,2,0:T(8,128)(2,1)}), bf16[16,128,512]{1,2,0:T(8,128)(2,1)}, u32[]{:S(2)}, u32[]{:S(2)}) %all-to-all-start.2) | async-done | bytes 2097184 | tf_op jit(solution)/shard_map/all_to_all | solution.py:29
  116.2 7.6 %all-to-all-start.3 = ((bf16[16,128,4,128]{1,3,2,0:T(8,128)(2,1)}), bf16[16,128,4,128]{1,3,2,0:T(8,128)(2,1)}, u32[]{:S(2)}, u32[]{:S(2)}) async-start(bf16[16,128,4,128]{1,3,2,0:T(8,128)(2,1)} %copy.107), calls=%async_computation.3 | async-start | bytes 4194304 | tf_op jit(solution)/shard_map/all_to_all | solution.py:51
  129.7 5.7 %copy-done = f32[2,2048,128,8]{2,1,3,0:T(8,128)} copy-done((f32[2,2048,128,8]{2,1,3,0:T(8,128)}, f32[2,2048,128,8]{2,1,3,0:T(8,128)S(1)}, u32[]{:S(2)}) %copy-start) | copy-done | bytes 16777240
  135.4 4.0 %select_reduce_fusion = f32[2,8,128]{2,1,0:T(8,128)S(1)} fusion(f32[2,2048,128,8]{2,1,3,0:T(8,128)S(1)} %get-tuple-element.33, f32[2,8,128]{2,1,0:T(8,128)S(1)} %get-tuple-element.32, pred[128,2048]{0,1:T(8,128)(4,1)S(1)} %compare_and_fusion), kind=kLoop, calls=%fused_computation.5 | loop fusion | flops 20969472 | bytes 17055744 | tf_op jit(solution)/shard_map/reduce_sum | solution.py:80
  139.4 9.5 %fusion.8 = bf16[2048,2,128]{2,0,1:T(8,128)(2,1)S(1)} fusion(bf16[128,2,8,128]{0,3,2,1:T(8,128)(2,1)S(1)} %bitcast.138, f32[2,2048,128,8]{2,1,3,0:T(8,128)} %copy-done, f32[2,8,128]{2,1,0:T(8,128)S(1)} %log_add_fusion, pred[128,2048]{0,1:T(8,128)(4,1)S(1)} %compare_and_fusion), kind=kOutput, calls=%fused_computation.14 | convolution fusion | flops 1095237632 | bytes 18620416 | tf_op jit(solution)/shard_map/giqk,qgid->kgd/dot_general | solution.py:101
  149.9 11.2 %multiply_reduce_fusion = (f32[128,2,8]{0,2,1:T(8,128)S(1)}, bf16[2,128,8,128]{3,1,2,0:T(8,128)(2,1)}) fusion(bf16[128,2,8,128]{0,3,2,1:T(8,128)(2,1)} %bitcast.139, bf16[2048,2,128,1]{0,2,3,1:T(8,128)(2,1)} %bitcast.134, f32[2,2048,128,8]{2,1,3,0:T(8,128)} %copy-done, f32[2,8,128]{2,1,0:T(8,128)S(1)} %log_add_fusion, pred[128,2048]{0,1:T(8,128)(4,1)S(1)} %compare_and_fusion), kind=kOutput, calls=%fused_computation.29 | convolution fusion | flops 1096022016 | bytes 19152896 | tf_op jit(solution)/shard_map/giqk,kgd->qgid/dot_general | solution.py:83
  161.0 5.5 %all-to-all-done.3 = bf16[16,128,4,128]{1,3,2,0:T(8,128)(2,1)} async-done(((bf16[16,128,4,128]{1,3,2,0:T(8,128)(2,1)}), bf16[16,128,4,128]{1,3,2,0:T(8,128)(2,1)}, u32[]{:S(2)}, u32[]{:S(2)}) %all-to-all-start.3) | async-done | bytes 2097184 | tf_op jit(solution)/shard_map/all_to_all | solution.py:51
  167.7 6.0 %all-to-all-start.6 = ((bf16[16,128,256]{1,2,0:T(8,128)(2,1)}), bf16[16,128,256]{1,2,0:T(8,128)(2,1)S(1)}, u32[]{:S(2)}, u32[]{:S(2)}) async-start(bf16[16,128,256]{1,2,0:T(8,128)(2,1)} %copy.115), calls=%async_computation.6 | async-start | bytes 2097152 | tf_op jit(solution)/shard_map/all_to_all | solution.py:33
  173.8 9.4 %fusion.1 = bf16[2,8,128,2048]{2,3,1,0:T(8,128)(2,1)S(1)} fusion(f32[2,2048,128,8]{2,1,3,0:T(8,128)} %copy-done, f32[2,8,128]{2,1,0:T(8,128)S(1)} %bitcast.143, f32[2,8,128]{2,1,0:T(8,128)S(1)} %log_add_fusion, pred[128,2048]{0,1:T(8,128)(4,1)S(1)} %compare_and_fusion, bf16[2048,2,128,1]{0,2,3,1:T(8,128)(2,1)S(1)} %bitcast.135, ...), kind=kOutput, calls=%fused_computation.2 | convolution fusion | flops 1103101952 | bytes 27017216 | tf_op jit(solution)/shard_map/qgid,kgd->giqk/dot_general | solution.py:89
  186.4 3.4 %fusion.7 = bf16[2048,2,128]{2,0,1:T(8,128)(2,1)} fusion(bf16[2,8,128,2048]{2,3,1,0:T(8,128)(2,1)S(1)} %fusion.1, bf16[128,2,8,128]{3,2,1,0:T(8,128)(2,1)S(1)} %bitcast.133), kind=kOutput, calls=%fused_computation.13 | convolution fusion | flops 1074790400 | bytes 9961472 | tf_op jit(solution)/shard_map/giqk,qgid->kgd/dot_general | solution.py:98
  192.9 3.5 %all-to-all-done.6 = bf16[16,128,256]{1,2,0:T(8,128)(2,1)S(1)} async-done(((bf16[16,128,256]{1,2,0:T(8,128)(2,1)}), bf16[16,128,256]{1,2,0:T(8,128)(2,1)S(1)}, u32[]{:S(2)}, u32[]{:S(2)}) %all-to-all-start.6) | async-done | bytes 1048608 | tf_op jit(solution)/shard_map/all_to_all | solution.py:33
  196.5 8.5 %all-to-all-start.4 = ((bf16[16,128,256]{1,2,0:T(8,128)(2,1)}), bf16[16,128,256]{1,2,0:T(8,128)(2,1)S(1)}, u32[]{:S(2)}, u32[]{:S(2)}) async-start(bf16[16,128,256]{1,2,0:T(8,128)(2,1)} %copy.112), calls=%async_computation.4 | async-start | bytes 2097152 | tf_op jit(solution)/shard_map/all_to_all | solution.py:33
  205.2 19.5 %all-to-all-done.4 = bf16[16,128,256]{1,2,0:T(8,128)(2,1)S(1)} async-done(((bf16[16,128,256]{1,2,0:T(8,128)(2,1)}), bf16[16,128,256]{1,2,0:T(8,128)(2,1)S(1)}, u32[]{:S(2)}, u32[]{:S(2)}) %all-to-all-start.4) | async-done | bytes 1048608 | tf_op jit(solution)/shard_map/all_to_all | solution.py:33
  225.8 4.8 %all-to-all-start.7 = ((bf16[16,128,256]{2,1,0:T(8,128)(2,1)}), bf16[16,128,256]{2,1,0:T(8,128)(2,1)S(1)}, u32[]{:S(2)}, u32[]{:S(2)}) async-start(bf16[16,128,256]{2,1,0:T(8,128)(2,1)} %broadcast_in_dim.46), calls=%async_computation.7 | async-start | bytes 2097152 | tf_op jit(solution)/shard_map/all_to_all | solution.py:29
  230.9 17.7 %all-to-all-done.7 = bf16[16,128,256]{2,1,0:T(8,128)(2,1)S(1)} async-done(((bf16[16,128,256]{2,1,0:T(8,128)(2,1)}), bf16[16,128,256]{2,1,0:T(8,128)(2,1)S(1)}, u32[]{:S(2)}, u32[]{:S(2)}) %all-to-all-start.7) | async-done | bytes 1048608 | tf_op jit(solution)/shard_map/all_to_all | solution.py:29
  249.7 5.1 %all-to-all-start.5 = ((bf16[16,128,256]{2,1,0:T(8,128)(2,1)}), bf16[16,128,256]{2,1,0:T(8,128)(2,1)S(1)}, u32[]{:S(2)}, u32[]{:S(2)}) async-start(bf16[16,128,256]{2,1,0:T(8,128)(2,1)} %broadcast_in_dim.24), calls=%async_computation.5 | async-start | bytes 2097152 | tf_op jit(solution)/shard_map/all_to_all | solution.py:29
  257.9 17.0 %all-to-all-done.5 = bf16[16,128,256]{2,1,0:T(8,128)(2,1)S(1)} async-done(((bf16[16,128,256]{2,1,0:T(8,128)(2,1)}), bf16[16,128,256]{2,1,0:T(8,128)(2,1)S(1)}, u32[]{:S(2)}, u32[]{:S(2)}) %all-to-all-start.5) | async-done | bytes 1048608 | tf_op jit(solution)/shard_map/all_to_all | solution.py:29
  279.5 25.1 %all-to-all-start.8 = ((f32[4,128,512]{2,1,0:T(8,128)}), f32[4,128,512]{2,1,0:T(8,128)S(1)}, u32[]{:S(2)}, u32[]{:S(2)}) async-start(f32[4,128,512]{2,1,0:T(8,128)} %pad_maximum_fusion), calls=%async_computation.8 | async-start | bytes 2097152 | tf_op jit(solution)/shard_map/all_to_all | solution.py:33
  306.6 4.6 %fusion.13 = bf16[2,128,8,128]{3,1,2,0:T(8,128)(2,1)S(1)} fusion(bf16[2048,2,128,1]{0,2,3,1:T(8,128)(2,1)S(1)} %bitcast.125, bf16[2,8,128,2048]{2,3,1,0:T(8,128)(2,1)} %copy-done.1), kind=kOutput, calls=%fused_computation.22 | convolution fusion | flops 1074266112 | bytes 9961472 | tf_op jit(solution)/shard_map/giqk,kgd->qgid/dot_general | solution.py:94
  312.3 5.1 %all-to-all-done.8 = f32[4,128,512]{2,1,0:T(8,128)S(1)} async-done(((f32[4,128,512]{2,1,0:T(8,128)}), f32[4,128,512]{2,1,0:T(8,128)S(1)}, u32[]{:S(2)}, u32[]{:S(2)}) %all-to-all-start.8) | async-done | bytes 1048608 | tf_op jit(solution)/shard_map/all_to_all | solution.py:33
  (53 shorter events, 48.9 us)
Async XLA Ops:
  6.6 66.1 %copy-start.6 = (s32[1,4]{1,0:T(1,128)S(1)}, s32[1,4]{1,0:T(1,128)}, u32[]{:S(2)}) copy-start(s32[1,4]{1,0:T(1,128)} %param.11) | copy-start | bytes 52
  6.6 28.8 %all-to-all-start = ((bf16[4,128,2048]{2,1,0:T(8,128)(2,1)}), bf16[4,128,2048]{2,1,0:T(8,128)(2,1)}, u32[]{:S(2)}, u32[]{:S(2)}) async-start(bf16[4,128,2048]{2,1,0:T(8,128)(2,1)} %bitcast.126), calls=%async_computation | async-start | bytes 4194304 | tf_op jit(solution)/shard_map/all_to_all | solution.py:56
  57.2 59.1 %all-to-all-start.2 = ((bf16[16,128,512]{1,2,0:T(8,128)(2,1)}), bf16[16,128,512]{1,2,0:T(8,128)(2,1)}, u32[]{:S(2)}, u32[]{:S(2)}) async-start(bf16[16,128,512]{1,2,0:T(8,128)(2,1)} %broadcast_in_dim.20), calls=%async_computation.2 | async-start | bytes 4194304 | tf_op jit(solution)/shard_map/all_to_all | solution.py:29
  69.8 69.6 %copy-start.5 = (bf16[1,128,2048]{1,2,0:T(8,128)(2,1)}, bf16[1,128,2048]{1,2,0:T(8,128)(2,1)S(1)}, u32[]{:S(2)}) copy-start(bf16[1,128,2048]{1,2,0:T(8,128)(2,1)S(1)} %copy.102) | copy-start | bytes 1572868
  71.1 58.5 %copy-start.2 = (bf16[16,8,16,128]{3,2,1,0:T(8,128)(2,1)}, bf16[16,8,16,128]{3,2,1,0:T(8,128)(2,1)S(1)}, u32[]{:S(2)}) copy-start(bf16[16,8,16,128]{3,2,1,0:T(8,128)(2,1)S(1)} %copy.139) | copy-start | bytes 1572868
  116.2 50.2 %all-to-all-start.3 = ((bf16[16,128,4,128]{1,3,2,0:T(8,128)(2,1)}), bf16[16,128,4,128]{1,3,2,0:T(8,128)(2,1)}, u32[]{:S(2)}, u32[]{:S(2)}) async-start(bf16[16,128,4,128]{1,3,2,0:T(8,128)(2,1)} %copy.107), calls=%async_computation.3 | async-start | bytes 4194304 | tf_op jit(solution)/shard_map/all_to_all | solution.py:51
  129.6 5.7 %copy-start = (f32[2,2048,128,8]{2,1,3,0:T(8,128)}, f32[2,2048,128,8]{2,1,3,0:T(8,128)S(1)}, u32[]{:S(2)}) copy-start(f32[2,2048,128,8]{2,1,3,0:T(8,128)S(1)} %get-tuple-element.33) | copy-start | bytes 50331652
  149.9 23.9 %copy-start.4 = (bf16[2048,256]{0,1:T(8,128)(2,1)S(1)}, bf16[2048,256]{0,1:T(8,128)(2,1)}, u32[]{:S(2)}) copy-start(bf16[2048,256]{0,1:T(8,128)(2,1)} %get-tuple-element.29) | copy-start | bytes 3145732
  167.7 28.7 %all-to-all-start.6 = ((bf16[16,128,256]{1,2,0:T(8,128)(2,1)}), bf16[16,128,256]{1,2,0:T(8,128)(2,1)S(1)}, u32[]{:S(2)}, u32[]{:S(2)}) async-start(bf16[16,128,256]{1,2,0:T(8,128)(2,1)} %copy.115), calls=%async_computation.6 | async-start | bytes 2097152 | tf_op jit(solution)/shard_map/all_to_all | solution.py:33
  173.8 12.6 %copy-start.3 = (bf16[16,8,16,128]{3,2,1,0:T(8,128)(2,1)S(1)}, bf16[16,8,16,128]{3,2,1,0:T(8,128)(2,1)}, u32[]{:S(2)}) copy-start(bf16[16,8,16,128]{3,2,1,0:T(8,128)(2,1)} %copy-done.2) | copy-start | bytes 1572868
  183.2 3.2 %copy-start.1 = (bf16[2,8,128,2048]{2,3,1,0:T(8,128)(2,1)}, bf16[2,8,128,2048]{2,3,1,0:T(8,128)(2,1)S(1)}, u32[]{:S(2)}) copy-start(bf16[2,8,128,2048]{2,3,1,0:T(8,128)(2,1)S(1)} %fusion.1) | copy-start | bytes 25165828
  196.5 28.2 %all-to-all-start.4 = ((bf16[16,128,256]{1,2,0:T(8,128)(2,1)}), bf16[16,128,256]{1,2,0:T(8,128)(2,1)S(1)}, u32[]{:S(2)}, u32[]{:S(2)}) async-start(bf16[16,128,256]{1,2,0:T(8,128)(2,1)} %copy.112), calls=%async_computation.4 | async-start | bytes 2097152 | tf_op jit(solution)/shard_map/all_to_all | solution.py:33
  225.8 22.7 %all-to-all-start.7 = ((bf16[16,128,256]{2,1,0:T(8,128)(2,1)}), bf16[16,128,256]{2,1,0:T(8,128)(2,1)S(1)}, u32[]{:S(2)}, u32[]{:S(2)}) async-start(bf16[16,128,256]{2,1,0:T(8,128)(2,1)} %broadcast_in_dim.46), calls=%async_computation.7 | async-start | bytes 2097152 | tf_op jit(solution)/shard_map/all_to_all | solution.py:29
  249.7 25.2 %all-to-all-start.5 = ((bf16[16,128,256]{2,1,0:T(8,128)(2,1)}), bf16[16,128,256]{2,1,0:T(8,128)(2,1)S(1)}, u32[]{:S(2)}, u32[]{:S(2)}) async-start(bf16[16,128,256]{2,1,0:T(8,128)(2,1)} %broadcast_in_dim.24), calls=%async_computation.5 | async-start | bytes 2097152 | tf_op jit(solution)/shard_map/all_to_all | solution.py:29
  279.5 37.9 %all-to-all-start.8 = ((f32[4,128,512]{2,1,0:T(8,128)}), f32[4,128,512]{2,1,0:T(8,128)S(1)}, u32[]{:S(2)}, u32[]{:S(2)}) async-start(f32[4,128,512]{2,1,0:T(8,128)} %pad_maximum_fusion), calls=%async_computation.8 | async-start | bytes 2097152 | tf_op jit(solution)/shard_map/all_to_all | solution.py:33

commit v4 on v3

--- a/solution.py
+++ b/solution.py
@@ -56,9 +56,10 @@
     by_dp = lax.all_to_all(by_dp, "dp", 0, 0, tiled=True)
     kv_part = jnp.einsum("str,rn->stn", by_dp, both_w, preferred_element_type=jnp.float32)
     kv = reduce_over(kv_part, "dp").astype(jnp.bfloat16)
-    kv_all = gather_over(kv, "cp", cp_count).reshape(seq_rows, 2 * kv_width)
-    key_heads = kv_all[:, :kv_width].reshape(seq_rows, kv_heads, DH)
-    value_heads = kv_all[:, kv_width:].reshape(seq_rows, kv_heads, DH)
+    key_all = gather_over(kv[:, :kv_width], "cp", cp_count)
+    value_all = lax.all_gather(kv[:, kv_width:], "cp", axis=0, tiled=True)
+    key_heads = key_all.reshape(seq_rows, kv_heads, DH)
+    value_heads = value_all.reshape(seq_rows, kv_heads, DH)
 
     own_rows = lax.axis_index("cp") * tok_rows + jnp.arange(tok_rows, dtype=jnp.int32)
     own_place = place(own_rows, tok_rows, seq_rows)
@@ -103,7 +104,9 @@
     )
     value_terms = value_term.reshape(cp_count, tok_rows, kv_width).astype(jnp.bfloat16)
     cols, value_terms = lax.optimization_barrier((cols, value_terms))
-    value_grads = gather_over(reduce_over(value_terms, "cp").astype(jnp.bfloat16), "cp", cp_count)
+    value_grads = lax.all_gather(
+        reduce_over(value_terms, "cp").astype(jnp.bfloat16), "cp", axis=0, tiled=True
+    ).reshape(cp_count, tok_rows, kv_width)
     key_terms = key_term.reshape(cp_count, tok_rows, kv_width).astype(jnp.bfloat16)
     key_grads = gather_over(reduce_over(key_terms, "cp").astype(jnp.bfloat16), "cp", cp_count)
 

time: 324 us -> 332 us (1.025)
  starting transfers between devices: 73 us -> 44.6 us
  waiting for transfers between devices: 131 us -> 154 us
  between operations: 0.98 us -> 14.3 us
    all_gather x0 -> x2, waiting for transfers between devices: none -> 81.4 us  [the longest x1 42.3 us: on_device(): lax.all_gather(reduce_over(value_terms, 'cp').astype(jnp.bfloat16), 'cp',...]
    all_to_all x3 -> x2, waiting for transfers between devices: 76.7 us -> 19.6 us  [gather_over(): return lax.all_to_all(spread, axis, 0, 0, tiled=True)]
    all_to_all x3, starting transfers between devices: 39.6 us -> 18.2 us  [reduce_over(): received = lax.all_to_all(blocks, axis, 0, 0, tiled=True)]
    all_to_all x3 -> x2, starting transfers between devices: 21.1 us -> 15.1 us  [gather_over(): return lax.all_to_all(spread, axis, 0, 0, tiled=True)]
    all_to_all x1, waiting for transfers between devices: 5.45 us -> 0.01 us  [on_device(): cols = lax.all_to_all(cols, 'cp', 0, 0, tiled=True)]
    all_to_all x3, waiting for transfers between devices: 28.1 us -> 32.8 us  [reduce_over(): received = lax.all_to_all(blocks, axis, 0, 0, tiled=True)]
    unnamed x23 -> x21, local copies, waits for them, and re-layouts: 22.1 us -> 23.4 us
  transfers between devices with their start and end apart: 8 -> 9, of which waited for: 8 -> 7; matrix products, arithmetic and copies ran while one was open for 21% -> 22% of each run, Pallas kernels for 0% -> 0%
where the time goes in v4:
time: 332 us; the launch traced here: 329 us
  waiting for transfers between devices  154 us (46%)
  matrix products  50.9 us (15%)
  starting transfers between devices  44.6 us (13%)
  local copies, waits for them, and re-layouts  39.2 us (12%)
  blocking collectives  16.9 us (5%)
  between operations  14.3 us (4%)
  other arithmetic  8.79 us (3%)
    all_gather x1, waiting for transfers between devices, on_device(): lax.all_gather(reduce_over(value_terms, 'cp').astype(jnp.bfloat16), 'cp',...  42.3 us
    all_gather x1, waiting for transfers between devices, on_device(): value_all = lax.all_gather(kv[:, kv_width:], 'cp', axis=0, tiled=True)  39.1 us
    all_to_all x3, waiting for transfers between devices, reduce_over(): received = lax.all_to_all(blocks, axis, 0, 0, tiled=True)  32.8 us
    unnamed x21, local copies, waits for them, and re-layouts  23.4 us
    all_to_all x1, waiting for transfers between devices, on_device(): by_dp = lax.all_to_all(by_dp, 'dp', 0, 0, tiled=True)  20.4 us
    all_to_all x2, waiting for transfers between devices, gather_over(): return lax.all_to_all(spread, axis, 0, 0, tiled=True)  19.6 us
    all_to_all x3, starting transfers between devices, reduce_over(): received = lax.all_to_all(blocks, axis, 0, 0, tiled=True)  18.2 us
    all_to_all x1, blocking collectives, reduce_over(): received = lax.all_to_all(blocks, axis, 0, 0, tiled=True)  16.9 us
  transfers between devices with their start and end apart: 9, of which 7 were waited for; matrix products, arithmetic and copies ran while one was open for 22% of the time, Pallas kernels for 0%

profile of v4, /device:TPU:36, one launch (start us, length us, event | category | flops | bytes accessed | tf_op | source)
XLA Modules:
  0.0 328.8 jit_solution(1458220221327437720)
XLA Ops:
  7.2 3.2 copy.97
  13.1 4.6 %all-to-all-start = ((bf16[4,128,2048]{2,1,0:T(8,128)(2,1)}), bf16[4,128,2048]{2,1,0:T(8,128)(2,1)}, u32[]{:S(2)}, u32[]{:S(2)}) async-start(bf16[4,128,2048]{2,1,0:T(8,128)(2,1)} %bitcast.124), calls=%async_computation | async-start | bytes 4194304 | tf_op jit(solution)/shard_map/all_to_all | solution.py:56
  21.5 20.4 %all-to-all-done = bf16[4,128,2048]{2,1,0:T(8,128)(2,1)} async-done(((bf16[4,128,2048]{2,1,0:T(8,128)(2,1)}), bf16[4,128,2048]{2,1,0:T(8,128)(2,1)}, u32[]{:S(2)}, u32[]{:S(2)}) %all-to-all-start) | async-done | bytes 2097184 | tf_op jit(solution)/shard_map/all_to_all | solution.py:56
  45.1 16.9 %all_to_all.40 = f32[4,128,512]{1,2,0:T(8,128)S(1)} all-to-all(f32[4,128,512]{1,2,0:T(8,128)S(1)} %fusion.12), channel_id=1, replica_groups=mesh['dp'=4,'cp'=16,'tp'=4] {'dp'}, dimensions={0} | all-to-all | bytes 2097152 | tf_op jit(solution)/shard_map/all_to_all | solution.py:33
  63.8 11.2 %all-to-all-start.2 = ((bf16[16,128,256]{1,2,0:T(8,128)(2,1)}), bf16[16,128,256]{1,2,0:T(8,128)(2,1)S(1)}, u32[]{:S(2)}, u32[]{:S(2)}) async-start(bf16[16,128,256]{1,2,0:T(8,128)(2,1)} %broadcast_in_dim.19), calls=%async_computation.2 | async-start | bytes 2097152 | tf_op jit(solution)/shard_map/all_to_all | solution.py:29
  82.1 19.6 %all-to-all-done.2 = bf16[16,128,256]{1,2,0:T(8,128)(2,1)S(1)} async-done(((bf16[16,128,256]{1,2,0:T(8,128)(2,1)}), bf16[16,128,256]{1,2,0:T(8,128)(2,1)S(1)}, u32[]{:S(2)}, u32[]{:S(2)}) %all-to-all-start.2) | async-done | bytes 1048608 | tf_op jit(solution)/shard_map/all_to_all | solution.py:29
  101.7 6.6 %all-to-all-start.3 = ((bf16[16,128,4,128]{1,3,2,0:T(8,128)(2,1)}), bf16[16,128,4,128]{1,3,2,0:T(8,128)(2,1)}, u32[]{:S(2)}, u32[]{:S(2)}) async-start(bf16[16,128,4,128]{1,3,2,0:T(8,128)(2,1)} %copy.108), calls=%async_computation.3 | async-start | bytes 4194304 | tf_op jit(solution)/shard_map/all_to_all | solution.py:51
  109.4 3.8 %fusion.3 = (f32[2,8,128]{2,1,0:T(8,128)S(1)}, f32[2,2048,128,8]{2,1,3,0:T(8,128)S(1)}) fusion(pred[128,2048]{0,1:T(8,128)(4,1)S(1)} %compare_and_fusion, bf16[128,2,8,128]{3,2,1,0:T(8,128)(2,1)} %bitcast.130, bf16[2048,2,128]{0,2,1:T(8,128)(2,1)S(1)} %reshape.141), kind=kOutput, calls=%fused_computation.7 | convolution fusion | flops 1086322688 | bytes 18620416 | tf_op jit(solution)/shard_map/qgid,kgd->giqk/dot_general | solution.py:75
  113.3 5.7 %copy-done = f32[2,2048,128,8]{2,1,3,0:T(8,128)} copy-done((f32[2,2048,128,8]{2,1,3,0:T(8,128)}, f32[2,2048,128,8]{2,1,3,0:T(8,128)S(1)}, u32[]{:S(2)}) %copy-start) | copy-done | bytes 16777240
  119.0 4.0 %select_reduce_fusion = f32[2,8,128]{2,1,0:T(8,128)S(1)} fusion(f32[2,2048,128,8]{2,1,3,0:T(8,128)S(1)} %get-tuple-element.33, f32[2,8,128]{2,1,0:T(8,128)S(1)} %get-tuple-element.32, pred[128,2048]{0,1:T(8,128)(4,1)S(1)} %compare_and_fusion), kind=kLoop, calls=%fused_computation.5 | loop fusion | flops 20969472 | bytes 17055744 | tf_op jit(solution)/shard_map/reduce_sum | solution.py:81
  123.0 9.5 %fusion.8 = bf16[2048,2,128]{2,0,1:T(8,128)(2,1)S(1)} fusion(bf16[128,2,8,128]{0,3,2,1:T(8,128)(2,1)S(1)} %bitcast.136, f32[2,2048,128,8]{2,1,3,0:T(8,128)} %copy-done, f32[2,8,128]{2,1,0:T(8,128)S(1)} %log_add_fusion, pred[128,2048]{0,1:T(8,128)(4,1)S(1)} %compare_and_fusion), kind=kOutput, calls=%fused_computation.14 | convolution fusion | flops 1095237632 | bytes 18620416 | tf_op jit(solution)/shard_map/giqk,qgid->kgd/dot_general | solution.py:102
  133.5 39.1 %all-gather.3.cloned.1.call-done = bf16[2048,256]{0,1:T(8,128)(2,1)} async-done(((bf16[128,256]{0,1:T(8,128)(2,1)}), bf16[2048,256]{0,1:T(8,128)(2,1)}) %all-gather.3.cloned.1.call-update) | async-done | bytes 1048592 | tf_op jit(solution)/shard_map/all_gather | solution.py:60
  172.6 11.1 %multiply_reduce_fusion = (f32[128,2,8]{0,2,1:T(8,128)S(1)}, bf16[2,128,8,128]{3,1,2,0:T(8,128)(2,1)}) fusion(bf16[128,2,8,128]{0,3,2,1:T(8,128)(2,1)} %bitcast.135, bf16[2048,2,128,1]{0,2,3,1:T(8,128)(2,1)} %bitcast.140, f32[2,2048,128,8]{2,1,3,0:T(8,128)} %copy-done, f32[2,8,128]{2,1,0:T(8,128)S(1)} %log_add_fusion, pred[128,2048]{0,1:T(8,128)(4,1)S(1)} %compare_and_fusion), kind=kOutput, calls=%fused_computation.30 | convolution fusion | flops 1096022016 | bytes 19152896 | tf_op jit(solution)/shard_map/giqk,kgd->qgid/dot_general | solution.py:84
  185.0 6.6 %all-to-all-start.6 = ((bf16[16,128,256]{1,2,0:T(8,128)(2,1)}), bf16[16,128,256]{1,2,0:T(8,128)(2,1)S(1)}, u32[]{:S(2)}, u32[]{:S(2)}) async-start(bf16[16,128,256]{1,2,0:T(8,128)(2,1)} %copy.116), calls=%async_computation.6 | async-start | bytes 2097152 | tf_op jit(solution)/shard_map/all_to_all | solution.py:33
  191.7 9.8 %fusion.1 = bf16[2,8,128,2048]{2,3,1,0:T(8,128)(2,1)S(1)} fusion(f32[2,2048,128,8]{2,1,3,0:T(8,128)} %copy-done, f32[2,8,128]{2,1,0:T(8,128)S(1)} %bitcast.142, f32[2,8,128]{2,1,0:T(8,128)S(1)} %log_add_fusion, pred[128,2048]{0,1:T(8,128)(4,1)S(1)} %compare_and_fusion, bf16[2048,2,128,1]{0,2,3,1:T(8,128)(2,1)} %bitcast.141, ...), kind=kOutput, calls=%fused_computation.2 | convolution fusion | flops 1103101952 | bytes 27017216 | tf_op jit(solution)/shard_map/qgid,kgd->giqk/dot_general | solution.py:90
  204.7 3.4 %fusion.7 = bf16[2048,2,128]{2,0,1:T(8,128)(2,1)} fusion(bf16[2,8,128,2048]{2,3,1,0:T(8,128)(2,1)S(1)} %fusion.1, bf16[128,2,8,128]{3,2,1,0:T(8,128)(2,1)S(1)} %bitcast.131), kind=kOutput, calls=%fused_computation.13 | convolution fusion | flops 1074790400 | bytes 9961472 | tf_op jit(solution)/shard_map/giqk,qgid->kgd/dot_general | solution.py:99
  211.1 4.0 %all-to-all-done.6 = bf16[16,128,256]{1,2,0:T(8,128)(2,1)S(1)} async-done(((bf16[16,128,256]{1,2,0:T(8,128)(2,1)}), bf16[16,128,256]{1,2,0:T(8,128)(2,1)S(1)}, u32[]{:S(2)}, u32[]{:S(2)}) %all-to-all-start.6) | async-done | bytes 1048608 | tf_op jit(solution)/shard_map/all_to_all | solution.py:33
  215.1 5.6 %all-to-all-start.4 = ((bf16[16,128,256]{1,2,0:T(8,128)(2,1)}), bf16[16,128,256]{1,2,0:T(8,128)(2,1)S(1)}, u32[]{:S(2)}, u32[]{:S(2)}) async-start(bf16[16,128,256]{1,2,0:T(8,128)(2,1)} %copy.113), calls=%async_computation.4 | async-start | bytes 2097152 | tf_op jit(solution)/shard_map/all_to_all | solution.py:33
  221.6 24.2 %all-to-all-done.4 = bf16[16,128,256]{1,2,0:T(8,128)(2,1)S(1)} async-done(((bf16[16,128,256]{1,2,0:T(8,128)(2,1)}), bf16[16,128,256]{1,2,0:T(8,128)(2,1)S(1)}, u32[]{:S(2)}, u32[]{:S(2)}) %all-to-all-start.4) | async-done | bytes 1048608 | tf_op jit(solution)/shard_map/all_to_all | solution.py:33
  247.1 3.9 %all-to-all-start.5 = ((bf16[16,128,256]{2,1,0:T(8,128)(2,1)}), bf16[16,128,256]{2,1,0:T(8,128)(2,1)S(1)}, u32[]{:S(2)}, u32[]{:S(2)}) async-start(bf16[16,128,256]{2,1,0:T(8,128)(2,1)} %broadcast_in_dim.39), calls=%async_computation.5 | async-start | bytes 2097152 | tf_op jit(solution)/shard_map/all_to_all | solution.py:29
  251.0 42.3 %all-gather.5.cloned.1.call-done = bf16[2048,256]{0,1:T(8,128)(2,1)} async-done(((bf16[128,256]{0,1:T(8,128)(2,1)}), bf16[2048,256]{0,1:T(8,128)(2,1)}) %all-gather.5.cloned.1.call-update) | async-done | bytes 1048592 | tf_op jit(solution)/shard_map/all_gather | solution.py:107
  302.3 6.0 %all-to-all-start.7 = ((f32[4,128,512]{2,1,0:T(8,128)}), f32[4,128,512]{2,1,0:T(8,128)S(1)}, u32[]{:S(2)}, u32[]{:S(2)}) async-start(f32[4,128,512]{2,1,0:T(8,128)} %pad_maximum_fusion), calls=%async_computation.7 | async-start | bytes 2097152 | tf_op jit(solution)/shard_map/all_to_all | solution.py:33
  310.8 4.6 %fusion.13 = bf16[2,128,8,128]{3,1,2,0:T(8,128)(2,1)S(1)} fusion(bf16[2,8,128,2048]{2,3,1,0:T(8,128)(2,1)} %copy-done.1, bf16[2048,2,128,1]{0,2,1,3:T(8,128)(2,1)S(1)} %reshape.149), kind=kOutput, calls=%fused_computation.21 | convolution fusion | flops 1074266112 | bytes 9961472 | tf_op jit(solution)/shard_map/giqk,kgd->qgid/dot_general | solution.py:95
  316.5 4.6 %all-to-all-done.7 = f32[4,128,512]{2,1,0:T(8,128)S(1)} async-done(((f32[4,128,512]{2,1,0:T(8,128)}), f32[4,128,512]{2,1,0:T(8,128)S(1)}, u32[]{:S(2)}, u32[]{:S(2)}) %all-to-all-start.7) | async-done | bytes 1048608 | tf_op jit(solution)/shard_map/all_to_all | solution.py:33
  (56 shorter events, 43.7 us)
Async XLA Ops:
  13.1 67.4 %copy-start.5 = (s32[1,4]{1,0:T(1,128)S(1)}, s32[1,4]{1,0:T(1,128)}, u32[]{:S(2)}) copy-start(s32[1,4]{1,0:T(1,128)} %param.11) | copy-start | bytes 52
  13.1 28.8 %all-to-all-start = ((bf16[4,128,2048]{2,1,0:T(8,128)(2,1)}), bf16[4,128,2048]{2,1,0:T(8,128)(2,1)}, u32[]{:S(2)}, u32[]{:S(2)}) async-start(bf16[4,128,2048]{2,1,0:T(8,128)(2,1)} %bitcast.124), calls=%async_computation | async-start | bytes 4194304 | tf_op jit(solution)/shard_map/all_to_all | solution.py:56
  63.8 37.9 %all-to-all-start.2 = ((bf16[16,128,256]{1,2,0:T(8,128)(2,1)}), bf16[16,128,256]{1,2,0:T(8,128)(2,1)S(1)}, u32[]{:S(2)}, u32[]{:S(2)}) async-start(bf16[16,128,256]{1,2,0:T(8,128)(2,1)} %broadcast_in_dim.19), calls=%async_computation.2 | async-start | bytes 2097152 | tf_op jit(solution)/shard_map/all_to_all | solution.py:29
  75.0 97.6 %all-gather.3.cloned.1.call-start = ((), (), s32[]{:S(2)}) async-start(), calls=%async_computation.8 | async-start | bytes 1114112 | tf_op jit(solution)/shard_map/all_gather | solution.py:60
  101.7 82.1 %all-to-all-start.3 = ((bf16[16,128,4,128]{1,3,2,0:T(8,128)(2,1)}), bf16[16,128,4,128]{1,3,2,0:T(8,128)(2,1)}, u32[]{:S(2)}, u32[]{:S(2)}) async-start(bf16[16,128,4,128]{1,3,2,0:T(8,128)(2,1)} %copy.108), calls=%async_computation.3 | async-start | bytes 4194304 | tf_op jit(solution)/shard_map/all_to_all | solution.py:51
  109.4 13.6 %copy-start.3 = (bf16[1,128,2048]{1,2,0:T(8,128)(2,1)S(1)}, bf16[1,128,2048]{1,2,0:T(8,128)(2,1)}, u32[]{:S(2)}) copy-start(bf16[1,128,2048]{1,2,0:T(8,128)(2,1)} %copy.103) | copy-start | bytes 1572868
  113.3 5.7 %copy-start = (f32[2,2048,128,8]{2,1,3,0:T(8,128)}, f32[2,2048,128,8]{2,1,3,0:T(8,128)S(1)}, u32[]{:S(2)}) copy-start(f32[2,2048,128,8]{2,1,3,0:T(8,128)S(1)} %get-tuple-element.33) | copy-start | bytes 50331652
  172.6 19.1 %copy-start.4 = (bf16[1,128,2048]{1,2,0:T(8,128)(2,1)S(1)}, bf16[1,128,2048]{1,2,0:T(8,128)(2,1)}, u32[]{:S(2)}) copy-start(bf16[1,128,2048]{1,2,0:T(8,128)(2,1)} %copy.103) | copy-start | bytes 1572868
  185.0 30.1 %all-to-all-start.6 = ((bf16[16,128,256]{1,2,0:T(8,128)(2,1)}), bf16[16,128,256]{1,2,0:T(8,128)(2,1)S(1)}, u32[]{:S(2)}, u32[]{:S(2)}) async-start(bf16[16,128,256]{1,2,0:T(8,128)(2,1)} %copy.116), calls=%async_computation.6 | async-start | bytes 2097152 | tf_op jit(solution)/shard_map/all_to_all | solution.py:33
  191.7 13.0 %copy-start.2 = (bf16[16,8,16,128]{3,2,1,0:T(8,128)(2,1)S(1)}, bf16[16,8,16,128]{3,2,1,0:T(8,128)(2,1)}, u32[]{:S(2)}) copy-start(bf16[16,8,16,128]{3,2,1,0:T(8,128)(2,1)} %copy.139) | copy-start | bytes 1572868
  201.5 3.2 copy-start.1
  215.1 30.6 %all-to-all-start.4 = ((bf16[16,128,256]{1,2,0:T(8,128)(2,1)}), bf16[16,128,256]{1,2,0:T(8,128)(2,1)S(1)}, u32[]{:S(2)}, u32[]{:S(2)}) async-start(bf16[16,128,256]{1,2,0:T(8,128)(2,1)} %copy.113), calls=%async_computation.4 | async-start | bytes 2097152 | tf_op jit(solution)/shard_map/all_to_all | solution.py:33
  220.7 72.5 %all-gather.5.cloned.1.call-start = ((), (), s32[]{:S(2)}) async-start(), calls=%async_computation.9 | async-start | bytes 1114112 | tf_op jit(solution)/shard_map/all_gather | solution.py:107
  247.1 50.8 %all-to-all-start.5 = ((bf16[16,128,256]{2,1,0:T(8,128)(2,1)}), bf16[16,128,256]{2,1,0:T(8,128)(2,1)S(1)}, u32[]{:S(2)}, u32[]{:S(2)}) async-start(bf16[16,128,256]{2,1,0:T(8,128)(2,1)} %broadcast_in_dim.39), calls=%async_computation.5 | async-start | bytes 2097152 | tf_op jit(solution)/shard_map/all_to_all | solution.py:29
  302.3 18.8 %all-to-all-start.7 = ((f32[4,128,512]{2,1,0:T(8,128)}), f32[4,128,512]{2,1,0:T(8,128)S(1)}, u32[]{:S(2)}, u32[]{:S(2)}) async-start(f32[4,128,512]{2,1,0:T(8,128)} %pad_maximum_fusion), calls=%async_computation.7 | async-start | bytes 2097152 | tf_op jit(solution)/shard_map/all_to_all | solution.py:33
Sparse Core Ops, SparseCore 0:
  82.2 90.3 all-gather.2
  224.5 68.7 all-gather.4

commit v5 on v3

v5 whole, which is shorter than its diff:
```python
import jax
import jax.numpy as jnp
from jax import lax
from jax.sharding import PartitionSpec as P

DH = 128


NEG_BIG = -1e30


def place(rows, tok_rows, seq_rows):
    stretch = rows // tok_rows
    within = rows % tok_rows
    half_rows = tok_rows // 2
    return jnp.where(
        within < half_rows,
        stretch * half_rows + within,
        seq_rows - (stretch + 1) * half_rows + within - half_rows,
    )


def doc_index(positions, starts):
    return jnp.sum((starts[None, :] <= positions[:, None]).astype(jnp.int32), axis=1) - 1


def gather_over(piece, axis, count):
    spread = jnp.broadcast_to(piece[None], (count,) + piece.shape)
    return lax.all_to_all(spread, axis, 0, 0, tiled=True)


def reduce_over(blocks, axis):
    received = lax.all_to_all(blocks, axis, 0, 0, tiled=True)
    return jnp.sum(received.astype(jnp.float32), axis=0)


def attend(queries, upstream, keys, values, allowed, score_scale):
    scores = (
        jnp.einsum("qid,kd->iqk", queries, keys, preferred_element_type=jnp.float32) * score_scale
    )
    scores = jnp.where(allowed, scores, NEG_BIG)
    top_score = jnp.max(scores, axis=-1)
    expos = jnp.where(allowed, jnp.exp(scores - top_score[..., None]), 0.0)
    log_total = top_score + jnp.log(jnp.sum(expos, axis=-1))
    weights = jnp.where(allowed, jnp.exp(scores - log_total[..., None]), 0.0)
    weights_bf = weights.astype(jnp.bfloat16)
    out_rows = jnp.einsum(
        "iqk,kd->qid", weights_bf, values, preferred_element_type=jnp.float32
    ).astype(jnp.bfloat16)
    delta = jnp.transpose(
        jnp.sum(upstream.astype(jnp.float32) * out_rows.astype(jnp.float32), axis=-1), (1, 0)
    )
    prob_grads = jnp.einsum("qid,kd->iqk", upstream, values, preferred_element_type=jnp.float32)
    score_grads = (weights * (prob_grads - delta[..., None])).astype(jnp.bfloat16)
    query_grad = (
        jnp.einsum("iqk,kd->qid", score_grads, keys, preferred_element_type=jnp.float32)
        * score_scale
    ).astype(jnp.bfloat16)
    key_term = (
        jnp.einsum("iqk,qid->kd", score_grads, queries, preferred_element_type=jnp.float32)
        * score_scale
    )
    value_term = jnp.einsum("iqk,qid->kd", weights_bf, upstream, preferred_element_type=jnp.float32)
    return out_rows, query_grad, key_term, value_term


def on_device(hidden, query, grad_out, k_weight, v_weight, doc_starts):
    inputs = hidden[0]
    tok_rows, width = inputs.shape
    cp_count = lax.axis_size("cp")
    dp_count = lax.axis_size("dp")
    seq_rows = tok_rows * cp_count
    score_scale = DH ** (-0.5)
    kv_width = k_weight.shape[1]
    kv_heads = kv_width // DH
    per_group = query.shape[2] // DH // kv_heads
    starts = doc_starts[0]

    blk = width // (dp_count * cp_count)
    cols = inputs.reshape(tok_rows, dp_count, cp_count, blk).transpose(2, 0, 1, 3)
    cols = lax.all_to_all(cols, "cp", 0, 0, tiled=True)

    both_w = jnp.concatenate([k_weight, v_weight], axis=1)
    w_rows = both_w.shape[0]
    by_dp = inputs.reshape(tok_rows, dp_count, w_rows).transpose(1, 0, 2)
    by_dp = lax.all_to_all(by_dp, "dp", 0, 0, tiled=True)
    kv_part = jnp.einsum("str,rn->stn", by_dp, both_w, preferred_element_type=jnp.float32)
    kv = reduce_over(kv_part, "dp").astype(jnp.bfloat16)

    own_rows = lax.axis_index("cp") * tok_rows + jnp.arange(tok_rows, dtype=jnp.int32)
    own_place = place(own_rows, tok_rows, seq_rows)
    own_doc = doc_index(own_place, starts)
    key_place = place(jnp.arange(seq_rows, dtype=jnp.int32), tok_rows, seq_rows)
    key_doc = doc_index(key_place, starts)
    allowed = (key_place[None, :] <= own_place[:, None]) & (key_doc[None, :] == own_doc[:, None])

    queries = query[0].reshape(tok_rows, kv_heads, per_group, DH)
    upstream = grad_out[0].reshape(tok_rows, kv_heads, per_group, DH)

    outs, qgrads, key_parts, value_parts = [], [], [], []
    for head in range(kv_heads):
        head_kv = jnp.concatenate(
            [kv[:, head * DH:(head + 1) * DH], kv[:, kv_width + head * DH:kv_width + (head + 1) * DH]],
            axis=1,
        )
        head_kv = gather_over(head_kv, "cp", cp_count).reshape(seq_rows, 2 * DH)
        head_out, head_qgrad, key_term, value_term = attend(
            queries[:, head], upstream[:, head], head_kv[:, :DH], head_kv[:, DH:], allowed, score_scale
        )
        outs.append(head_out)
        qgrads.append(head_qgrad)
        terms = jnp.concatenate([key_term, value_term], axis=1)
        terms = terms.reshape(cp_count, tok_rows, 2 * DH).astype(jnp.bfloat16)
        if head == 0:
            cols, terms = lax.optimization_barrier((cols, terms))
        head_grads = gather_over(reduce_over(terms, "cp").astype(jnp.bfloat16), "cp", cp_count)
        key_parts.append(head_grads[..., :DH])
        value_parts.append(head_grads[..., DH:])
    out_rows = jnp.stack(outs, axis=1)
    query_acc = jnp.stack(qgrads, axis=1)
    key_grads = jnp.concatenate(key_parts, axis=2)
    value_grads = jnp.concatenate(value_parts, axis=2)

    value_part = jnp.einsum("ctjb,ctn->jbn", cols, value_grads, preferred_element_type=jnp.float32)
    key_part = jnp.einsum("ctjb,ctn->jbn", cols, key_grads, preferred_element_type=jnp.float32)
    result = reduce_over(jnp.concatenate([key_part, value_part], axis=2), "dp")

    attn_rows = out_rows.reshape(1, tok_rows, kv_heads * per_group * DH)
    query_rows = query_acc.reshape(1, tok_rows, kv_heads * per_group * DH)
    return (attn_rows, query_rows, result[:, :kv_width], result[:, kv_width:])


def solution(mesh):
    placed = (
        P("dp", "cp", None),
        P("dp", "cp", "tp"),
        P("dp", "cp", "tp"),
        P("dp", "tp"),
        P("dp", "tp"),
        P("dp", None),
    )
    return jax.shard_map(
        on_device,
        mesh=mesh,
        in_specs=placed,
        out_specs=(
            P("dp", "cp", "tp"),
            P("dp", "cp", "tp"),
            P(("dp", "cp"), "tp"),
            P(("dp", "cp"), "tp"),
        ),
        check_vma=False,
    )
```

time: 324 us -> 340 us (1.049)
  waiting for transfers between devices: 131 us -> 147 us
  starting transfers between devices: 73 us -> 87.2 us
  local copies, waits for them, and re-layouts: 39.1 us -> 25.7 us
    all_to_all x3 -> x4, starting transfers between devices: 21.1 us -> 34.2 us  [gather_over(): return lax.all_to_all(spread, axis, 0, 0, tiled=True)]
    unnamed x23 -> x28, local copies, waits for them, and re-layouts: 22.1 us -> 13.2 us
    all_to_all x1, waiting for transfers between devices: 5.45 us -> 12.5 us  [on_device(): cols = lax.all_to_all(cols, 'cp', 0, 0, tiled=True)]
    all_to_all x3 -> x4, waiting for transfers between devices: 76.7 us -> 83.6 us  [gather_over(): return lax.all_to_all(spread, axis, 0, 0, tiled=True)]
    convert_element_type x3 -> x0, local copies, waits for them, and re-layouts: 3.58 us -> none  [the longest x2 2.82 us: on_device(): key_term.reshape(cp_count, tok_rows, kv_width).astype(jnp.bfloat16)]
    dot_general x6 -> x12, matrix products: 40.8 us -> 43.8 us  [the longest x2 11.7 us: attend(): jnp.einsum('qid,kd->iqk', queries, keys, preferred_element_type=jnp.float32)]
  transfers between devices with their start and end apart: 8 -> 9, of which waited for: 8 -> 9; matrix products, arithmetic and copies ran while one was open for 21% -> 18% of each run, Pallas kernels for 0% -> 0%
where the time goes in v5:
time: 340 us; the launch traced here: 337 us
  waiting for transfers between devices  147 us (43%)
  starting transfers between devices  87.2 us (26%)
  matrix products  51.7 us (15%)
  local copies, waits for them, and re-layouts  25.7 us (8%)
  blocking collectives  16.9 us (5%)
  other arithmetic  7.53 us (2%)
    all_to_all x4, waiting for transfers between devices, gather_over(): return lax.all_to_all(spread, axis, 0, 0, tiled=True)  83.6 us
    all_to_all x3, starting transfers between devices, reduce_over(): received = lax.all_to_all(blocks, axis, 0, 0, tiled=True)  40.1 us
    all_to_all x4, starting transfers between devices, gather_over(): return lax.all_to_all(spread, axis, 0, 0, tiled=True)  34.2 us
    all_to_all x3, waiting for transfers between devices, reduce_over(): received = lax.all_to_all(blocks, axis, 0, 0, tiled=True)  29.5 us
    all_to_all x1, waiting for transfers between devices, on_device(): by_dp = lax.all_to_all(by_dp, 'dp', 0, 0, tiled=True)  21.2 us
    all_to_all x1, blocking collectives, reduce_over(): received = lax.all_to_all(blocks, axis, 0, 0, tiled=True)  16.9 us
    unnamed x28, local copies, waits for them, and re-layouts  13.2 us
    all_to_all x1, waiting for transfers between devices, on_device(): cols = lax.all_to_all(cols, 'cp', 0, 0, tiled=True)  12.5 us
  transfers between devices with their start and end apart: 9, of which 9 were waited for; matrix products, arithmetic and copies ran while one was open for 18% of the time, Pallas kernels for 0%

profile of v5, /device:TPU:36, one launch (start us, length us, event | category | flops | bytes accessed | tf_op | source)
XLA Modules:
  0.0 336.9 jit_solution(1156056678137522108)
XLA Ops:
  6.7 4.5 %all-to-all-start = ((bf16[4,128,2048]{2,1,0:T(8,128)(2,1)}), bf16[4,128,2048]{2,1,0:T(8,128)(2,1)}, u32[]{:S(2)}, u32[]{:S(2)}) async-start(bf16[4,128,2048]{2,1,0:T(8,128)(2,1)} %bitcast.182), calls=%async_computation | async-start | bytes 4194304 | tf_op jit(solution)/shard_map/all_to_all | solution.py:86
  14.1 21.2 %all-to-all-done = bf16[4,128,2048]{2,1,0:T(8,128)(2,1)} async-done(((bf16[4,128,2048]{2,1,0:T(8,128)(2,1)}), bf16[4,128,2048]{2,1,0:T(8,128)(2,1)}, u32[]{:S(2)}, u32[]{:S(2)}) %all-to-all-start) | async-done | bytes 2097184 | tf_op jit(solution)/shard_map/all_to_all | solution.py:86
  38.6 16.9 %all_to_all.50 = f32[4,128,512]{1,2,0:T(8,128)S(1)} all-to-all(f32[4,128,512]{1,2,0:T(8,128)S(1)} %fusion.17), channel_id=1, replica_groups=mesh['dp'=4,'cp'=16,'tp'=4] {'dp'}, dimensions={0} | all-to-all | bytes 2097152 | tf_op jit(solution)/shard_map/all_to_all | solution.py:33
  56.7 11.2 %all-to-all-start.2 = ((bf16[16,128,256]{2,1,0:T(8,128)(2,1)}), bf16[16,128,256]{2,1,0:T(8,128)(2,1)S(1)}, u32[]{:S(2)}, u32[]{:S(2)}) async-start(bf16[16,128,256]{2,1,0:T(8,128)(2,1)} %broadcast_in_dim.28), calls=%async_computation.2 | async-start | bytes 2097152 | tf_op jit(solution)/shard_map/all_to_all | solution.py:29
  68.0 26.5 %all-to-all-done.2 = bf16[16,128,256]{2,1,0:T(8,128)(2,1)S(1)} async-done(((bf16[16,128,256]{2,1,0:T(8,128)(2,1)}), bf16[16,128,256]{2,1,0:T(8,128)(2,1)S(1)}, u32[]{:S(2)}, u32[]{:S(2)}) %all-to-all-start.2) | async-done | bytes 1048608 | tf_op jit(solution)/shard_map/all_to_all | solution.py:29
  95.6 6.2 %all-to-all-start.3 = ((bf16[16,128,256]{2,1,0:T(8,128)(2,1)}), bf16[16,128,256]{2,1,0:T(8,128)(2,1)}, u32[]{:S(2)}, u32[]{:S(2)}) async-start(bf16[16,128,256]{2,1,0:T(8,128)(2,1)} %broadcast_in_dim.60), calls=%async_computation.3 | async-start | bytes 2097152 | tf_op jit(solution)/shard_map/all_to_all | solution.py:29
  109.0 5.6 %fusion.6 = (f32[8,128]{1,0:T(8,128)S(1)}, f32[2048,128,8]{1,0,2:T(8,128)}) fusion(pred[128,2048]{0,1:T(8,128)(4,1)S(1)} %compare_and_fusion, bf16[128,2,8,128]{0,3,2,1:T(8,128)(2,1)} %bitcast.195, bf16[2048,256]{1,0:T(8,128)(2,1)S(1)} %bitcast.184), kind=kOutput, calls=%fused_computation.14 | convolution fusion | flops 543161344 | bytes 9441280 | tf_op jit(solution)/shard_map/qid,kd->iqk/dot_general | solution.py:39
  114.6 11.4 %all-to-all-done.3 = bf16[16,128,256]{2,1,0:T(8,128)(2,1)} async-done(((bf16[16,128,256]{2,1,0:T(8,128)(2,1)}), bf16[16,128,256]{2,1,0:T(8,128)(2,1)}, u32[]{:S(2)}, u32[]{:S(2)}) %all-to-all-start.3) | async-done | bytes 1048608 | tf_op jit(solution)/shard_map/all_to_all | solution.py:29
  126.0 8.4 %all-to-all-start.4 = ((bf16[16,128,4,128]{1,3,2,0:T(8,128)(2,1)}), bf16[16,128,4,128]{1,3,2,0:T(8,128)(2,1)}, u32[]{:S(2)}, u32[]{:S(2)}) async-start(bf16[16,128,4,128]{1,3,2,0:T(8,128)(2,1)} %copy.152), calls=%async_computation.4 | async-start | bytes 4194304 | tf_op jit(solution)/shard_map/all_to_all | solution.py:81
  134.4 6.1 %select_reduce_fusion.1 = (f32[8,128]{1,0:T(8,128)S(1)}, f32[8,128]{1,0:T(8,128)S(1)}, f32[2048,128,8]{1,0,2:T(8,128)S(1)}) fusion(f32[2048,128,8]{1,0,2:T(8,128)} %get-tuple-element.43, f32[8,128]{1,0:T(8,128)S(1)} %get-tuple-element.42, pred[128,2048]{0,1:T(8,128)(4,1)S(1)} %compare_and_fusion, bf16[128,2,8,128]{0,3,2,1:T(8,128)(2,1)S(1)} %bitcast.196, ...), kind=kOutput, calls=%fused_computation.11 | convolution fusion | flops 553646080 | bytes 17838080 | tf_op jit(solution)/shard_map/qid,kd->iqk/dot_general | solution.py:39
  142.7 3.9 %convolution_convert_fusion = bf16[128,8,128]{2,0,1:T(8,128)(2,1)S(1)} fusion(bf16[2048,256]{1,0:T(8,128)(2,1)} %bitcast.13, f32[2048,128,8]{1,0,2:T(8,128)S(1)} %get-tuple-element.44, f32[8,128]{1,0:T(8,128)S(1)} %log_add_fusion, pred[128,2048]{0,1:T(8,128)(4,1)S(1)} %compare_and_fusion), kind=kOutput, calls=%fused_computation.37 | convolution fusion | flops 547487744 | bytes 9441280 | tf_op jit(solution)/shard_map/iqk,kd->qid/dot_general | solution.py:47
  157.3 12.5 %all-to-all-done.4 = bf16[16,128,4,128]{1,3,2,0:T(8,128)(2,1)} async-done(((bf16[16,128,4,128]{1,3,2,0:T(8,128)(2,1)}), bf16[16,128,4,128]{1,3,2,0:T(8,128)(2,1)}, u32[]{:S(2)}, u32[]{:S(2)}) %all-to-all-start.4) | async-done | bytes 2097184 | tf_op jit(solution)/shard_map/all_to_all | solution.py:81
  171.1 9.6 %all-to-all-start.5 = ((bf16[16,128,256]{1,2,0:T(8,128)(2,1)}), bf16[16,128,256]{1,2,0:T(8,128)(2,1)S(1)}, u32[]{:S(2)}, u32[]{:S(2)}) async-start(bf16[16,128,256]{1,2,0:T(8,128)(2,1)} %copy.156), calls=%async_computation.5 | async-start | bytes 2097152 | tf_op jit(solution)/shard_map/all_to_all | solution.py:33
  180.7 5.2 %fusion.1 = bf16[8,128,2048]{1,2,0:T(8,128)(2,1)S(1)} fusion(f32[2048,128,8]{1,0,2:T(8,128)} %copy-done, f32[8,128]{1,0:T(8,128)S(1)} %bitcast.205, f32[8,128]{1,0:T(8,128)S(1)} %log_add_fusion, pred[128,2048]{0,1:T(8,128)(4,1)S(1)} %compare_and_fusion, bf16[2048,256]{1,0:T(8,128)(2,1)} %bitcast.13, bf16[128,2,8,128]{0,3,2,1:T(8,128)(2,1)S(1)} %bitcast.193), kind=kOutput, calls=%fused_computation.2 | convolution fusion | flops 551550976 | bytes 13639680 | tf_op jit(solution)/shard_map/qid,kd->iqk/dot_general | solution.py:53
  187.5 5.6 %fusion.13 = bf16[2048,128]{0,1:T(8,128)(2,1)S(1)} fusion(bf16[128,2,8,128]{0,3,2,1:T(8,128)(2,1)S(1)} %bitcast.194, f32[2048,128,8]{1,0,2:T(8,128)} %copy-done, f32[8,128]{1,0:T(8,128)S(1)} %log_add_fusion, pred[128,2048]{0,1:T(8,128)(4,1)S(1)} %compare_and_fusion), kind=kOutput, calls=%fused_computation.25 | convolution fusion | flops 547618816 | bytes 9441280 | tf_op jit(solution)/shard_map/iqk,qid->kd/dot_general | solution.py:63
  194.4 5.9 %all-to-all-done.5 = bf16[16,128,256]{1,2,0:T(8,128)(2,1)S(1)} async-done(((bf16[16,128,256]{1,2,0:T(8,128)(2,1)}), bf16[16,128,256]{1,2,0:T(8,128)(2,1)S(1)}, u32[]{:S(2)}, u32[]{:S(2)}) %all-to-all-start.5) | async-done | bytes 1048608 | tf_op jit(solution)/shard_map/all_to_all | solution.py:33
  200.3 3.7 %all-to-all-start.7 = ((bf16[16,128,256]{1,2,0:T(8,128)(2,1)}), bf16[16,128,256]{1,2,0:T(8,128)(2,1)S(1)}, u32[]{:S(2)}, u32[]{:S(2)}) async-start(bf16[16,128,256]{1,2,0:T(8,128)(2,1)} %copy_bitcast_fusion), calls=%async_computation.7 | async-start | bytes 2097152 | tf_op jit(solution)/shard_map/all_to_all | solution.py:33
  204.3 19.9 %all-to-all-done.7 = bf16[16,128,256]{1,2,0:T(8,128)(2,1)S(1)} async-done(((bf16[16,128,256]{1,2,0:T(8,128)(2,1)}), bf16[16,128,256]{1,2,0:T(8,128)(2,1)S(1)}, u32[]{:S(2)}, u32[]{:S(2)}) %all-to-all-start.7) | async-done | bytes 1048608 | tf_op jit(solution)/shard_map/all_to_all | solution.py:33
  225.3 10.7 %all-to-all-start.6 = ((bf16[16,128,256]{2,1,0:T(8,128)(2,1)}), bf16[16,128,256]{2,1,0:T(8,128)(2,1)S(1)}, u32[]{:S(2)}, u32[]{:S(2)}) async-start(bf16[16,128,256]{2,1,0:T(8,128)(2,1)} %broadcast_in_dim.61), calls=%async_computation.6 | async-start | bytes 2097152 | tf_op jit(solution)/shard_map/all_to_all | solution.py:29
  236.3 27.9 %all-to-all-done.6 = bf16[16,128,256]{2,1,0:T(8,128)(2,1)S(1)} async-done(((bf16[16,128,256]{2,1,0:T(8,128)(2,1)}), bf16[16,128,256]{2,1,0:T(8,128)(2,1)S(1)}, u32[]{:S(2)}, u32[]{:S(2)}) %all-to-all-start.6) | async-done | bytes 1048608 | tf_op jit(solution)/shard_map/all_to_all | solution.py:29
  265.3 6.0 %all-to-all-start.8 = ((bf16[16,128,256]{2,1,0:T(8,128)(2,1)}), bf16[16,128,256]{2,1,0:T(8,128)(2,1)S(1)}, u32[]{:S(2)}, u32[]{:S(2)}) async-start(bf16[16,128,256]{2,1,0:T(8,128)(2,1)} %broadcast_in_dim.62), calls=%async_computation.8 | async-start | bytes 2097152 | tf_op jit(solution)/shard_map/all_to_all | solution.py:29
  272.6 17.7 %all-to-all-done.8 = bf16[16,128,256]{2,1,0:T(8,128)(2,1)S(1)} async-done(((bf16[16,128,256]{2,1,0:T(8,128)(2,1)}), bf16[16,128,256]{2,1,0:T(8,128)(2,1)S(1)}, u32[]{:S(2)}, u32[]{:S(2)}) %all-to-all-start.8) | async-done | bytes 1048608 | tf_op jit(solution)/shard_map/all_to_all | solution.py:29
  296.5 26.8 %all-to-all-start.9 = ((f32[4,128,512]{2,1,0:T(8,128)}), f32[4,128,512]{2,1,0:T(8,128)S(1)}, u32[]{:S(2)}, u32[]{:S(2)}) async-start(f32[4,128,512]{2,1,0:T(8,128)} %pad_maximum_fusion), calls=%async_computation.9 | async-start | bytes 2097152 | tf_op jit(solution)/shard_map/all_to_all | solution.py:33
  332.4 3.7 %all-to-all-done.9 = f32[4,128,512]{2,1,0:T(8,128)S(1)} async-done(((f32[4,128,512]{2,1,0:T(8,128)}), f32[4,128,512]{2,1,0:T(8,128)S(1)}, u32[]{:S(2)}, u32[]{:S(2)}) %all-to-all-start.9) | async-done | bytes 1048608 | tf_op jit(solution)/shard_map/all_to_all | solution.py:33
  (74 shorter events, 58.5 us)
Async XLA Ops:
  0.6 10.6 %copy-start.3 = (bf16[2048,256]{1,0:T(8,128)(2,1)S(1)}, bf16[2048,256]{1,0:T(8,128)(2,1)}, u32[]{:S(2)}) copy-start(bf16[2048,256]{1,0:T(8,128)(2,1)} %param.9) | copy-start | bytes 3145732
  6.7 28.7 %all-to-all-start = ((bf16[4,128,2048]{2,1,0:T(8,128)(2,1)}), bf16[4,128,2048]{2,1,0:T(8,128)(2,1)}, u32[]{:S(2)}, u32[]{:S(2)}) async-start(bf16[4,128,2048]{2,1,0:T(8,128)(2,1)} %bitcast.182), calls=%async_computation | async-start | bytes 4194304 | tf_op jit(solution)/shard_map/all_to_all | solution.py:86
  38.5 68.9 %copy-start.7 = (s32[1,4]{1,0:T(1,128)S(1)}, s32[1,4]{1,0:T(1,128)}, u32[]{:S(2)}) copy-start(s32[1,4]{1,0:T(1,128)} %param.11) | copy-start | bytes 52
  56.7 37.9 %all-to-all-start.2 = ((bf16[16,128,256]{2,1,0:T(8,128)(2,1)}), bf16[16,128,256]{2,1,0:T(8,128)(2,1)S(1)}, u32[]{:S(2)}, u32[]{:S(2)}) async-start(bf16[16,128,256]{2,1,0:T(8,128)(2,1)} %broadcast_in_dim.28), calls=%async_computation.2 | async-start | bytes 2097152 | tf_op jit(solution)/shard_map/all_to_all | solution.py:29
  95.6 30.4 %all-to-all-start.3 = ((bf16[16,128,256]{2,1,0:T(8,128)(2,1)}), bf16[16,128,256]{2,1,0:T(8,128)(2,1)}, u32[]{:S(2)}, u32[]{:S(2)}) async-start(bf16[16,128,256]{2,1,0:T(8,128)(2,1)} %broadcast_in_dim.60), calls=%async_computation.3 | async-start | bytes 2097152 | tf_op jit(solution)/shard_map/all_to_all | solution.py:29
  109.0 25.4 %copy-start.5 = (bf16[1,128,2048]{1,2,0:T(8,128)(2,1)S(1)}, bf16[1,128,2048]{1,2,0:T(8,128)(2,1)}, u32[]{:S(2)}) copy-start(bf16[1,128,2048]{1,2,0:T(8,128)(2,1)} %copy.136) | copy-start | bytes 1572868
  126.0 43.8 %all-to-all-start.4 = ((bf16[16,128,4,128]{1,3,2,0:T(8,128)(2,1)}), bf16[16,128,4,128]{1,3,2,0:T(8,128)(2,1)}, u32[]{:S(2)}, u32[]{:S(2)}) async-start(bf16[16,128,4,128]{1,3,2,0:T(8,128)(2,1)} %copy.152), calls=%async_computation.4 | async-start | bytes 4194304 | tf_op jit(solution)/shard_map/all_to_all | solution.py:81
  140.5 6.0 %copy-start = (f32[2048,128,8]{1,0,2:T(8,128)}, f32[2048,128,8]{1,0,2:T(8,128)S(1)}, u32[]{:S(2)}) copy-start(f32[2048,128,8]{1,0,2:T(8,128)S(1)} %get-tuple-element.44) | copy-start | bytes 25165828
  142.6 3.9 %copy-start.4 = (bf16[1,128,2048]{1,2,0:T(8,128)(2,1)S(1)}, bf16[1,128,2048]{1,2,0:T(8,128)(2,1)}, u32[]{:S(2)}) copy-start(bf16[1,128,2048]{1,2,0:T(8,128)(2,1)} %copy.144) | copy-start | bytes 1572868
  142.6 3.9 %slice-start = ((s8[8388608]{0:T(1024)(128)(4,1)}), s8[4194304]{0:T(1024)(128)(4,1)S(1)}, s32[]{:S(2)}) async-start(s8[8388608]{0:T(1024)(128)(4,1)} %bitcast.203), calls=%async_computation.10 | async-start | bytes 8388608
  142.6 4.5 %slice-start.1 = ((s8[8388608]{0:T(1024)(128)(4,1)}), s8[4194304]{0:T(1024)(128)(4,1)S(1)}, s32[]{:S(2)}) async-start(s8[8388608]{0:T(1024)(128)(4,1)} %bitcast.203), calls=%async_computation.11 | async-start | bytes 8388608
  153.1 3.9 %copy-start.1 = (bf16[8,128,2048]{1,2,0:T(8,128)(2,1)}, bf16[8,128,2048]{1,2,0:T(8,128)(2,1)S(1)}, u32[]{:S(2)}) copy-start(bf16[8,128,2048]{1,2,0:T(8,128)(2,1)S(1)} %fusion.3) | copy-start | bytes 12582916
  171.1 29.2 %all-to-all-start.5 = ((bf16[16,128,256]{1,2,0:T(8,128)(2,1)}), bf16[16,128,256]{1,2,0:T(8,128)(2,1)S(1)}, u32[]{:S(2)}, u32[]{:S(2)}) async-start(bf16[16,128,256]{1,2,0:T(8,128)(2,1)} %copy.156), calls=%async_computation.5 | async-start | bytes 2097152 | tf_op jit(solution)/shard_map/all_to_all | solution.py:33
  180.7 5.3 %copy-start.6 = (bf16[1,128,2048]{1,2,0:T(8,128)(2,1)S(1)}, bf16[1,128,2048]{1,2,0:T(8,128)(2,1)}, u32[]{:S(2)}) copy-start(bf16[1,128,2048]{1,2,0:T(8,128)(2,1)} %copy.136) | copy-start | bytes 1572868
  186.0 7.1 %copy-start.2 = (bf16[8,128,2048]{1,2,0:T(8,128)(2,1)}, bf16[8,128,2048]{1,2,0:T(8,128)(2,1)S(1)}, u32[]{:S(2)}) copy-start(bf16[8,128,2048]{1,2,0:T(8,128)(2,1)S(1)} %fusion.1) | copy-start | bytes 12582916
  200.3 23.8 %all-to-all-start.7 = ((bf16[16,128,256]{1,2,0:T(8,128)(2,1)}), bf16[16,128,256]{1,2,0:T(8,128)(2,1)S(1)}, u32[]{:S(2)}, u32[]{:S(2)}) async-start(bf16[16,128,256]{1,2,0:T(8,128)(2,1)} %copy_bitcast_fusion), calls=%async_computation.7 | async-start | bytes 2097152 | tf_op jit(solution)/shard_map/all_to_all | solution.py:33
  225.3 38.9 %all-to-all-start.6 = ((bf16[16,128,256]{2,1,0:T(8,128)(2,1)}), bf16[16,128,256]{2,1,0:T(8,128)(2,1)S(1)}, u32[]{:S(2)}, u32[]{:S(2)}) async-start(bf16[16,128,256]{2,1,0:T(8,128)(2,1)} %broadcast_in_dim.61), calls=%async_computation.6 | async-start | bytes 2097152 | tf_op jit(solution)/shard_map/all_to_all | solution.py:29
  265.3 25.0 %all-to-all-start.8 = ((bf16[16,128,256]{2,1,0:T(8,128)(2,1)}), bf16[16,128,256]{2,1,0:T(8,128)(2,1)S(1)}, u32[]{:S(2)}, u32[]{:S(2)}) async-start(bf16[16,128,256]{2,1,0:T(8,128)(2,1)} %broadcast_in_dim.62), calls=%async_computation.8 | async-start | bytes 2097152 | tf_op jit(solution)/shard_map/all_to_all | solution.py:29
  296.5 39.6 %all-to-all-start.9 = ((f32[4,128,512]{2,1,0:T(8,128)}), f32[4,128,512]{2,1,0:T(8,128)S(1)}, u32[]{:S(2)}, u32[]{:S(2)}) async-start(f32[4,128,512]{2,1,0:T(8,128)} %pad_maximum_fusion), calls=%async_computation.9 | async-start | bytes 2097152 | tf_op jit(solution)/shard_map/all_to_all | solution.py:33

commit v6 on v3

--- a/solution.py
+++ b/solution.py
@@ -47,7 +47,10 @@
     starts = doc_starts[0]
 
     blk = width // (dp_count * cp_count)
-    cols = inputs.reshape(tok_rows, dp_count, cp_count, blk).transpose(2, 0, 1, 3)
+    tp_count = lax.axis_size("tp")
+    quarter = tok_rows // tp_count
+    my_rows = lax.dynamic_slice_in_dim(inputs, lax.axis_index("tp") * quarter, quarter, 0)
+    cols = my_rows.reshape(quarter, dp_count, cp_count, blk).transpose(2, 0, 1, 3)
     cols = lax.all_to_all(cols, "cp", 0, 0, tiled=True)
 
     both_w = jnp.concatenate([k_weight, v_weight], axis=1)
@@ -103,6 +106,7 @@
     )
     value_terms = value_term.reshape(cp_count, tok_rows, kv_width).astype(jnp.bfloat16)
     cols, value_terms = lax.optimization_barrier((cols, value_terms))
+    cols = lax.all_gather(cols, "tp", axis=1, tiled=True)
     value_grads = gather_over(reduce_over(value_terms, "cp").astype(jnp.bfloat16), "cp", cp_count)
     key_terms = key_term.reshape(cp_count, tok_rows, kv_width).astype(jnp.bfloat16)
     key_grads = gather_over(reduce_over(key_terms, "cp").astype(jnp.bfloat16), "cp", cp_count)

time: 324 us -> 339 us (1.046)
  between operations: 0.98 us -> 14.4 us
  waiting for transfers between devices: 131 us -> 136 us
    all_to_all x3, waiting for transfers between devices: 28.1 us -> 38 us  [reduce_over(): received = lax.all_to_all(blocks, axis, 0, 0, tiled=True)]
    all_gather x0 -> x1, waiting for transfers between devices: none -> 6.85 us  [on_device(): cols = lax.all_gather(cols, 'tp', axis=1, tiled=True)]
    all_to_all x3, starting transfers between devices: 39.6 us -> 33.2 us  [reduce_over(): received = lax.all_to_all(blocks, axis, 0, 0, tiled=True)]
    all_to_all x3, waiting for transfers between devices: 76.7 us -> 70.7 us  [gather_over(): return lax.all_to_all(spread, axis, 0, 0, tiled=True)]
    all_to_all x3, starting transfers between devices: 21.1 us -> 27 us  [gather_over(): return lax.all_to_all(spread, axis, 0, 0, tiled=True)]
    all_to_all x1, waiting for transfers between devices: 5.45 us -> 0.01 us  [on_device(): cols = lax.all_to_all(cols, 'cp', 0, 0, tiled=True)]
    unnamed x23 -> x25, local copies, waits for them, and re-layouts: 22.1 us -> 23.5 us
  transfers between devices with their start and end apart: 8 -> 9, of which waited for: 8 -> 8; matrix products, arithmetic and copies ran while one was open for 21% -> 21% of each run, Pallas kernels for 0% -> 0%
where the time goes in v6:
time: 339 us; the launch traced here: 336 us
  waiting for transfers between devices  136 us (40%)
  starting transfers between devices  71.7 us (21%)
  matrix products  48.8 us (14%)
  local copies, waits for them, and re-layouts  40.3 us (12%)
  blocking collectives  16.9 us (5%)
  between operations  14.4 us (4%)
  other arithmetic  8.16 us (2%)
    all_to_all x3, waiting for transfers between devices, gather_over(): return lax.all_to_all(spread, axis, 0, 0, tiled=True)  70.7 us
    all_to_all x3, waiting for transfers between devices, reduce_over(): received = lax.all_to_all(blocks, axis, 0, 0, tiled=True)  38 us
    all_to_all x3, starting transfers between devices, reduce_over(): received = lax.all_to_all(blocks, axis, 0, 0, tiled=True)  33.2 us
    all_to_all x3, starting transfers between devices, gather_over(): return lax.all_to_all(spread, axis, 0, 0, tiled=True)  27 us
    unnamed x25, local copies, waits for them, and re-layouts  23.5 us
    all_to_all x1, waiting for transfers between devices, on_device(): by_dp = lax.all_to_all(by_dp, 'dp', 0, 0, tiled=True)  20.3 us
    all_to_all x1, blocking collectives, reduce_over(): received = lax.all_to_all(blocks, axis, 0, 0, tiled=True)  16.9 us
    dot_general x1, matrix products, on_device(): jnp.einsum('giqk,kgd->qgid', weights_bf, value_heads, preferred_element_t...  11.2 us
  transfers between devices with their start and end apart: 9, of which 8 were waited for; matrix products, arithmetic and copies ran while one was open for 21% of the time, Pallas kernels for 0%

profile of v6, /device:TPU:36, one launch (start us, length us, event | category | flops | bytes accessed | tf_op | source)
XLA Modules:
  0.0 336.1 jit_solution(6638432806748669761)
XLA Ops:
  13.1 3.8 %all-to-all-start = ((bf16[4,128,2048]{2,1,0:T(8,128)(2,1)}), bf16[4,128,2048]{2,1,0:T(8,128)(2,1)S(1)}, u32[]{:S(2)}, u32[]{:S(2)}) async-start(bf16[4,128,2048]{2,1,0:T(8,128)(2,1)} %bitcast.2), calls=%async_computation | async-start | bytes 4194304 | tf_op jit(solution)/shard_map/all_to_all | solution.py:59
  20.7 20.3 %all-to-all-done = bf16[4,128,2048]{2,1,0:T(8,128)(2,1)S(1)} async-done(((bf16[4,128,2048]{2,1,0:T(8,128)(2,1)}), bf16[4,128,2048]{2,1,0:T(8,128)(2,1)S(1)}, u32[]{:S(2)}, u32[]{:S(2)}) %all-to-all-start) | async-done | bytes 2097184 | tf_op jit(solution)/shard_map/all_to_all | solution.py:59
  43.5 16.9 %all_to_all.45 = f32[4,128,512]{1,2,0:T(8,128)S(1)} all-to-all(f32[4,128,512]{1,2,0:T(8,128)S(1)} %fusion.12), channel_id=1, replica_groups=mesh['dp'=4,'cp'=16,'tp'=4] {'dp'}, dimensions={0} | all-to-all | bytes 2097152 | tf_op jit(solution)/shard_map/all_to_all | solution.py:33
  62.1 11.2 %all-to-all-start.2 = ((bf16[16,128,512]{1,2,0:T(8,128)(2,1)}), bf16[16,128,512]{1,2,0:T(8,128)(2,1)S(1)}, u32[]{:S(2)}, u32[]{:S(2)}) async-start(bf16[16,128,512]{1,2,0:T(8,128)(2,1)} %broadcast_in_dim.20), calls=%async_computation.2 | async-start | bytes 4194304 | tf_op jit(solution)/shard_map/all_to_all | solution.py:29
  80.1 40.9 %all-to-all-done.2 = bf16[16,128,512]{1,2,0:T(8,128)(2,1)S(1)} async-done(((bf16[16,128,512]{1,2,0:T(8,128)(2,1)}), bf16[16,128,512]{1,2,0:T(8,128)(2,1)S(1)}, u32[]{:S(2)}, u32[]{:S(2)}) %all-to-all-start.2) | async-done | bytes 2097184 | tf_op jit(solution)/shard_map/all_to_all | solution.py:29
  121.1 7.6 %all-to-all-start.3 = ((bf16[16,32,4,128]{3,1,2,0:T(8,128)(2,1)}), bf16[16,32,4,128]{3,1,2,0:T(8,128)(2,1)}, u32[]{:S(2)}, u32[]{:S(2)}) async-start(bf16[16,32,4,128]{3,1,2,0:T(8,128)(2,1)} %copy.79), calls=%async_computation.3 | async-start | bytes 1048576 | tf_op jit(solution)/shard_map/all_to_all | solution.py:54
  132.9 5.7 %copy-done = f32[2,2048,128,8]{2,1,3,0:T(8,128)} copy-done((f32[2,2048,128,8]{2,1,3,0:T(8,128)}, f32[2,2048,128,8]{2,1,3,0:T(8,128)S(1)}, u32[]{:S(2)}) %copy-start) | copy-done | bytes 16777240
  138.7 4.0 %select_reduce_fusion = f32[2,8,128]{2,1,0:T(8,128)S(1)} fusion(f32[2,2048,128,8]{2,1,3,0:T(8,128)S(1)} %get-tuple-element.29, f32[2,8,128]{2,1,0:T(8,128)S(1)} %get-tuple-element.28, pred[128,2048]{0,1:T(8,128)(4,1)S(1)} %compare_and_fusion), kind=kLoop, calls=%fused_computation.5 | loop fusion | flops 20969472 | bytes 17055744 | tf_op jit(solution)/shard_map/reduce_sum | solution.py:83
  142.7 9.5 %fusion.8 = bf16[2048,2,128]{2,0,1:T(8,128)(2,1)S(1)} fusion(bf16[128,2,8,128]{0,3,2,1:T(8,128)(2,1)S(1)} %bitcast.139, f32[2,2048,128,8]{2,1,3,0:T(8,128)} %copy-done, f32[2,8,128]{2,1,0:T(8,128)S(1)} %log_add_fusion, pred[128,2048]{0,1:T(8,128)(4,1)S(1)} %compare_and_fusion), kind=kOutput, calls=%fused_computation.14 | convolution fusion | flops 1095237632 | bytes 18620416 | tf_op jit(solution)/shard_map/giqk,qgid->kgd/dot_general | solution.py:104
  153.2 11.2 %multiply_reduce_fusion = (f32[128,2,8]{0,2,1:T(8,128)S(1)}, bf16[2,128,8,128]{3,1,2,0:T(8,128)(2,1)}) fusion(bf16[128,2,8,128]{0,3,2,1:T(8,128)(2,1)} %bitcast.140, bf16[2048,2,128,1]{0,2,3,1:T(8,128)(2,1)} %bitcast.135, f32[2,2048,128,8]{2,1,3,0:T(8,128)} %copy-done, f32[2,8,128]{2,1,0:T(8,128)S(1)} %log_add_fusion, pred[128,2048]{0,1:T(8,128)(4,1)S(1)} %compare_and_fusion), kind=kOutput, calls=%fused_computation.29 | convolution fusion | flops 1096022016 | bytes 19152896 | tf_op jit(solution)/shard_map/giqk,kgd->qgid/dot_general | solution.py:86
  165.6 9.6 %all-to-all-start.6 = ((bf16[16,128,256]{1,2,0:T(8,128)(2,1)}), bf16[16,128,256]{1,2,0:T(8,128)(2,1)S(1)}, u32[]{:S(2)}, u32[]{:S(2)}) async-start(bf16[16,128,256]{1,2,0:T(8,128)(2,1)} %copy.88), calls=%async_computation.6 | async-start | bytes 2097152 | tf_op jit(solution)/shard_map/all_to_all | solution.py:33
  175.2 9.4 %fusion.1 = bf16[2,8,128,2048]{2,3,1,0:T(8,128)(2,1)S(1)} fusion(f32[2,2048,128,8]{2,1,3,0:T(8,128)} %copy-done, f32[2,8,128]{2,1,0:T(8,128)S(1)} %bitcast.144, f32[2,8,128]{2,1,0:T(8,128)S(1)} %log_add_fusion, pred[128,2048]{0,1:T(8,128)(4,1)S(1)} %compare_and_fusion, bf16[2048,2,128,1]{0,2,3,1:T(8,128)(2,1)S(1)} %bitcast.136, ...), kind=kOutput, calls=%fused_computation.2 | convolution fusion | flops 1103101952 | bytes 27017216 | tf_op jit(solution)/shard_map/qgid,kgd->giqk/dot_general | solution.py:92
  187.8 3.4 %fusion.7 = bf16[2048,2,128]{2,0,1:T(8,128)(2,1)} fusion(bf16[2,8,128,2048]{2,3,1,0:T(8,128)(2,1)S(1)} %fusion.1, bf16[128,2,8,128]{3,2,1,0:T(8,128)(2,1)S(1)} %bitcast.133), kind=kOutput, calls=%fused_computation.13 | convolution fusion | flops 1074790400 | bytes 9961472 | tf_op jit(solution)/shard_map/giqk,qgid->kgd/dot_general | solution.py:101
  194.2 5.1 %all-to-all-done.6 = bf16[16,128,256]{1,2,0:T(8,128)(2,1)S(1)} async-done(((bf16[16,128,256]{1,2,0:T(8,128)(2,1)}), bf16[16,128,256]{1,2,0:T(8,128)(2,1)S(1)}, u32[]{:S(2)}, u32[]{:S(2)}) %all-to-all-start.6) | async-done | bytes 1048608 | tf_op jit(solution)/shard_map/all_to_all | solution.py:33
  199.3 7.6 %all-to-all-start.4 = ((bf16[16,128,256]{1,2,0:T(8,128)(2,1)}), bf16[16,128,256]{1,2,0:T(8,128)(2,1)S(1)}, u32[]{:S(2)}, u32[]{:S(2)}) async-start(bf16[16,128,256]{1,2,0:T(8,128)(2,1)} %copy.85), calls=%async_computation.4 | async-start | bytes 2097152 | tf_op jit(solution)/shard_map/all_to_all | solution.py:33
  207.2 27.9 %all-to-all-done.4 = bf16[16,128,256]{1,2,0:T(8,128)(2,1)S(1)} async-done(((bf16[16,128,256]{1,2,0:T(8,128)(2,1)}), bf16[16,128,256]{1,2,0:T(8,128)(2,1)S(1)}, u32[]{:S(2)}, u32[]{:S(2)}) %all-to-all-start.4) | async-done | bytes 1048608 | tf_op jit(solution)/shard_map/all_to_all | solution.py:33
  236.2 7.9 %all-to-all-start.7 = ((bf16[16,128,256]{2,1,0:T(8,128)(2,1)}), bf16[16,128,256]{2,1,0:T(8,128)(2,1)S(1)}, u32[]{:S(2)}, u32[]{:S(2)}) async-start(bf16[16,128,256]{2,1,0:T(8,128)(2,1)} %broadcast_in_dim.46), calls=%async_computation.7 | async-start | bytes 2097152 | tf_op jit(solution)/shard_map/all_to_all | solution.py:29
  246.4 21.8 %all-to-all-done.7 = bf16[16,128,256]{2,1,0:T(8,128)(2,1)S(1)} async-done(((bf16[16,128,256]{2,1,0:T(8,128)(2,1)}), bf16[16,128,256]{2,1,0:T(8,128)(2,1)S(1)}, u32[]{:S(2)}, u32[]{:S(2)}) %all-to-all-start.7) | async-done | bytes 1048608 | tf_op jit(solution)/shard_map/all_to_all | solution.py:29
  269.3 7.8 %all-to-all-start.5 = ((bf16[16,128,256]{2,1,0:T(8,128)(2,1)}), bf16[16,128,256]{2,1,0:T(8,128)(2,1)S(1)}, u32[]{:S(2)}, u32[]{:S(2)}) async-start(bf16[16,128,256]{2,1,0:T(8,128)(2,1)} %broadcast_in_dim.24), calls=%async_computation.5 | async-start | bytes 2097152 | tf_op jit(solution)/shard_map/all_to_all | solution.py:29
  277.1 6.9 %all-gather.2.cloned.1.call-done = bf16[16,128,4,128]{3,1,0,2:T(8,128)(2,1)} async-done(((bf16[16,32,4,128]{3,1,0,2:T(8,128)(2,1)}), bf16[16,128,4,128]{3,1,0,2:T(8,128)(2,1)}) %all-gather.2.cloned.1.call-update) | async-done | bytes 2097168 | tf_op jit(solution)/shard_map/all_gather | solution.py:109
  287.1 7.9 %all-to-all-done.5 = bf16[16,128,256]{2,1,0:T(8,128)(2,1)S(1)} async-done(((bf16[16,128,256]{2,1,0:T(8,128)(2,1)}), bf16[16,128,256]{2,1,0:T(8,128)(2,1)S(1)}, u32[]{:S(2)}, u32[]{:S(2)}) %all-to-all-start.5) | async-done | bytes 1048608 | tf_op jit(solution)/shard_map/all_to_all | solution.py:29
  299.6 16.0 %all-to-all-start.8 = ((f32[4,128,512]{2,1,0:T(8,128)}), f32[4,128,512]{2,1,0:T(8,128)S(1)}, u32[]{:S(2)}, u32[]{:S(2)}) async-start(f32[4,128,512]{2,1,0:T(8,128)} %pad_maximum_fusion), calls=%async_computation.8 | async-start | bytes 2097152 | tf_op jit(solution)/shard_map/all_to_all | solution.py:33
  317.6 4.6 %fusion.13 = bf16[2,128,8,128]{3,1,2,0:T(8,128)(2,1)S(1)} fusion(bf16[2048,2,128,1]{0,2,3,1:T(8,128)(2,1)S(1)} %bitcast.125, bf16[2,8,128,2048]{2,3,1,0:T(8,128)(2,1)} %copy-done.1), kind=kOutput, calls=%fused_computation.22 | convolution fusion | flops 1074266112 | bytes 9961472 | tf_op jit(solution)/shard_map/giqk,kgd->qgid/dot_general | solution.py:97
  323.3 5.1 %all-to-all-done.8 = f32[4,128,512]{2,1,0:T(8,128)S(1)} async-done(((f32[4,128,512]{2,1,0:T(8,128)}), f32[4,128,512]{2,1,0:T(8,128)S(1)}, u32[]{:S(2)}, u32[]{:S(2)}) %all-to-all-start.8) | async-done | bytes 1048608 | tf_op jit(solution)/shard_map/all_to_all | solution.py:33
  (59 shorter events, 49.5 us)
Async XLA Ops:
  13.1 65.5 %copy-start.6 = (s32[1,4]{1,0:T(1,128)S(1)}, s32[1,4]{1,0:T(1,128)}, u32[]{:S(2)}) copy-start(s32[1,4]{1,0:T(1,128)} %param.11) | copy-start | bytes 52
  13.1 27.9 %all-to-all-start = ((bf16[4,128,2048]{2,1,0:T(8,128)(2,1)}), bf16[4,128,2048]{2,1,0:T(8,128)(2,1)S(1)}, u32[]{:S(2)}, u32[]{:S(2)}) async-start(bf16[4,128,2048]{2,1,0:T(8,128)(2,1)} %bitcast.2), calls=%async_computation | async-start | bytes 4194304 | tf_op jit(solution)/shard_map/all_to_all | solution.py:59
  62.1 58.9 %all-to-all-start.2 = ((bf16[16,128,512]{1,2,0:T(8,128)(2,1)}), bf16[16,128,512]{1,2,0:T(8,128)(2,1)S(1)}, u32[]{:S(2)}, u32[]{:S(2)}) async-start(bf16[16,128,512]{1,2,0:T(8,128)(2,1)} %broadcast_in_dim.20), calls=%async_computation.2 | async-start | bytes 4194304 | tf_op jit(solution)/shard_map/all_to_all | solution.py:29
  74.6 68.0 %copy-start.5 = (bf16[1,128,2048]{1,2,0:T(8,128)(2,1)}, bf16[1,128,2048]{1,2,0:T(8,128)(2,1)S(1)}, u32[]{:S(2)}) copy-start(bf16[1,128,2048]{1,2,0:T(8,128)(2,1)S(1)} %copy.75) | copy-start | bytes 1572868
  76.0 56.9 %copy-start.2 = (bf16[16,8,16,128]{3,2,1,0:T(8,128)(2,1)}, bf16[16,8,16,128]{3,2,1,0:T(8,128)(2,1)S(1)}, u32[]{:S(2)}) copy-start(bf16[16,8,16,128]{3,2,1,0:T(8,128)(2,1)S(1)} %copy.112) | copy-start | bytes 1572868
  121.1 43.3 %all-to-all-start.3 = ((bf16[16,32,4,128]{3,1,2,0:T(8,128)(2,1)}), bf16[16,32,4,128]{3,1,2,0:T(8,128)(2,1)}, u32[]{:S(2)}, u32[]{:S(2)}) async-start(bf16[16,32,4,128]{3,1,2,0:T(8,128)(2,1)} %copy.79), calls=%async_computation.3 | async-start | bytes 1048576 | tf_op jit(solution)/shard_map/all_to_all | solution.py:54
  132.9 5.7 %copy-start = (f32[2,2048,128,8]{2,1,3,0:T(8,128)}, f32[2,2048,128,8]{2,1,3,0:T(8,128)S(1)}, u32[]{:S(2)}) copy-start(f32[2,2048,128,8]{2,1,3,0:T(8,128)S(1)} %get-tuple-element.29) | copy-start | bytes 50331652
  153.1 22.0 %copy-start.4 = (bf16[2048,256]{0,1:T(8,128)(2,1)S(1)}, bf16[2048,256]{0,1:T(8,128)(2,1)}, u32[]{:S(2)}) copy-start(bf16[2048,256]{0,1:T(8,128)(2,1)} %get-tuple-element.25) | copy-start | bytes 3145732
  165.6 33.7 %all-to-all-start.6 = ((bf16[16,128,256]{1,2,0:T(8,128)(2,1)}), bf16[16,128,256]{1,2,0:T(8,128)(2,1)S(1)}, u32[]{:S(2)}, u32[]{:S(2)}) async-start(bf16[16,128,256]{1,2,0:T(8,128)(2,1)} %copy.88), calls=%async_computation.6 | async-start | bytes 2097152 | tf_op jit(solution)/shard_map/all_to_all | solution.py:33
  175.1 12.6 %copy-start.3 = (bf16[16,8,16,128]{3,2,1,0:T(8,128)(2,1)S(1)}, bf16[16,8,16,128]{3,2,1,0:T(8,128)(2,1)}, u32[]{:S(2)}) copy-start(bf16[16,8,16,128]{3,2,1,0:T(8,128)(2,1)} %copy-done.2) | copy-start | bytes 1572868
  184.5 3.2 copy-start.1
  199.3 35.8 %all-to-all-start.4 = ((bf16[16,128,256]{1,2,0:T(8,128)(2,1)}), bf16[16,128,256]{1,2,0:T(8,128)(2,1)S(1)}, u32[]{:S(2)}, u32[]{:S(2)}) async-start(bf16[16,128,256]{1,2,0:T(8,128)(2,1)} %copy.85), calls=%async_computation.4 | async-start | bytes 2097152 | tf_op jit(solution)/shard_map/all_to_all | solution.py:33
  236.2 32.0 %all-to-all-start.7 = ((bf16[16,128,256]{2,1,0:T(8,128)(2,1)}), bf16[16,128,256]{2,1,0:T(8,128)(2,1)S(1)}, u32[]{:S(2)}, u32[]{:S(2)}) async-start(bf16[16,128,256]{2,1,0:T(8,128)(2,1)} %broadcast_in_dim.46), calls=%async_computation.7 | async-start | bytes 2097152 | tf_op jit(solution)/shard_map/all_to_all | solution.py:29
  244.1 39.8 %all-gather.2.cloned.1.call-start = ((), (), s32[]{:S(2)}) async-start(), calls=%async_computation.9 | async-start | bytes 2621440 | tf_op jit(solution)/shard_map/all_gather | solution.py:109
  269.3 25.8 %all-to-all-start.5 = ((bf16[16,128,256]{2,1,0:T(8,128)(2,1)}), bf16[16,128,256]{2,1,0:T(8,128)(2,1)S(1)}, u32[]{:S(2)}, u32[]{:S(2)}) async-start(bf16[16,128,256]{2,1,0:T(8,128)(2,1)} %broadcast_in_dim.24), calls=%async_computation.5 | async-start | bytes 2097152 | tf_op jit(solution)/shard_map/all_to_all | solution.py:29
  299.6 28.8 %all-to-all-start.8 = ((f32[4,128,512]{2,1,0:T(8,128)}), f32[4,128,512]{2,1,0:T(8,128)S(1)}, u32[]{:S(2)}, u32[]{:S(2)}) async-start(f32[4,128,512]{2,1,0:T(8,128)} %pad_maximum_fusion), calls=%async_computation.8 | async-start | bytes 2097152 | tf_op jit(solution)/shard_map/all_to_all | solution.py:33
Sparse Core Ops, SparseCore 0:
  247.3 36.5 all-gather.1

commit v7 on v6

--- a/solution.py
+++ b/solution.py
@@ -106,10 +106,17 @@
     )
     value_terms = value_term.reshape(cp_count, tok_rows, kv_width).astype(jnp.bfloat16)
     cols, value_terms = lax.optimization_barrier((cols, value_terms))
-    cols = lax.all_gather(cols, "tp", axis=1, tiled=True)
-    value_grads = gather_over(reduce_over(value_terms, "cp").astype(jnp.bfloat16), "cp", cp_count)
+    cols = gather_over(cols, "tp", tp_count)
+    cols = jnp.moveaxis(cols, 0, 1).reshape(cp_count, tok_rows, dp_count, blk)
+    value_own = reduce_over(value_terms, "cp").astype(jnp.bfloat16)
     key_terms = key_term.reshape(cp_count, tok_rows, kv_width).astype(jnp.bfloat16)
-    key_grads = gather_over(reduce_over(key_terms, "cp").astype(jnp.bfloat16), "cp", cp_count)
+    mixed = jnp.concatenate(
+        [jnp.broadcast_to(value_own[None], (cp_count, tok_rows, kv_width)), key_terms], axis=2
+    )
+    mixed = lax.all_to_all(mixed, "cp", 0, 0, tiled=True)
+    value_grads = mixed[..., :kv_width]
+    key_own = jnp.sum(mixed[..., kv_width:].astype(jnp.float32), axis=0).astype(jnp.bfloat16)
+    key_grads = gather_over(key_own, "cp", cp_count)
 
     value_part = jnp.einsum("ctjb,ctn->jbn", cols, value_grads, preferred_element_type=jnp.float32)
     key_part = jnp.einsum("ctjb,ctn->jbn", cols, key_grads, preferred_element_type=jnp.float32)

time: 339 us -> 344 us (1.015)
  between operations: 14.4 us -> 0.96 us
  local copies, waits for them, and re-layouts: 40.3 us -> 48.1 us
  waiting for transfers between devices: 136 us -> 142 us
    all_to_all x0 -> x1, waiting for transfers between devices: none -> 40.4 us  [on_device(): mixed = lax.all_to_all(mixed, 'cp', 0, 0, tiled=True)]
    all_to_all x3 -> x2, waiting for transfers between devices: 38 us -> 5.09 us  [reduce_over(): received = lax.all_to_all(blocks, axis, 0, 0, tiled=True)]
    all_to_all x0 -> x1, starting transfers between devices: none -> 9.62 us  [on_device(): mixed = lax.all_to_all(mixed, 'cp', 0, 0, tiled=True)]
    convert_element_type x2, local copies, waits for them, and re-layouts: 2.81 us -> 10.2 us  [on_device(): key_term.reshape(cp_count, tok_rows, kv_width).astype(jnp.bfloat16)]
    all_gather x1 -> x0, waiting for transfers between devices: 6.85 us -> none  [on_device(): cols = lax.all_gather(cols, 'tp', axis=1, tiled=True)]
    all_to_all x3, starting transfers between devices: 27 us -> 20.7 us  [gather_over(): return lax.all_to_all(spread, axis, 0, 0, tiled=True)]
    all_to_all x3, waiting for transfers between devices: 70.7 us -> 75.7 us  [gather_over(): return lax.all_to_all(spread, axis, 0, 0, tiled=True)]
    unnamed x25 -> x28, local copies, waits for them, and re-layouts: 23.5 us -> 19.6 us
  transfers between devices with their start and end apart: 9 -> 8, of which waited for: 8 -> 6; matrix products, arithmetic and copies ran while one was open for 21% -> 23% of each run, Pallas kernels for 0% -> 0%
where the time goes in v7:
time: 344 us; the launch traced here: 339 us
  waiting for transfers between devices  142 us (41%)
  starting transfers between devices  72.3 us (21%)
  local copies, waits for them, and re-layouts  48.1 us (14%)
  matrix products  47 us (14%)
  blocking collectives  16.9 us (5%)
  other arithmetic  11 us (3%)
    all_to_all x3, waiting for transfers between devices, gather_over(): return lax.all_to_all(spread, axis, 0, 0, tiled=True)  75.7 us
    all_to_all x1, waiting for transfers between devices, on_device(): mixed = lax.all_to_all(mixed, 'cp', 0, 0, tiled=True)  40.4 us
    all_to_all x2, starting transfers between devices, reduce_over(): received = lax.all_to_all(blocks, axis, 0, 0, tiled=True)  30.6 us
    all_to_all x1, waiting for transfers between devices, on_device(): by_dp = lax.all_to_all(by_dp, 'dp', 0, 0, tiled=True)  21.1 us
    all_to_all x3, starting transfers between devices, gather_over(): return lax.all_to_all(spread, axis, 0, 0, tiled=True)  20.7 us
    unnamed x28, local copies, waits for them, and re-layouts  19.6 us
    all_to_all x1, blocking collectives, reduce_over(): received = lax.all_to_all(blocks, axis, 0, 0, tiled=True)  16.9 us
    dot_general x1, matrix products, on_device(): jnp.einsum('giqk,kgd->qgid', weights_bf, value_heads, preferred_element_t...  11.1 us
  transfers between devices with their start and end apart: 8, of which 6 were waited for; matrix products, arithmetic and copies ran while one was open for 23% of the time, Pallas kernels for 0%

profile of v7, /device:TPU:36, one launch (start us, length us, event | category | flops | bytes accessed | tf_op | source)
XLA Modules:
  0.0 338.5 jit_solution(15991538413497815144)
XLA Ops:
  0.6 3.3 copy.73
  6.6 3.7 %all-to-all-start = ((bf16[4,128,2048]{2,1,0:T(8,128)(2,1)}), bf16[4,128,2048]{2,1,0:T(8,128)(2,1)S(1)}, u32[]{:S(2)}, u32[]{:S(2)}) async-start(bf16[4,128,2048]{2,1,0:T(8,128)(2,1)} %bitcast.2), calls=%async_computation | async-start | bytes 4194304 | tf_op jit(solution)/shard_map/all_to_all | solution.py:59
  13.2 21.1 %all-to-all-done = bf16[4,128,2048]{2,1,0:T(8,128)(2,1)S(1)} async-done(((bf16[4,128,2048]{2,1,0:T(8,128)(2,1)}), bf16[4,128,2048]{2,1,0:T(8,128)(2,1)S(1)}, u32[]{:S(2)}, u32[]{:S(2)}) %all-to-all-start) | async-done | bytes 2097184 | tf_op jit(solution)/shard_map/all_to_all | solution.py:59
  36.9 16.9 %all_to_all.45 = f32[4,128,512]{1,2,0:T(8,128)S(1)} all-to-all(f32[4,128,512]{1,2,0:T(8,128)S(1)} %fusion.12), channel_id=1, replica_groups=mesh['dp'=4,'cp'=16,'tp'=4] {'dp'}, dimensions={0} | all-to-all | bytes 2097152 | tf_op jit(solution)/shard_map/all_to_all | solution.py:33
  55.5 11.2 %all-to-all-start.2 = ((bf16[16,128,512]{1,2,0:T(8,128)(2,1)}), bf16[16,128,512]{1,2,0:T(8,128)(2,1)S(1)}, u32[]{:S(2)}, u32[]{:S(2)}) async-start(bf16[16,128,512]{1,2,0:T(8,128)(2,1)} %broadcast_in_dim.22), calls=%async_computation.2 | async-start | bytes 4194304 | tf_op jit(solution)/shard_map/all_to_all | solution.py:29
  74.6 39.9 %all-to-all-done.2 = bf16[16,128,512]{1,2,0:T(8,128)(2,1)S(1)} async-done(((bf16[16,128,512]{1,2,0:T(8,128)(2,1)}), bf16[16,128,512]{1,2,0:T(8,128)(2,1)S(1)}, u32[]{:S(2)}, u32[]{:S(2)}) %all-to-all-start.2) | async-done | bytes 2097184 | tf_op jit(solution)/shard_map/all_to_all | solution.py:29
  114.5 7.6 %all-to-all-start.3 = ((bf16[16,32,4,128]{3,2,1,0:T(4,128)(2,1)}), bf16[16,32,4,128]{3,2,1,0:T(4,128)(2,1)}, u32[]{:S(2)}, u32[]{:S(2)}) async-start(bf16[16,32,4,128]{3,2,1,0:T(4,128)(2,1)} %copy.83), calls=%async_computation.3 | async-start | bytes 1048576 | tf_op jit(solution)/shard_map/all_to_all | solution.py:54
  126.3 4.0 %select_reduce_fusion = f32[2,8,128]{2,1,0:T(8,128)S(1)} fusion(f32[2,2048,128,8]{2,1,3,0:T(8,128)S(1)} %get-tuple-element.29, f32[2,8,128]{2,1,0:T(8,128)S(1)} %get-tuple-element.28, pred[128,2048]{0,1:T(8,128)(4,1)S(1)} %compare_and_fusion), kind=kLoop, calls=%fused_computation.5 | loop fusion | flops 20969472 | bytes 17055744 | tf_op jit(solution)/shard_map/reduce_sum | solution.py:83
  132.0 9.5 %fusion.8 = bf16[2048,2,128]{2,0,1:T(8,128)(2,1)S(1)} fusion(bf16[128,2,8,128]{0,3,2,1:T(8,128)(2,1)S(1)} %bitcast.141, f32[2,2048,128,8]{2,1,3,0:T(8,128)} %copy-done, f32[2,8,128]{2,1,0:T(8,128)S(1)} %log_add_fusion, pred[128,2048]{0,1:T(8,128)(4,1)S(1)} %compare_and_fusion), kind=kOutput, calls=%fused_computation.14 | convolution fusion | flops 1095237632 | bytes 18620416 | tf_op jit(solution)/shard_map/giqk,qgid->kgd/dot_general | solution.py:104
  142.6 11.1 %multiply_reduce_fusion = (f32[128,2,8]{0,2,1:T(8,128)S(1)}, bf16[2,128,8,128]{3,1,2,0:T(8,128)(2,1)}) fusion(bf16[128,2,8,128]{0,3,2,1:T(8,128)(2,1)} %bitcast.139, bf16[2048,2,128,1]{0,2,3,1:T(8,128)(2,1)} %bitcast.135, f32[2,2048,128,8]{2,1,3,0:T(8,128)} %copy-done, f32[2,8,128]{2,1,0:T(8,128)S(1)} %log_add_fusion, pred[128,2048]{0,1:T(8,128)(4,1)S(1)} %compare_and_fusion), kind=kOutput, calls=%fused_computation.31 | convolution fusion | flops 1096022016 | bytes 19152896 | tf_op jit(solution)/shard_map/giqk,kgd->qgid/dot_general | solution.py:86
  155.0 9.5 %all-to-all-start.5 = ((bf16[16,128,256]{1,2,0:T(8,128)(2,1)}), bf16[16,128,256]{1,2,0:T(8,128)(2,1)S(1)}, u32[]{:S(2)}, u32[]{:S(2)}) async-start(bf16[16,128,256]{1,2,0:T(8,128)(2,1)} %copy.88), calls=%async_computation.5 | async-start | bytes 2097152 | tf_op jit(solution)/shard_map/all_to_all | solution.py:33
  164.6 9.4 %fusion.1 = bf16[2,8,128,2048]{2,3,1,0:T(8,128)(2,1)S(1)} fusion(f32[2,2048,128,8]{2,1,3,0:T(8,128)} %copy-done, f32[2,8,128]{2,1,0:T(8,128)S(1)} %bitcast.144, f32[2,8,128]{2,1,0:T(8,128)S(1)} %log_add_fusion, pred[128,2048]{0,1:T(8,128)(4,1)S(1)} %compare_and_fusion, bf16[2048,2,128,1]{0,2,3,1:T(8,128)(2,1)S(1)} %bitcast.136, ...), kind=kOutput, calls=%fused_computation.2 | convolution fusion | flops 1103101952 | bytes 27017216 | tf_op jit(solution)/shard_map/qgid,kgd->giqk/dot_general | solution.py:92
  174.0 3.2 copy-done.1
  179.6 8.7 %copy.116 = bf16[2048,2,128]{2,1,0:T(2,128)(2,1)S(1)} copy(bf16[2048,2,128]{2,0,1:T(8,128)(2,1)S(1)} %fusion.7) | data formatting | bytes 2097152 | tf_op jit(solution)/shard_map/convert_element_type | solution.py:112
  192.9 9.6 %all-to-all-start.6 = ((bf16[16,128,512]{2,1,0:T(8,128)(2,1)}), bf16[16,128,512]{2,1,0:T(8,128)(2,1)S(1)}, u32[]{:S(2)}, u32[]{:S(2)}) async-start(bf16[16,128,512]{2,1,0:T(8,128)(2,1)} %pad_maximum_fusion), calls=%async_computation.6 | async-start | bytes 4194304 | tf_op jit(solution)/shard_map/all_to_all | solution.py:116
  204.5 40.4 %all-to-all-done.6 = bf16[16,128,512]{2,1,0:T(8,128)(2,1)S(1)} async-done(((bf16[16,128,512]{2,1,0:T(8,128)(2,1)}), bf16[16,128,512]{2,1,0:T(8,128)(2,1)S(1)}, u32[]{:S(2)}, u32[]{:S(2)}) %all-to-all-start.6) | async-done | bytes 2097184 | tf_op jit(solution)/shard_map/all_to_all | solution.py:116
  244.9 3.2 broadcast_in_dim.26
  248.2 4.9 %all-to-all-start.4 = ((bf16[4,16,32,4,128]{4,2,3,1,0:T(8,128)(2,1)}), bf16[4,16,32,4,128]{4,2,3,1,0:T(8,128)(2,1)}, u32[]{:S(2)}, u32[]{:S(2)}) async-start(bf16[4,16,32,4,128]{4,2,3,1,0:T(8,128)(2,1)} %broadcast_in_dim.26), calls=%async_computation.4 | async-start | bytes 4194304 | tf_op jit(solution)/shard_map/all_to_all | solution.py:29
  253.2 20.2 %all-to-all-done.4 = bf16[4,16,32,4,128]{4,2,3,1,0:T(8,128)(2,1)} async-done(((bf16[4,16,32,4,128]{4,2,3,1,0:T(8,128)(2,1)}), bf16[4,16,32,4,128]{4,2,3,1,0:T(8,128)(2,1)}, u32[]{:S(2)}, u32[]{:S(2)}) %all-to-all-start.4) | async-done | bytes 2097184 | tf_op jit(solution)/shard_map/all_to_all | solution.py:29
  274.6 4.6 %all-to-all-start.7 = ((bf16[16,128,256]{2,1,0:T(8,128)(2,1)}), bf16[16,128,256]{2,1,0:T(8,128)(2,1)}, u32[]{:S(2)}, u32[]{:S(2)}) async-start(bf16[16,128,256]{2,1,0:T(8,128)(2,1)} %broadcast_in_dim.28), calls=%async_computation.7 | async-start | bytes 2097152 | tf_op jit(solution)/shard_map/all_to_all | solution.py:29
  284.1 15.5 %all-to-all-done.7 = bf16[16,128,256]{2,1,0:T(8,128)(2,1)} async-done(((bf16[16,128,256]{2,1,0:T(8,128)(2,1)}), bf16[16,128,256]{2,1,0:T(8,128)(2,1)}, u32[]{:S(2)}, u32[]{:S(2)}) %all-to-all-start.7) | async-done | bytes 1048608 | tf_op jit(solution)/shard_map/all_to_all | solution.py:29
  303.8 21.1 %all-to-all-start.8 = ((f32[4,128,512]{2,1,0:T(8,128)}), f32[4,128,512]{2,1,0:T(8,128)S(1)}, u32[]{:S(2)}, u32[]{:S(2)}) async-start(f32[4,128,512]{2,1,0:T(8,128)} %pad_maximum_fusion.1), calls=%async_computation.8 | async-start | bytes 2097152 | tf_op jit(solution)/shard_map/all_to_all | solution.py:33
  327.0 4.7 %fusion.13 = bf16[2,128,8,128]{3,1,2,0:T(8,128)(2,1)S(1)} fusion(bf16[2048,2,128,1]{0,2,3,1:T(8,128)(2,1)S(1)} %bitcast.127, bf16[2,8,128,2048]{2,3,1,0:T(8,128)(2,1)} %copy-done.1), kind=kOutput, calls=%fused_computation.23 | convolution fusion | flops 1074266112 | bytes 9961472 | tf_op jit(solution)/shard_map/giqk,kgd->qgid/dot_general | solution.py:97
  332.6 5.1 %all-to-all-done.8 = f32[4,128,512]{2,1,0:T(8,128)S(1)} async-done(((f32[4,128,512]{2,1,0:T(8,128)}), f32[4,128,512]{2,1,0:T(8,128)S(1)}, u32[]{:S(2)}, u32[]{:S(2)}) %all-to-all-start.8) | async-done | bytes 1048608 | tf_op jit(solution)/shard_map/all_to_all | solution.py:33
  (61 shorter events, 49.0 us)
Async XLA Ops:
  0.6 9.7 %copy-start.5 = (bf16[2048,256]{1,0:T(8,128)(2,1)S(1)}, bf16[2048,256]{1,0:T(8,128)(2,1)}, u32[]{:S(2)}) copy-start(bf16[2048,256]{1,0:T(8,128)(2,1)} %param.10) | copy-start | bytes 3145732
  6.6 27.7 %all-to-all-start = ((bf16[4,128,2048]{2,1,0:T(8,128)(2,1)}), bf16[4,128,2048]{2,1,0:T(8,128)(2,1)S(1)}, u32[]{:S(2)}, u32[]{:S(2)}) async-start(bf16[4,128,2048]{2,1,0:T(8,128)(2,1)} %bitcast.2), calls=%async_computation | async-start | bytes 4194304 | tf_op jit(solution)/shard_map/all_to_all | solution.py:59
  36.9 36.1 %copy-start.8 = (s32[1,4]{1,0:T(1,128)S(1)}, s32[1,4]{1,0:T(1,128)}, u32[]{:S(2)}) copy-start(s32[1,4]{1,0:T(1,128)} %param.11) | copy-start | bytes 52
  55.5 58.9 %all-to-all-start.2 = ((bf16[16,128,512]{1,2,0:T(8,128)(2,1)}), bf16[16,128,512]{1,2,0:T(8,128)(2,1)S(1)}, u32[]{:S(2)}, u32[]{:S(2)}) async-start(bf16[16,128,512]{1,2,0:T(8,128)(2,1)} %broadcast_in_dim.22), calls=%async_computation.2 | async-start | bytes 4194304 | tf_op jit(solution)/shard_map/all_to_all | solution.py:29
  114.5 39.2 %all-to-all-start.3 = ((bf16[16,32,4,128]{3,2,1,0:T(4,128)(2,1)}), bf16[16,32,4,128]{3,2,1,0:T(4,128)(2,1)}, u32[]{:S(2)}, u32[]{:S(2)}) async-start(bf16[16,32,4,128]{3,2,1,0:T(4,128)(2,1)} %copy.83), calls=%async_computation.3 | async-start | bytes 1048576 | tf_op jit(solution)/shard_map/all_to_all | solution.py:54
  122.1 1.4 copy-start.3
  126.3 5.7 %copy-start = (f32[2,2048,128,8]{2,1,3,0:T(8,128)}, f32[2,2048,128,8]{2,1,3,0:T(8,128)S(1)}, u32[]{:S(2)}) copy-start(f32[2,2048,128,8]{2,1,3,0:T(8,128)S(1)} %get-tuple-element.29) | copy-start | bytes 50331652
  126.3 5.7 %copy-start.7 = (bf16[1,128,2048]{1,2,0:T(8,128)(2,1)S(1)}, bf16[1,128,2048]{1,2,0:T(8,128)(2,1)}, u32[]{:S(2)}) copy-start(bf16[1,128,2048]{1,2,0:T(8,128)(2,1)} %copy.79) | copy-start | bytes 1572868
  142.5 22.0 %copy-start.6 = (bf16[2048,256]{0,1:T(8,128)(2,1)S(1)}, bf16[2048,256]{0,1:T(8,128)(2,1)}, u32[]{:S(2)}) copy-start(bf16[2048,256]{0,1:T(8,128)(2,1)} %get-tuple-element.25) | copy-start | bytes 3145732
  155.0 34.8 %all-to-all-start.5 = ((bf16[16,128,256]{1,2,0:T(8,128)(2,1)}), bf16[16,128,256]{1,2,0:T(8,128)(2,1)S(1)}, u32[]{:S(2)}, u32[]{:S(2)}) async-start(bf16[16,128,256]{1,2,0:T(8,128)(2,1)} %copy.88), calls=%async_computation.5 | async-start | bytes 2097152 | tf_op jit(solution)/shard_map/all_to_all | solution.py:33
  164.6 12.6 %copy-start.4 = (bf16[16,8,16,128]{3,2,1,0:T(8,128)(2,1)S(1)}, bf16[16,8,16,128]{3,2,1,0:T(8,128)(2,1)}, u32[]{:S(2)}) copy-start(bf16[16,8,16,128]{3,2,1,0:T(8,128)(2,1)} %copy.120) | copy-start | bytes 1572868
  174.0 3.2 copy-start.1
  192.9 52.0 %all-to-all-start.6 = ((bf16[16,128,512]{2,1,0:T(8,128)(2,1)}), bf16[16,128,512]{2,1,0:T(8,128)(2,1)S(1)}, u32[]{:S(2)}, u32[]{:S(2)}) async-start(bf16[16,128,512]{2,1,0:T(8,128)(2,1)} %pad_maximum_fusion), calls=%async_computation.6 | async-start | bytes 4194304 | tf_op jit(solution)/shard_map/all_to_all | solution.py:116
  244.9 29.7 %copy-start.2 = (bf16[16,128,512]{2,1,0:T(8,128)(2,1)}, bf16[16,128,512]{2,1,0:T(8,128)(2,1)S(1)}, u32[]{:S(2)}) copy-start(bf16[16,128,512]{2,1,0:T(8,128)(2,1)S(1)} %all-to-all-done.6) | copy-start | bytes 6291460
  248.2 25.3 %all-to-all-start.4 = ((bf16[4,16,32,4,128]{4,2,3,1,0:T(8,128)(2,1)}), bf16[4,16,32,4,128]{4,2,3,1,0:T(8,128)(2,1)}, u32[]{:S(2)}, u32[]{:S(2)}) async-start(bf16[4,16,32,4,128]{4,2,3,1,0:T(8,128)(2,1)} %broadcast_in_dim.26), calls=%async_computation.4 | async-start | bytes 4194304 | tf_op jit(solution)/shard_map/all_to_all | solution.py:29
  274.6 25.1 %all-to-all-start.7 = ((bf16[16,128,256]{2,1,0:T(8,128)(2,1)}), bf16[16,128,256]{2,1,0:T(8,128)(2,1)}, u32[]{:S(2)}, u32[]{:S(2)}) async-start(bf16[16,128,256]{2,1,0:T(8,128)(2,1)} %broadcast_in_dim.28), calls=%async_computation.7 | async-start | bytes 2097152 | tf_op jit(solution)/shard_map/all_to_all | solution.py:29
  303.8 33.9 %all-to-all-start.8 = ((f32[4,128,512]{2,1,0:T(8,128)}), f32[4,128,512]{2,1,0:T(8,128)S(1)}, u32[]{:S(2)}, u32[]{:S(2)}) async-start(f32[4,128,512]{2,1,0:T(8,128)} %pad_maximum_fusion.1), calls=%async_computation.8 | async-start | bytes 2097152 | tf_op jit(solution)/shard_map/all_to_all | solution.py:33

commit v8 on v7

--- a/solution.py
+++ b/solution.py
@@ -47,10 +47,7 @@
     starts = doc_starts[0]
 
     blk = width // (dp_count * cp_count)
-    tp_count = lax.axis_size("tp")
-    quarter = tok_rows // tp_count
-    my_rows = lax.dynamic_slice_in_dim(inputs, lax.axis_index("tp") * quarter, quarter, 0)
-    cols = my_rows.reshape(quarter, dp_count, cp_count, blk).transpose(2, 0, 1, 3)
+    cols = inputs.reshape(tok_rows, dp_count, cp_count, blk).transpose(2, 0, 1, 3)
     cols = lax.all_to_all(cols, "cp", 0, 0, tiled=True)
 
     both_w = jnp.concatenate([k_weight, v_weight], axis=1)
@@ -106,8 +103,6 @@
     )
     value_terms = value_term.reshape(cp_count, tok_rows, kv_width).astype(jnp.bfloat16)
     cols, value_terms = lax.optimization_barrier((cols, value_terms))
-    cols = gather_over(cols, "tp", tp_count)
-    cols = jnp.moveaxis(cols, 0, 1).reshape(cp_count, tok_rows, dp_count, blk)
     value_own = reduce_over(value_terms, "cp").astype(jnp.bfloat16)
     key_terms = key_term.reshape(cp_count, tok_rows, kv_width).astype(jnp.bfloat16)
     mixed = jnp.concatenate(

time: 344 us -> 325 us (0.945)
  blocking collectives: 16.9 us -> 65.6 us
  waiting for transfers between devices: 142 us -> 93.4 us
  local copies, waits for them, and re-layouts: 48.1 us -> 39.2 us
  starting transfers between devices: 72.3 us -> 64.2 us
    all_to_all x0 -> x1, blocking collectives: none -> 48.7 us  [on_device(): mixed = lax.all_to_all(mixed, 'cp', 0, 0, tiled=True)]
    all_to_all x1 -> x0, waiting for transfers between devices: 40.4 us -> none  [on_device(): mixed = lax.all_to_all(mixed, 'cp', 0, 0, tiled=True)]
    all_to_all x3 -> x2, waiting for transfers between devices: 75.7 us -> 56.6 us  [gather_over(): return lax.all_to_all(spread, axis, 0, 0, tiled=True)]
    all_to_all x1 -> x0, starting transfers between devices: 9.62 us -> none  [on_device(): mixed = lax.all_to_all(mixed, 'cp', 0, 0, tiled=True)]
    all_to_all x1, waiting for transfers between devices: 0.01 us -> 9.46 us  [on_device(): cols = lax.all_to_all(cols, 'cp', 0, 0, tiled=True)]
    all_to_all x3 -> x2, starting transfers between devices: 20.7 us -> 25.3 us  [gather_over(): return lax.all_to_all(spread, axis, 0, 0, tiled=True)]
    all_to_all x2, starting transfers between devices: 30.6 us -> 26.8 us  [reduce_over(): received = lax.all_to_all(blocks, axis, 0, 0, tiled=True)]
    unnamed x28 -> x26, local copies, waits for them, and re-layouts: 19.6 us -> 16.1 us
  transfers between devices with their start and end apart: 8 -> 6, of which waited for: 6 -> 5; matrix products, arithmetic and copies ran while one was open for 23% -> 22% of each run, Pallas kernels for 0% -> 0%
where the time goes in v8:
time: 325 us; the launch traced here: 322 us
  waiting for transfers between devices  93.4 us (29%)
  blocking collectives  65.6 us (20%)
  starting transfers between devices  64.2 us (20%)
  matrix products  48.7 us (15%)
  local copies, waits for them, and re-layouts  39.2 us (12%)
  other arithmetic  9.57 us (3%)
    all_to_all x2, waiting for transfers between devices, gather_over(): return lax.all_to_all(spread, axis, 0, 0, tiled=True)  56.6 us
    all_to_all x1, blocking collectives, on_device(): mixed = lax.all_to_all(mixed, 'cp', 0, 0, tiled=True)  48.7 us
    all_to_all x2, starting transfers between devices, reduce_over(): received = lax.all_to_all(blocks, axis, 0, 0, tiled=True)  26.8 us
    all_to_all x2, starting transfers between devices, gather_over(): return lax.all_to_all(spread, axis, 0, 0, tiled=True)  25.3 us
    all_to_all x1, waiting for transfers between devices, on_device(): by_dp = lax.all_to_all(by_dp, 'dp', 0, 0, tiled=True)  21.2 us
    all_to_all x1, blocking collectives, reduce_over(): received = lax.all_to_all(blocks, axis, 0, 0, tiled=True)  16.9 us
    unnamed x26, local copies, waits for them, and re-layouts  16.1 us
    dot_general x1, matrix products, on_device(): jnp.einsum('giqk,kgd->qgid', weights_bf, value_heads, preferred_element_t...  11.2 us
  transfers between devices with their start and end apart: 6, of which 5 were waited for; matrix products, arithmetic and copies ran while one was open for 22% of the time, Pallas kernels for 0%

profile of v8, /device:TPU:36, one launch (start us, length us, event | category | flops | bytes accessed | tf_op | source)
XLA Modules:
  0.0 321.5 jit_solution(11539304739253648255)
XLA Ops:
  0.6 3.3 %copy.93 = bf16[1,128,8192]{1,2,0:T(8,128)(2,1)S(1)} copy(bf16[1,128,8192]{2,1,0:T(8,128)(2,1)} %param.6) | data formatting | bytes 4194304 | tf_op args[0]
  6.7 4.5 %all-to-all-start = ((bf16[4,128,2048]{2,1,0:T(8,128)(2,1)}), bf16[4,128,2048]{2,1,0:T(8,128)(2,1)}, u32[]{:S(2)}, u32[]{:S(2)}) async-start(bf16[4,128,2048]{2,1,0:T(8,128)(2,1)} %bitcast.121), calls=%async_computation | async-start | bytes 4194304 | tf_op jit(solution)/shard_map/all_to_all | solution.py:56
  14.1 21.2 %all-to-all-done = bf16[4,128,2048]{2,1,0:T(8,128)(2,1)} async-done(((bf16[4,128,2048]{2,1,0:T(8,128)(2,1)}), bf16[4,128,2048]{2,1,0:T(8,128)(2,1)}, u32[]{:S(2)}, u32[]{:S(2)}) %all-to-all-start) | async-done | bytes 2097184 | tf_op jit(solution)/shard_map/all_to_all | solution.py:56
  35.3 3.2 fusion.12
  38.5 16.9 %all_to_all.40 = f32[4,128,512]{1,2,0:T(8,128)S(1)} all-to-all(f32[4,128,512]{1,2,0:T(8,128)S(1)} %fusion.12), channel_id=1, replica_groups=mesh['dp'=4,'cp'=16,'tp'=4] {'dp'}, dimensions={0} | all-to-all | bytes 2097152 | tf_op jit(solution)/shard_map/all_to_all | solution.py:33
  57.1 11.2 %all-to-all-start.2 = ((bf16[16,128,512]{1,2,0:T(8,128)(2,1)}), bf16[16,128,512]{1,2,0:T(8,128)(2,1)}, u32[]{:S(2)}, u32[]{:S(2)}) async-start(bf16[16,128,512]{1,2,0:T(8,128)(2,1)} %broadcast_in_dim.20), calls=%async_computation.2 | async-start | bytes 4194304 | tf_op jit(solution)/shard_map/all_to_all | solution.py:29
  74.1 42.1 %all-to-all-done.2 = bf16[16,128,512]{1,2,0:T(8,128)(2,1)} async-done(((bf16[16,128,512]{1,2,0:T(8,128)(2,1)}), bf16[16,128,512]{1,2,0:T(8,128)(2,1)}, u32[]{:S(2)}, u32[]{:S(2)}) %all-to-all-start.2) | async-done | bytes 2097184 | tf_op jit(solution)/shard_map/all_to_all | solution.py:29
  116.2 7.6 %all-to-all-start.3 = ((bf16[16,128,4,128]{1,3,2,0:T(8,128)(2,1)}), bf16[16,128,4,128]{1,3,2,0:T(8,128)(2,1)}, u32[]{:S(2)}, u32[]{:S(2)}) async-start(bf16[16,128,4,128]{1,3,2,0:T(8,128)(2,1)} %copy.104), calls=%async_computation.3 | async-start | bytes 4194304 | tf_op jit(solution)/shard_map/all_to_all | solution.py:51
  126.8 2.7 fusion.3
  129.6 4.0 %select_reduce_fusion = f32[2,8,128]{2,1,0:T(8,128)S(1)} fusion(f32[2,2048,128,8]{2,1,3,0:T(8,128)S(1)} %get-tuple-element.33, f32[2,8,128]{2,1,0:T(8,128)S(1)} %get-tuple-element.32, pred[128,2048]{0,1:T(8,128)(4,1)S(1)} %compare_and_fusion), kind=kLoop, calls=%fused_computation.5 | loop fusion | flops 20969472 | bytes 17055744 | tf_op jit(solution)/shard_map/reduce_sum | solution.py:80
  135.3 9.5 %fusion.8 = bf16[2048,2,128]{2,0,1:T(8,128)(2,1)S(1)} fusion(bf16[128,2,8,128]{0,3,2,1:T(8,128)(2,1)S(1)} %bitcast.131, f32[2,2048,128,8]{2,1,3,0:T(8,128)} %copy-done, f32[2,8,128]{2,1,0:T(8,128)S(1)} %log_add_fusion, pred[128,2048]{0,1:T(8,128)(4,1)S(1)} %compare_and_fusion), kind=kOutput, calls=%fused_computation.14 | convolution fusion | flops 1095237632 | bytes 18620416 | tf_op jit(solution)/shard_map/giqk,qgid->kgd/dot_general | solution.py:101
  145.8 11.2 %multiply_reduce_fusion = (f32[128,2,8]{0,2,1:T(8,128)S(1)}, bf16[2,128,8,128]{3,1,2,0:T(8,128)(2,1)}) fusion(bf16[128,2,8,128]{0,3,2,1:T(8,128)(2,1)} %bitcast.132, bf16[2048,2,128,1]{0,2,3,1:T(8,128)(2,1)} %bitcast.127, f32[2,2048,128,8]{2,1,3,0:T(8,128)} %copy-done, f32[2,8,128]{2,1,0:T(8,128)S(1)} %log_add_fusion, pred[128,2048]{0,1:T(8,128)(4,1)S(1)} %compare_and_fusion), kind=kOutput, calls=%fused_computation.31 | convolution fusion | flops 1096022016 | bytes 19152896 | tf_op jit(solution)/shard_map/giqk,kgd->qgid/dot_general | solution.py:83
  156.9 9.5 %all-to-all-done.3 = bf16[16,128,4,128]{1,3,2,0:T(8,128)(2,1)} async-done(((bf16[16,128,4,128]{1,3,2,0:T(8,128)(2,1)}), bf16[16,128,4,128]{1,3,2,0:T(8,128)(2,1)}, u32[]{:S(2)}, u32[]{:S(2)}) %all-to-all-start.3) | async-done | bytes 2097184 | tf_op jit(solution)/shard_map/all_to_all | solution.py:51
  167.7 6.0 %all-to-all-start.4 = ((bf16[16,128,256]{1,2,0:T(8,128)(2,1)}), bf16[16,128,256]{1,2,0:T(8,128)(2,1)S(1)}, u32[]{:S(2)}, u32[]{:S(2)}) async-start(bf16[16,128,256]{1,2,0:T(8,128)(2,1)} %copy.107), calls=%async_computation.4 | async-start | bytes 2097152 | tf_op jit(solution)/shard_map/all_to_all | solution.py:33
  173.7 9.4 %fusion.1 = bf16[2,8,128,2048]{2,3,1,0:T(8,128)(2,1)S(1)} fusion(f32[2,2048,128,8]{2,1,3,0:T(8,128)} %copy-done, f32[2,8,128]{2,1,0:T(8,128)S(1)} %bitcast.136, f32[2,8,128]{2,1,0:T(8,128)S(1)} %log_add_fusion, pred[128,2048]{0,1:T(8,128)(4,1)S(1)} %compare_and_fusion, bf16[2048,2,128,1]{0,2,3,1:T(8,128)(2,1)S(1)} %bitcast.128, ...), kind=kOutput, calls=%fused_computation.2 | convolution fusion | flops 1103101952 | bytes 27017216 | tf_op jit(solution)/shard_map/qgid,kgd->giqk/dot_general | solution.py:89
  183.1 3.2 copy-done.1
  188.7 8.7 %copy.131 = bf16[2048,2,128]{2,1,0:T(2,128)(2,1)S(1)} copy(bf16[2048,2,128]{2,0,1:T(8,128)(2,1)S(1)} %fusion.7) | data formatting | bytes 2097152 | tf_op jit(solution)/shard_map/convert_element_type | solution.py:107
  200.7 48.7 %all_to_all.41 = bf16[16,128,512]{2,1,0:T(8,128)(2,1)S(1)} all-to-all(bf16[16,128,512]{2,1,0:T(8,128)(2,1)S(1)} %pad_maximum_fusion), channel_id=1, replica_groups=mesh['dp'=4,'cp'=16,'tp'=4] {'cp'}, dimensions={0} | all-to-all | bytes 4194304 | tf_op jit(solution)/shard_map/all_to_all | solution.py:111
  250.7 14.0 %all-to-all-start.6 = ((bf16[16,128,256]{2,1,0:T(8,128)(2,1)}), bf16[16,128,256]{2,1,0:T(8,128)(2,1)}, u32[]{:S(2)}, u32[]{:S(2)}) async-start(bf16[16,128,256]{2,1,0:T(8,128)(2,1)} %broadcast_in_dim.46), calls=%async_computation.6 | async-start | bytes 2097152 | tf_op jit(solution)/shard_map/all_to_all | solution.py:29
  264.7 3.1 convolution_bitcast_fusion.2
  267.8 14.6 %all-to-all-done.6 = bf16[16,128,256]{2,1,0:T(8,128)(2,1)} async-done(((bf16[16,128,256]{2,1,0:T(8,128)(2,1)}), bf16[16,128,256]{2,1,0:T(8,128)(2,1)}, u32[]{:S(2)}, u32[]{:S(2)}) %all-to-all-start.6) | async-done | bytes 1048608 | tf_op jit(solution)/shard_map/all_to_all | solution.py:29
  287.1 20.8 %all-to-all-start.7 = ((f32[4,128,512]{2,1,0:T(8,128)}), f32[4,128,512]{2,1,0:T(8,128)S(1)}, u32[]{:S(2)}, u32[]{:S(2)}) async-start(f32[4,128,512]{2,1,0:T(8,128)} %pad_maximum_fusion.1), calls=%async_computation.7 | async-start | bytes 2097152 | tf_op jit(solution)/shard_map/all_to_all | solution.py:33
  307.9 4.7 %fusion.13 = bf16[2,128,8,128]{3,1,2,0:T(8,128)(2,1)S(1)} fusion(bf16[2048,2,128,1]{0,2,3,1:T(8,128)(2,1)S(1)} %bitcast.120, bf16[2,8,128,2048]{2,3,1,0:T(8,128)(2,1)} %copy-done.1), kind=kOutput, calls=%fused_computation.23 | convolution fusion | flops 1074266112 | bytes 9961472 | tf_op jit(solution)/shard_map/giqk,kgd->qgid/dot_general | solution.py:94
  314.6 6.1 %all-to-all-done.7 = f32[4,128,512]{2,1,0:T(8,128)S(1)} async-done(((f32[4,128,512]{2,1,0:T(8,128)}), f32[4,128,512]{2,1,0:T(8,128)S(1)}, u32[]{:S(2)}, u32[]{:S(2)}) %all-to-all-start.7) | async-done | bytes 1048608 | tf_op jit(solution)/shard_map/all_to_all | solution.py:33
  (53 shorter events, 34.5 us)
Async XLA Ops:
  0.6 10.5 %copy-start.4 = (bf16[2048,256]{1,0:T(8,128)(2,1)S(1)}, bf16[2048,256]{1,0:T(8,128)(2,1)}, u32[]{:S(2)}) copy-start(bf16[2048,256]{1,0:T(8,128)(2,1)} %param.9) | copy-start | bytes 3145732
  6.7 28.6 %all-to-all-start = ((bf16[4,128,2048]{2,1,0:T(8,128)(2,1)}), bf16[4,128,2048]{2,1,0:T(8,128)(2,1)}, u32[]{:S(2)}, u32[]{:S(2)}) async-start(bf16[4,128,2048]{2,1,0:T(8,128)(2,1)} %bitcast.121), calls=%async_computation | async-start | bytes 4194304 | tf_op jit(solution)/shard_map/all_to_all | solution.py:56
  38.5 34.1 %copy-start.8 = (s32[1,4]{1,0:T(1,128)S(1)}, s32[1,4]{1,0:T(1,128)}, u32[]{:S(2)}) copy-start(s32[1,4]{1,0:T(1,128)} %param.11) | copy-start | bytes 52
  57.1 59.0 %all-to-all-start.2 = ((bf16[16,128,512]{1,2,0:T(8,128)(2,1)}), bf16[16,128,512]{1,2,0:T(8,128)(2,1)}, u32[]{:S(2)}, u32[]{:S(2)}) async-start(bf16[16,128,512]{1,2,0:T(8,128)(2,1)} %broadcast_in_dim.20), calls=%async_computation.2 | async-start | bytes 4194304 | tf_op jit(solution)/shard_map/all_to_all | solution.py:29
  69.5 57.3 %copy-start.2 = (bf16[16,8,16,128]{3,2,1,0:T(8,128)(2,1)}, bf16[16,8,16,128]{3,2,1,0:T(8,128)(2,1)S(1)}, u32[]{:S(2)}) copy-start(bf16[16,8,16,128]{3,2,1,0:T(8,128)(2,1)S(1)} %copy.135) | copy-start | bytes 1572868
  71.1 64.2 %copy-start.7 = (bf16[1,128,2048]{1,2,0:T(8,128)(2,1)}, bf16[1,128,2048]{1,2,0:T(8,128)(2,1)S(1)}, u32[]{:S(2)}) copy-start(bf16[1,128,2048]{1,2,0:T(8,128)(2,1)S(1)} %copy.99) | copy-start | bytes 1572868
  116.2 50.2 %all-to-all-start.3 = ((bf16[16,128,4,128]{1,3,2,0:T(8,128)(2,1)}), bf16[16,128,4,128]{1,3,2,0:T(8,128)(2,1)}, u32[]{:S(2)}, u32[]{:S(2)}) async-start(bf16[16,128,4,128]{1,3,2,0:T(8,128)(2,1)} %copy.104), calls=%async_computation.3 | async-start | bytes 4194304 | tf_op jit(solution)/shard_map/all_to_all | solution.py:51
  129.6 5.7 %copy-start = (f32[2,2048,128,8]{2,1,3,0:T(8,128)}, f32[2,2048,128,8]{2,1,3,0:T(8,128)S(1)}, u32[]{:S(2)}) copy-start(f32[2,2048,128,8]{2,1,3,0:T(8,128)S(1)} %get-tuple-element.33) | copy-start | bytes 50331652
  145.8 27.9 %copy-start.5 = (bf16[2048,256]{0,1:T(8,128)(2,1)S(1)}, bf16[2048,256]{0,1:T(8,128)(2,1)}, u32[]{:S(2)}) copy-start(bf16[2048,256]{0,1:T(8,128)(2,1)} %get-tuple-element.29) | copy-start | bytes 3145732
  167.7 31.3 %all-to-all-start.4 = ((bf16[16,128,256]{1,2,0:T(8,128)(2,1)}), bf16[16,128,256]{1,2,0:T(8,128)(2,1)S(1)}, u32[]{:S(2)}, u32[]{:S(2)}) async-start(bf16[16,128,256]{1,2,0:T(8,128)(2,1)} %copy.107), calls=%async_computation.4 | async-start | bytes 2097152 | tf_op jit(solution)/shard_map/all_to_all | solution.py:33
  173.7 12.6 %copy-start.3 = (bf16[16,8,16,128]{3,2,1,0:T(8,128)(2,1)S(1)}, bf16[16,8,16,128]{3,2,1,0:T(8,128)(2,1)}, u32[]{:S(2)}) copy-start(bf16[16,8,16,128]{3,2,1,0:T(8,128)(2,1)} %copy-done.2) | copy-start | bytes 1572868
  183.1 3.2 %copy-start.1 = (bf16[2,8,128,2048]{2,3,1,0:T(8,128)(2,1)}, bf16[2,8,128,2048]{2,3,1,0:T(8,128)(2,1)S(1)}, u32[]{:S(2)}) copy-start(bf16[2,8,128,2048]{2,3,1,0:T(8,128)(2,1)S(1)} %fusion.1) | copy-start | bytes 25165828
  250.7 31.7 %all-to-all-start.6 = ((bf16[16,128,256]{2,1,0:T(8,128)(2,1)}), bf16[16,128,256]{2,1,0:T(8,128)(2,1)}, u32[]{:S(2)}, u32[]{:S(2)}) async-start(bf16[16,128,256]{2,1,0:T(8,128)(2,1)} %broadcast_in_dim.46), calls=%async_computation.6 | async-start | bytes 2097152 | tf_op jit(solution)/shard_map/all_to_all | solution.py:29
  287.1 33.6 %all-to-all-start.7 = ((f32[4,128,512]{2,1,0:T(8,128)}), f32[4,128,512]{2,1,0:T(8,128)S(1)}, u32[]{:S(2)}, u32[]{:S(2)}) async-start(f32[4,128,512]{2,1,0:T(8,128)} %pad_maximum_fusion.1), calls=%async_computation.7 | async-start | bytes 2097152 | tf_op jit(solution)/shard_map/all_to_all | solution.py:33
  307.9 5.7 %copy-start.6 = (bf16[2,128,8,128]{3,1,2,0:T(8,128)(2,1)S(1)}, bf16[2,128,8,128]{3,1,2,0:T(8,128)(2,1)}, u32[]{:S(2)}) copy-start(bf16[2,128,8,128]{3,1,2,0:T(8,128)(2,1)} %get-tuple-element.35) | copy-start | bytes 1572868
